TPU v7x, 256 devices: a whole 4x4x8 slice. The times are simulated.
256 devices in a mesh: cells: 128 (over z, x, y), slab: 2 (over core).
Axes of the slice: x: 4, y: 4, z: 8, core: 2. Of those that a mesh axis runs over, the one named last changes fastest.
Arguments:
- block_owner: int32 [32768], P(('cells', 'slab')), may hold values from 0 to 127, as said below
- contact_elem: int32 [4194304], P(('cells', 'slab')), may hold values from 0 to 8191, as said below
- grain_offset: float32 [3, 4194304], P(None, ('cells', 'slab')), may hold values from -2 to 2
- grain_vel: float32 [3, 4194304], P(None, ('cells', 'slab')), may hold values from -6 to 6
- grain_radius: float32 [4194304], P(('cells', 'slab')), may hold values from 0.5 to 1
- disp_cached: float32 [3, 4194304], P(None, ('cells', 'slab')), may hold values from -1.5 to 1.5
- wall_disp: float32 [3, 128, 16384], P(None, 'slab', 'cells'), may hold values from -4 to 4
- wall_vel: float32 [3, 128, 16384], P(None, 'slab', 'cells'), may hold values from -4 to 4
- wall_stiff: float32 [128, 16384], P('slab', 'cells'), may hold values from 0.5 to 2
Outputs:
- wall_next: float32 [3, 128, 16384], P(None, 'slab', 'cells')
- contact_gap: float32 [4194304], P(('cells', 'slab'))
Inputs may be any that keep to these rules, and one draw needn't show every extreme that they name: Tile t of a device is the contacts t * 128 to (t + 1) * 128 - 1 of that device; its contacts touch wall patch block_owner[t] within the device's own height slab. One patch, the outlet, the same for all devices, is named exactly 2 times by every device; every other patch is named at most once by each device (each device's tiles name one patch other than the outlet not at all). The contact touches row contact_elem // 128 and column contact_elem % 128 of its tile's patch.
All inputs are finite; a program needn't handle non-finite values.
Results may differ from a plain program's by a relative error of at most 0.000078.
Values sent between devices are 32-bit elements; how exact they have to be, the bound alone decides.
No kernel may reach another device: no remote copies, remote signals or barrier semaphores. Data moves between devices by JAX's collectives and lax.ppermute only.
A program may use at most 64 MiB of HBM per device.

v0:
```python
import math

import jax
import jax.numpy as jnp
from jax import lax
from jax.sharding import PartitionSpec as P

SUBSTEPS = 4


SPRING_RATE = 2.0
SOFTNESS = 0.25
APPROACH_DAMP = 0.5
FRICTION = 0.4
SLIP_SPEED = 0.1
HOOP_RATE = 0.5
SHELL_DAMP = 0.3
TIME_STEP = 0.2
FULL_TURN = 2.0 * math.pi
HIGHEST = lax.Precision.HIGHEST


def with_halo(array, sides, width, wrap):
    for axis, dim in sides:
        count, length = (lax.axis_size(axis), array.shape[dim])
        up = [(i, (i + 1) % count) for i in range(count if wrap else count - 1)]
        down = [(j, i) for i, j in up]
        last = lax.slice_in_dim(array, length - width, length, axis=dim)
        leading = lax.slice_in_dim(array, 0, width, axis=dim)
        before = lax.ppermute(last, axis, up)
        after = lax.ppermute(leading, axis, down)
        array = jnp.concatenate([before, array, after], axis=dim)
    return array


def normals(column, total_cols):
    angle = (column.astype(jnp.float32) + 0.5) * (FULL_TURN / total_cols)
    return (jnp.cos(angle), jnp.sin(angle))


def contact_push(offset, velocity, radius, cached, facing_cos, facing_sin):
    reach = offset[0] * facing_cos + offset[1] * facing_sin
    intersection = radius + reach - (cached[0] * facing_cos + cached[1] * facing_sin)
    spring = SPRING_RATE * SOFTNESS * jax.nn.softplus(intersection / SOFTNESS)
    approach = velocity[0] * facing_cos + velocity[1] * facing_sin
    pressing = spring + APPROACH_DAMP * approach
    slide_x = velocity[0] - approach * facing_cos
    slide_y = velocity[1] - approach * facing_sin
    slide_z = velocity[2]
    speed = jnp.sqrt(
        slide_x * slide_x + slide_y * slide_y + slide_z * slide_z + SLIP_SPEED * SLIP_SPEED
    )
    friction = FRICTION * spring / speed
    push = jnp.stack(
        [
            pressing * facing_cos + friction * slide_x,
            pressing * facing_sin + friction * slide_y,
            friction * slide_z,
        ]
    )
    return (push, reach)


def advance(displace, velocity, traction, stiffness, vertical, sideways, facing_cos, facing_sin):
    internal = stiffness * (vertical + sideways - 4.0 * displace)
    radial = HOOP_RATE * stiffness * (displace[0] * facing_cos + displace[1] * facing_sin)
    hoop = jnp.stack([radial * facing_cos, radial * facing_sin, jnp.zeros_like(radial)])
    acceleration = internal - hoop + traction - SHELL_DAMP * velocity
    velocity = velocity + TIME_STEP * acceleration
    return (displace + TIME_STEP * velocity, velocity)


def element_hots(ids_block, patch_rows, patch_cols):
    row_ids = ids_block // patch_cols
    col_ids = ids_block % patch_cols
    rows_hot = (row_ids[None, :] == jnp.arange(patch_rows, dtype=jnp.int32)[:, None]).astype(
        jnp.float32
    )
    cols_hot = (col_ids[:, None] == jnp.arange(patch_cols, dtype=jnp.int32)[None, :]).astype(
        jnp.float32
    )
    return (rows_hot, cols_hot)


def gather_elements(field, ids_blocks, patch_rows, patch_cols):
    comps = field.shape[0]
    flat_field = field.reshape(comps * patch_rows, patch_cols)

    def one_block(ids_block):
        rows_hot, cols_hot = element_hots(ids_block, patch_rows, patch_cols)
        picked = jnp.dot(flat_field, cols_hot.T, precision=HIGHEST).reshape(comps, patch_rows, -1)
        return jnp.sum(picked * rows_hot[None], axis=1)

    values = lax.map(one_block, ids_blocks)
    return jnp.transpose(values, (1, 0, 2)).reshape(comps, -1)


def on_device(
    block_owner,
    contact_elem,
    grain_offset,
    grain_vel,
    grain_radius,
    disp_cached,
    wall_disp,
    wall_vel,
    wall_stiff,
):
    owners = lax.axis_size("cells")
    blocks = block_owner.shape[0]
    tile_len = contact_elem.shape[0] // blocks
    patch_rows, patch_cols = wall_stiff.shape
    total_cols = patch_cols * owners
    capacity = 2 * (blocks // owners)
    slots = owners * capacity
    sentinel = patch_rows * patch_cols
    elements = contact_elem.reshape(blocks, tile_len)
    radius_tiles = grain_radius.reshape(blocks, tile_len)
    col_index = block_owner[:, None] * patch_cols + elements % patch_cols
    facing_cos, facing_sin = normals(col_index, total_cols)
    push, reach = contact_push(
        grain_offset.reshape(3, blocks, tile_len),
        grain_vel.reshape(3, blocks, tile_len),
        radius_tiles,
        disp_cached.reshape(3, blocks, tile_len),
        facing_cos,
        facing_sin,
    )
    patches = jnp.arange(owners, dtype=jnp.int32)
    member = (block_owner[:, None] == patches[None, :]).astype(jnp.float32)
    tile_ids = jnp.arange(blocks, dtype=jnp.int32)
    before = (tile_ids[None, :] < tile_ids[:, None]).astype(jnp.float32)
    earlier = jnp.dot(before, member, precision=HIGHEST)
    slot = block_owner * capacity + jnp.sum(earlier * member, axis=1).astype(jnp.int32)
    placing = (slot[None, :] == jnp.arange(slots, dtype=jnp.int32)[:, None]).astype(jnp.float32)
    push_out = jnp.einsum("sb,cbl->csl", placing, push, precision=HIGHEST)
    ids_float = jnp.dot(placing, elements.astype(jnp.float32), precision=HIGHEST)
    filled = jnp.sum(placing, axis=1)
    ids_out = jnp.where(filled[:, None] > 0.5, ids_float.astype(jnp.int32), sentinel)
    push_in, ids_in = (
        lax.all_to_all(
            push_out.reshape(3, owners, capacity, tile_len),
            "cells",
            split_axis=1,
            concat_axis=1,
            tiled=True,
        ),
        lax.all_to_all(
            ids_out.reshape(1, owners, capacity, tile_len),
            "cells",
            split_axis=1,
            concat_axis=1,
            tiled=True,
        ),
    )
    grouped = 1
    while owners % (grouped * 2) == 0 and grouped * 2 * capacity * tile_len <= 4096:
        grouped = grouped * 2
    block_len = grouped * capacity * tile_len
    turns = slots * tile_len // block_len
    ids_blocks = ids_in.reshape(turns, block_len)
    push_blocks = jnp.transpose(push_in.reshape(3, turns, block_len), (1, 0, 2))

    def add_block(total, pieces):
        ids_block, push_block = pieces
        rows_hot, cols_hot = element_hots(ids_block, patch_rows, patch_cols)
        weighted = (push_block[:, None, :] * rows_hot[None]).reshape(3 * patch_rows, block_len)
        return (total + jnp.dot(weighted, cols_hot, precision=HIGHEST), None)

    traction_flat, unused = lax.scan(
        add_block, jnp.zeros((3 * patch_rows, patch_cols), jnp.float32), (ids_blocks, push_blocks)
    )
    traction = traction_flat.reshape(3, patch_rows, patch_cols)
    first_col = lax.axis_index("cells") * patch_cols
    columns = first_col + jnp.arange(patch_cols, dtype=jnp.int32)
    wall_cos, wall_sin = normals(columns, total_cols)
    displace, velocity = (wall_disp, wall_vel)
    for substep in range(SUBSTEPS):
        tall = with_halo(displace, (("slab", 1),), 1, False)
        wide = with_halo(displace, (("cells", 2),), 1, True)
        vertical = tall[:, 2:] + tall[:, :-2]
        sideways = wide[:, :, 2:] + wide[:, :, :-2]
        displace, velocity = advance(
            displace, velocity, traction, wall_stiff, vertical, sideways, wall_cos, wall_sin
        )
    values_out = gather_elements(displace, ids_blocks, patch_rows, patch_cols)
    values_in = lax.all_to_all(values_out, "cells", split_axis=1, concat_axis=1, tiled=True)
    mine = jnp.einsum(
        "sb,csl->cbl", placing, values_in.reshape(3, slots, tile_len), precision=HIGHEST
    )
    landed = mine[0] * facing_cos + mine[1] * facing_sin
    contact_gap = radius_tiles + reach - landed
    return (displace, contact_gap.reshape(-1))


def solution(mesh):
    return jax.shard_map(
        on_device,
        mesh=mesh,
        in_specs=(
            P(("cells", "slab")),
            P(("cells", "slab")),
            P(None, ("cells", "slab")),
            P(None, ("cells", "slab")),
            P(("cells", "slab")),
            P(None, ("cells", "slab")),
            P(None, "slab", "cells"),
            P(None, "slab", "cells"),
            P("slab", "cells"),
        ),
        out_specs=(P(None, "slab", "cells"), P(("cells", "slab"))),
        check_vma=False,
    )
```

profile of v0, /device:TPU:2, one launch (start us, length us, event | category | flops | bytes accessed | tf_op | source)
XLA Modules:
  0.0 186.9 jit_solution(1762343224001675424)
XLA Ops:
  2.3 1.7 fusion.9
  4.0 15.4 %all-to-all-start.1 = ((s32[1,128,2,128]{3,2,0,1:T(2,128)}), s32[1,128,2,128]{3,2,0,1:T(2,128)S(1)}, u32[]{:S(2)}, u32[]{:S(2)}) async-start(s32[1,128,2,128]{3,2,0,1:T(2,128)} %bitcast.24), calls=%async_computation.1 | async-start | bytes 262144 | tf_op jit(solution)/shard_map/all_to_all | solution.py:148
  19.5 1.4 fusion.104
  21.2 1.1 fusion.102
  22.6 1.1 fusion.103
  28.0 3.3 %all-to-all-done.1 = s32[1,128,2,128]{3,2,0,1:T(2,128)S(1)} async-done(((s32[1,128,2,128]{3,2,0,1:T(2,128)}), s32[1,128,2,128]{3,2,0,1:T(2,128)S(1)}, u32[]{:S(2)}, u32[]{:S(2)}) %all-to-all-start.1) | async-done | bytes 131104 | tf_op jit(solution)/shard_map/all_to_all | solution.py:148
  31.3 10.4 %all-to-all-start = ((f32[3,128,2,128]{3,2,0,1:T(2,128)}), f32[3,128,2,128]{3,2,0,1:T(2,128)S(1)}, u32[]{:S(2)}, u32[]{:S(2)}) async-start(f32[3,128,2,128]{3,2,0,1:T(2,128)} %copy.48), calls=%async_computation | async-start | bytes 786432 | tf_op jit(solution)/shard_map/all_to_all | solution.py:141
  42.5 2.7 %collective-permute-start.2 = (f32[3,64,1]{2,1,0:T(8,128)}, f32[3,64,1]{2,1,0:T(8,128)}, u32[]{:S(2)}, u32[]{:S(2)}) collective-permute-start(f32[3,64,1]{2,1,0:T(8,128)} %get-tuple-element.200), channel_id=1, source_target_pairs={{2,0},{4,2},{6,4},{8,6},{10,8},{12,10},{14,12},{16,14},{18,16},{20... | collective-permute-start | bytes 2312 | tf_op jit(solution)/shard_map/ppermute | solution.py:31
  45.8 1.3 collective-permute-start
  47.0 4.1 %collective-permute-start.1 = (f32[3,1,128]{2,1,0:T(1,128)}, f32[3,1,128]{2,1,0:T(1,128)}, u32[]{:S(2)}, u32[]{:S(2)}) collective-permute-start(f32[3,1,128]{2,1,0:T(1,128)} %get-tuple-element.199), channel_id=1, source_target_pairs={{0,1},{2,3},{4,5},{6,7},{8,9},{10,11},{12,13},{14,15},{16,17},{18,... | collective-permute-start | bytes 4616 | tf_op jit(solution)/shard_map/ppermute | solution.py:30
  52.6 5.9 %all-to-all-done = f32[3,128,2,128]{3,2,0,1:T(2,128)S(1)} async-done(((f32[3,128,2,128]{3,2,0,1:T(2,128)}), f32[3,128,2,128]{3,2,0,1:T(2,128)S(1)}, u32[]{:S(2)}, u32[]{:S(2)}) %all-to-all-start) | async-done | bytes 393248 | tf_op jit(solution)/shard_map/all_to_all | solution.py:141
  58.7 1.1 reshape.594
  59.8 28.1 %while.26 = (s32[]{:T(128)}, f32[192,128]{1,0:T(8,128)S(1)}, f32[8,3,4096]{2,0,1:T(8,128)}, s32[8,4096]{1,0:T(8,128)S(1)}, s32[]{:T(128)}, /*index=5*/s32[]{:T(128)}) while((s32[]{:T(128)}, f32[192,128]{1,0:T(8,128)S(1)}, f32[8,3,4096]{2,0,1:T(8,128)}, s32[8,4096]{1,0:T(8,128)S(1)}, s32[]{:T(128)}, /*index=5*/s32[]{:T(128)}) %tuple.86), condition=%wide.region_3.4_spmd.clone, body=%wide.region_2.3_spmd.clone.sunk | while | flops 1209950208 | bytes 8945751 | solution.py:170
  59.9 1.0 constant_dynamic-slice_fusion.6
  61.4 1.9 fusion.128
  63.5 1.0 constant_dynamic-slice_fusion.6
  64.9 1.9 fusion.128
  67.0 1.0 constant_dynamic-slice_fusion.6
  68.4 1.9 fusion.128
  71.9 1.9 fusion.128
  74.0 1.0 constant_dynamic-slice_fusion.6
  75.5 1.9 fusion.128
  79.0 1.9 fusion.128
  82.5 1.9 fusion.128
  86.0 1.9 fusion.128
  88.0 1.2 multiply_add_fusion.2
  89.3 2.0 %collective-permute-start.6 = (f32[3,64,1]{2,1,0:T(8,128)S(1)}, f32[3,64,1]{2,1,0:T(8,128)S(1)}, u32[]{:S(2)}, u32[]{:S(2)}) collective-permute-start(f32[3,64,1]{2,1,0:T(8,128)S(1)} %get-tuple-element.196), channel_id=1, source_target_pairs={{2,0},{4,2},{6,4},{8,6},{10,8},{12,10},{14,12},{16,14},{18,16},{20... | collective-permute-start | bytes 2312 | tf_op jit(solution)/shard_map/ppermute | solution.py:31
  91.6 1.3 collective-permute-start.4
  92.9 3.0 %collective-permute-start.5 = (f32[3,1,128]{2,1,0:T(1,128)S(1)}, f32[3,1,128]{2,1,0:T(1,128)S(1)}, u32[]{:S(2)}, u32[]{:S(2)}) collective-permute-start(f32[3,1,128]{2,1,0:T(1,128)S(1)} %get-tuple-element.195), channel_id=1, source_target_pairs={{0,1},{2,3},{4,5},{6,7},{8,9},{10,11},{12,13},{14,15},{16,17},{18,... | collective-permute-start | bytes 4616 | tf_op jit(solution)/shard_map/ppermute | solution.py:30
  96.6 1.4 collective-permute-done.7
  98.9 2.6 %collective-permute-start.10 = (f32[3,64,1]{2,1,0:T(8,128)S(1)}, f32[3,64,1]{2,1,0:T(8,128)S(1)}, u32[]{:S(2)}, u32[]{:S(2)}) collective-permute-start(f32[3,64,1]{2,1,0:T(8,128)S(1)} %get-tuple-element.192), channel_id=1, source_target_pairs={{2,0},{4,2},{6,4},{8,6},{10,8},{12,10},{14,12},{16,14},{18,16},{20... | collective-permute-start | bytes 2312 | tf_op jit(solution)/shard_map/ppermute | solution.py:31
  101.5 1.3 collective-permute-start.8
  102.8 3.0 %collective-permute-start.9 = (f32[3,1,128]{2,1,0:T(1,128)S(1)}, f32[3,1,128]{2,1,0:T(1,128)S(1)}, u32[]{:S(2)}, u32[]{:S(2)}) collective-permute-start(f32[3,1,128]{2,1,0:T(1,128)S(1)} %get-tuple-element.191), channel_id=1, source_target_pairs={{0,1},{2,3},{4,5},{6,7},{8,9},{10,11},{12,13},{14,15},{16,17},{18,... | collective-permute-start | bytes 4616 | tf_op jit(solution)/shard_map/ppermute | solution.py:30
  106.6 1.8 collective-permute-done.11
  109.3 2.5 %collective-permute-start.14 = (f32[3,64,1]{2,1,0:T(8,128)S(1)}, f32[3,64,1]{2,1,0:T(8,128)S(1)}, u32[]{:S(2)}, u32[]{:S(2)}) collective-permute-start(f32[3,64,1]{2,1,0:T(8,128)S(1)} %get-tuple-element.188), channel_id=1, source_target_pairs={{2,0},{4,2},{6,4},{8,6},{10,8},{12,10},{14,12},{16,14},{18,16},{20... | collective-permute-start | bytes 2312 | tf_op jit(solution)/shard_map/ppermute | solution.py:31
  111.7 1.3 collective-permute-start.12
  113.0 3.0 %collective-permute-start.13 = (f32[3,1,128]{2,1,0:T(1,128)S(1)}, f32[3,1,128]{2,1,0:T(1,128)S(1)}, u32[]{:S(2)}, u32[]{:S(2)}) collective-permute-start(f32[3,1,128]{2,1,0:T(1,128)S(1)} %get-tuple-element.187), channel_id=1, source_target_pairs={{0,1},{2,3},{4,5},{6,7},{8,9},{10,11},{12,13},{14,15},{16,17},{18,... | collective-permute-start | bytes 4616 | tf_op jit(solution)/shard_map/ppermute | solution.py:30
  116.1 2.5 %collective-permute-done.15 = f32[3,64,1]{2,1,0:T(8,128)S(1)} collective-permute-done((f32[3,64,1]{2,1,0:T(8,128)S(1)}, f32[3,64,1]{2,1,0:T(8,128)S(1)}, u32[]{:S(2)}, u32[]{:S(2)}) %collective-permute-start.15) | collective-permute-done | bytes 800 | tf_op jit(solution)/shard_map/ppermute | solution.py:30
  118.8 25.1 %while.25 = (s32[]{:T(128)}, f32[8,3,4096]{2,1,0:T(4,128)S(1)}, s32[8,4096]{1,0:T(8,128)S(1)}, f32[192,128]{1,0:T(8,128)S(1)}, s32[]{:T(128)}) while((s32[]{:T(128)}, f32[8,3,4096]{2,1,0:T(4,128)S(1)}, s32[8,4096]{1,0:T(8,128)S(1)}, f32[192,128]{1,0:T(8,128)S(1)}, s32[]{:T(128)}) %tuple.94), condition=%wide.region_6.7_spmd, body=%wide.region_4.6_spmd.sunk | while | flops 1210675200 | bytes 8781893 | solution.py:94
  118.9 2.5 %fusion.124 = f32[4096,192]{0,1:T(8,128)S(1)} fusion(f32[192,128]{1,0:T(8,128)S(1)} %get-tuple-element.293, s32[4096]{0:T(1024)S(1)} %add_select_fusion.6), kind=kOutput, calls=%fused_computation.2.clone.1 | convolution fusion | flops 1208483840 | bytes 3260416 | tf_op jit(solution)/shard_map/while/body/eval_jaxpr/dot_general | solution.py:91
  122.1 2.5 %fusion.124 = f32[4096,192]{0,1:T(8,128)S(1)} fusion(f32[192,128]{1,0:T(8,128)S(1)} %get-tuple-element.293, s32[4096]{0:T(1024)S(1)} %add_select_fusion.6), kind=kOutput, calls=%fused_computation.2.clone.1 | convolution fusion | flops 1208483840 | bytes 3260416 | tf_op jit(solution)/shard_map/while/body/eval_jaxpr/dot_general | solution.py:91
  125.2 2.5 %fusion.124 = f32[4096,192]{0,1:T(8,128)S(1)} fusion(f32[192,128]{1,0:T(8,128)S(1)} %get-tuple-element.293, s32[4096]{0:T(1024)S(1)} %add_select_fusion.6), kind=kOutput, calls=%fused_computation.2.clone.1 | convolution fusion | flops 1208483840 | bytes 3260416 | tf_op jit(solution)/shard_map/while/body/eval_jaxpr/dot_general | solution.py:91
  128.4 2.5 %fusion.124 = f32[4096,192]{0,1:T(8,128)S(1)} fusion(f32[192,128]{1,0:T(8,128)S(1)} %get-tuple-element.293, s32[4096]{0:T(1024)S(1)} %add_select_fusion.6), kind=kOutput, calls=%fused_computation.2.clone.1 | convolution fusion | flops 1208483840 | bytes 3260416 | tf_op jit(solution)/shard_map/while/body/eval_jaxpr/dot_general | solution.py:91
  131.5 2.5 %fusion.124 = f32[4096,192]{0,1:T(8,128)S(1)} fusion(f32[192,128]{1,0:T(8,128)S(1)} %get-tuple-element.293, s32[4096]{0:T(1024)S(1)} %add_select_fusion.6), kind=kOutput, calls=%fused_computation.2.clone.1 | convolution fusion | flops 1208483840 | bytes 3260416 | tf_op jit(solution)/shard_map/while/body/eval_jaxpr/dot_general | solution.py:91
  134.6 2.5 %fusion.124 = f32[4096,192]{0,1:T(8,128)S(1)} fusion(f32[192,128]{1,0:T(8,128)S(1)} %get-tuple-element.293, s32[4096]{0:T(1024)S(1)} %add_select_fusion.6), kind=kOutput, calls=%fused_computation.2.clone.1 | convolution fusion | flops 1208483840 | bytes 3260416 | tf_op jit(solution)/shard_map/while/body/eval_jaxpr/dot_general | solution.py:91
  137.8 2.5 %fusion.124 = f32[4096,192]{0,1:T(8,128)S(1)} fusion(f32[192,128]{1,0:T(8,128)S(1)} %get-tuple-element.293, s32[4096]{0:T(1024)S(1)} %add_select_fusion.6), kind=kOutput, calls=%fused_computation.2.clone.1 | convolution fusion | flops 1208483840 | bytes 3260416 | tf_op jit(solution)/shard_map/while/body/eval_jaxpr/dot_general | solution.py:91
  140.9 2.5 %fusion.124 = f32[4096,192]{0,1:T(8,128)S(1)} fusion(f32[192,128]{1,0:T(8,128)S(1)} %get-tuple-element.293, s32[4096]{0:T(1024)S(1)} %add_select_fusion.6), kind=kOutput, calls=%fused_computation.2.clone.1 | convolution fusion | flops 1208483840 | bytes 3260416 | tf_op jit(solution)/shard_map/while/body/eval_jaxpr/dot_general | solution.py:91
  144.0 41.0 %all_to_all.19 = f32[3,128,256]{2,0,1:T(4,128)S(1)} all-to-all(f32[3,128,256]{2,0,1:T(4,128)S(1)} %bitcast.204), channel_id=1, replica_groups=mesh['cells'=128,'slab'=2] {'cells'}, dimensions={1} | all-to-all | bytes 786432 | tf_op jit(solution)/shard_map/all_to_all | solution.py:187
  (186 shorter events, 28.1 us)
Async XLA Ops:
  2.2 29.1 %copy-start.14 = (s32[128]{0:T(128)}, s32[128]{0:T(128)S(1)}, u32[]{:S(2)}) copy-start(s32[128]{0:T(128)S(1)} %get-tuple-element.203) | copy-start | bytes 1540
  2.2 29.1 %copy-start.16 = (s32[128]{0:T(128)}, s32[128]{0:T(128)S(1)}, u32[]{:S(2)}) copy-start(s32[128]{0:T(128)S(1)} %get-tuple-element.202) | copy-start | bytes 1540
  4.0 27.3 %all-to-all-start.1 = ((s32[1,128,2,128]{3,2,0,1:T(2,128)}), s32[1,128,2,128]{3,2,0,1:T(2,128)S(1)}, u32[]{:S(2)}, u32[]{:S(2)}) async-start(s32[1,128,2,128]{3,2,0,1:T(2,128)} %bitcast.24), calls=%async_computation.1 | async-start | bytes 262144 | tf_op jit(solution)/shard_map/all_to_all | solution.py:148
  19.5 22.3 %copy-start.2 = (f32[3,64,128]{2,1,0:T(8,128)S(1)}, f32[3,64,128]{2,1,0:T(8,128)}, u32[]{:S(2)}) copy-start(f32[3,64,128]{2,1,0:T(8,128)} %param.19) | copy-start | bytes 294916
  20.9 31.0 %copy-start.1 = (f32[64,128]{1,0:T(8,128)S(1)}, f32[64,128]{1,0:T(8,128)}, u32[]{:S(2)}) copy-start(f32[64,128]{1,0:T(8,128)} %param.21) | copy-start | bytes 98308
  22.4 1.6 copy-start.4
  22.4 4.2 %copy-start.6 = (f32[1,16384]{1,0:T(1,128)}, f32[1,16384]{1,0:T(1,128)S(1)}, u32[]{:S(2)}) copy-start(f32[1,16384]{1,0:T(1,128)S(1)} %get-tuple-element.170) | copy-start | bytes 196612
  31.3 27.2 %all-to-all-start = ((f32[3,128,2,128]{3,2,0,1:T(2,128)}), f32[3,128,2,128]{3,2,0,1:T(2,128)S(1)}, u32[]{:S(2)}, u32[]{:S(2)}) async-start(f32[3,128,2,128]{3,2,0,1:T(2,128)} %copy.48), calls=%async_computation | async-start | bytes 786432 | tf_op jit(solution)/shard_map/all_to_all | solution.py:141
  42.5 45.5 %collective-permute-start.2 = (f32[3,64,1]{2,1,0:T(8,128)}, f32[3,64,1]{2,1,0:T(8,128)}, u32[]{:S(2)}, u32[]{:S(2)}) collective-permute-start(f32[3,64,1]{2,1,0:T(8,128)} %get-tuple-element.200), channel_id=1, source_target_pairs={{2,0},{4,2},{6,4},{8,6},{10,8},{12,10},{14,12},{16,14},{18,16},{20... | collective-permute-start | bytes 2312 | tf_op jit(solution)/shard_map/ppermute | solution.py:31
  45.2 42.8 %collective-permute-start.3 = (f32[3,64,1]{2,1,0:T(8,128)}, f32[3,64,1]{2,1,0:T(8,128)}, u32[]{:S(2)}, u32[]{:S(2)}) collective-permute-start(f32[3,64,1]{2,1,0:T(8,128)} %get-tuple-element.201), channel_id=1, source_target_pairs={{0,2},{2,4},{4,6},{6,8},{8,10},{10,12},{12,14},{14,16},{16,18},{18... | collective-permute-start | bytes 2312 | tf_op jit(solution)/shard_map/ppermute | solution.py:30
  45.8 42.2 %collective-permute-start = (f32[3,1,128]{2,1,0:T(1,128)}, f32[3,1,128]{2,1,0:T(1,128)}, u32[]{:S(2)}, u32[]{:S(2)}) collective-permute-start(f32[3,1,128]{2,1,0:T(1,128)} %get-tuple-element.198), channel_id=1, source_target_pairs={{1,0},{3,2},{5,4},{7,6},{9,8},{11,10},{13,12},{15,14},{17,16},{19,... | collective-permute-start | bytes 4616 | tf_op jit(solution)/shard_map/ppermute | solution.py:31
  47.0 40.9 %collective-permute-start.1 = (f32[3,1,128]{2,1,0:T(1,128)}, f32[3,1,128]{2,1,0:T(1,128)}, u32[]{:S(2)}, u32[]{:S(2)}) collective-permute-start(f32[3,1,128]{2,1,0:T(1,128)} %get-tuple-element.199), channel_id=1, source_target_pairs={{0,1},{2,3},{4,5},{6,7},{8,9},{10,11},{12,13},{14,15},{16,17},{18,... | collective-permute-start | bytes 4616 | tf_op jit(solution)/shard_map/ppermute | solution.py:30
  51.8 7.9 %copy-start.10 = (f32[128]{0:T(128)}, f32[128]{0:T(128)S(1)}, u32[]{:S(2)}) copy-start(f32[128]{0:T(128)S(1)} %fusion.96) | copy-start | bytes 1540
  51.9 7.9 %copy-start.12 = (f32[128]{0:T(128)}, f32[128]{0:T(128)S(1)}, u32[]{:S(2)}) copy-start(f32[128]{0:T(128)S(1)} %fusion.97) | copy-start | bytes 1540
  87.9 28.2 %copy-start.11 = (f32[128]{0:T(128)S(1)}, f32[128]{0:T(128)}, u32[]{:S(2)}) copy-start(f32[128]{0:T(128)} %copy-done.10) | copy-start | bytes 1540
  87.9 28.2 %copy-start.13 = (f32[128]{0:T(128)S(1)}, f32[128]{0:T(128)}, u32[]{:S(2)}) copy-start(f32[128]{0:T(128)} %copy-done.12) | copy-start | bytes 1540
  87.9 30.7 %copy-start.18 = (f32[3]{0:T(128)S(1)}, f32[3]{0:T(128)}, u32[]{:S(2)}) copy-start(f32[3]{0:T(128)} %pad.38.clone) | copy-start | bytes 40
  87.9 30.9 %copy-start.8 = (f32[8,3,4096]{2,1,0:T(4,128)S(1)}, f32[8,3,4096]{2,1,0:T(4,128)}, u32[]{:S(2)}) copy-start(f32[8,3,4096]{2,1,0:T(4,128)} %custom-call.1) | copy-start | bytes 1179652
  89.3 7.3 %collective-permute-start.6 = (f32[3,64,1]{2,1,0:T(8,128)S(1)}, f32[3,64,1]{2,1,0:T(8,128)S(1)}, u32[]{:S(2)}, u32[]{:S(2)}) collective-permute-start(f32[3,64,1]{2,1,0:T(8,128)S(1)} %get-tuple-element.196), channel_id=1, source_target_pairs={{2,0},{4,2},{6,4},{8,6},{10,8},{12,10},{14,12},{16,14},{18,16},{20... | collective-permute-start | bytes 2312 | tf_op jit(solution)/shard_map/ppermute | solution.py:31
  91.3 6.7 %collective-permute-start.7 = (f32[3,64,1]{2,1,0:T(8,128)S(1)}, f32[3,64,1]{2,1,0:T(8,128)S(1)}, u32[]{:S(2)}, u32[]{:S(2)}) collective-permute-start(f32[3,64,1]{2,1,0:T(8,128)S(1)} %get-tuple-element.197), channel_id=1, source_target_pairs={{0,2},{2,4},{4,6},{6,8},{8,10},{10,12},{12,14},{14,16},{16,18},{18... | collective-permute-start | bytes 2312 | tf_op jit(solution)/shard_map/ppermute | solution.py:30
  91.6 6.5 %collective-permute-start.4 = (f32[3,1,128]{2,1,0:T(1,128)S(1)}, f32[3,1,128]{2,1,0:T(1,128)S(1)}, u32[]{:S(2)}, u32[]{:S(2)}) collective-permute-start(f32[3,1,128]{2,1,0:T(1,128)S(1)} %get-tuple-element.194), channel_id=1, source_target_pairs={{1,0},{3,2},{5,4},{7,6},{9,8},{11,10},{13,12},{15,14},{17,16},{19,... | collective-permute-start | bytes 4616 | tf_op jit(solution)/shard_map/ppermute | solution.py:31
  92.9 5.2 %collective-permute-start.5 = (f32[3,1,128]{2,1,0:T(1,128)S(1)}, f32[3,1,128]{2,1,0:T(1,128)S(1)}, u32[]{:S(2)}, u32[]{:S(2)}) collective-permute-start(f32[3,1,128]{2,1,0:T(1,128)S(1)} %get-tuple-element.195), channel_id=1, source_target_pairs={{0,1},{2,3},{4,5},{6,7},{8,9},{10,11},{12,13},{14,15},{16,17},{18,... | collective-permute-start | bytes 4616 | tf_op jit(solution)/shard_map/ppermute | solution.py:30
  98.9 7.6 %collective-permute-start.10 = (f32[3,64,1]{2,1,0:T(8,128)S(1)}, f32[3,64,1]{2,1,0:T(8,128)S(1)}, u32[]{:S(2)}, u32[]{:S(2)}) collective-permute-start(f32[3,64,1]{2,1,0:T(8,128)S(1)} %get-tuple-element.192), channel_id=1, source_target_pairs={{2,0},{4,2},{6,4},{8,6},{10,8},{12,10},{14,12},{16,14},{18,16},{20... | collective-permute-start | bytes 2312 | tf_op jit(solution)/shard_map/ppermute | solution.py:31
  101.5 6.9 %collective-permute-start.11 = (f32[3,64,1]{2,1,0:T(8,128)S(1)}, f32[3,64,1]{2,1,0:T(8,128)S(1)}, u32[]{:S(2)}, u32[]{:S(2)}) collective-permute-start(f32[3,64,1]{2,1,0:T(8,128)S(1)} %get-tuple-element.193), channel_id=1, source_target_pairs={{0,2},{2,4},{4,6},{6,8},{8,10},{10,12},{12,14},{14,16},{16,18},{18... | collective-permute-start | bytes 2312 | tf_op jit(solution)/shard_map/ppermute | solution.py:30
  101.5 6.9 %collective-permute-start.8 = (f32[3,1,128]{2,1,0:T(1,128)S(1)}, f32[3,1,128]{2,1,0:T(1,128)S(1)}, u32[]{:S(2)}, u32[]{:S(2)}) collective-permute-start(f32[3,1,128]{2,1,0:T(1,128)S(1)} %get-tuple-element.190), channel_id=1, source_target_pairs={{1,0},{3,2},{5,4},{7,6},{9,8},{11,10},{13,12},{15,14},{17,16},{19,... | collective-permute-start | bytes 4616 | tf_op jit(solution)/shard_map/ppermute | solution.py:31
  102.8 5.6 %collective-permute-start.9 = (f32[3,1,128]{2,1,0:T(1,128)S(1)}, f32[3,1,128]{2,1,0:T(1,128)S(1)}, u32[]{:S(2)}, u32[]{:S(2)}) collective-permute-start(f32[3,1,128]{2,1,0:T(1,128)S(1)} %get-tuple-element.191), channel_id=1, source_target_pairs={{0,1},{2,3},{4,5},{6,7},{8,9},{10,11},{12,13},{14,15},{16,17},{18,... | collective-permute-start | bytes 4616 | tf_op jit(solution)/shard_map/ppermute | solution.py:30
  109.3 6.8 %collective-permute-start.14 = (f32[3,64,1]{2,1,0:T(8,128)S(1)}, f32[3,64,1]{2,1,0:T(8,128)S(1)}, u32[]{:S(2)}, u32[]{:S(2)}) collective-permute-start(f32[3,64,1]{2,1,0:T(8,128)S(1)} %get-tuple-element.188), channel_id=1, source_target_pairs={{2,0},{4,2},{6,4},{8,6},{10,8},{12,10},{14,12},{16,14},{18,16},{20... | collective-permute-start | bytes 2312 | tf_op jit(solution)/shard_map/ppermute | solution.py:31
  111.7 6.9 %collective-permute-start.15 = (f32[3,64,1]{2,1,0:T(8,128)S(1)}, f32[3,64,1]{2,1,0:T(8,128)S(1)}, u32[]{:S(2)}, u32[]{:S(2)}) collective-permute-start(f32[3,64,1]{2,1,0:T(8,128)S(1)} %get-tuple-element.189), channel_id=1, source_target_pairs={{0,2},{2,4},{4,6},{6,8},{8,10},{10,12},{12,14},{14,16},{16,18},{18... | collective-permute-start | bytes 2312 | tf_op jit(solution)/shard_map/ppermute | solution.py:30
  111.7 6.9 %collective-permute-start.12 = (f32[3,1,128]{2,1,0:T(1,128)S(1)}, f32[3,1,128]{2,1,0:T(1,128)S(1)}, u32[]{:S(2)}, u32[]{:S(2)}) collective-permute-start(f32[3,1,128]{2,1,0:T(1,128)S(1)} %get-tuple-element.186), channel_id=1, source_target_pairs={{1,0},{3,2},{5,4},{7,6},{9,8},{11,10},{13,12},{15,14},{17,16},{19,... | collective-permute-start | bytes 4616 | tf_op jit(solution)/shard_map/ppermute | solution.py:31
  113.0 5.6 %collective-permute-start.13 = (f32[3,1,128]{2,1,0:T(1,128)S(1)}, f32[3,1,128]{2,1,0:T(1,128)S(1)}, u32[]{:S(2)}, u32[]{:S(2)}) collective-permute-start(f32[3,1,128]{2,1,0:T(1,128)S(1)} %get-tuple-element.187), channel_id=1, source_target_pairs={{0,1},{2,3},{4,5},{6,7},{8,9},{10,11},{12,13},{14,15},{16,17},{18,... | collective-permute-start | bytes 4616 | tf_op jit(solution)/shard_map/ppermute | solution.py:30
  118.8 66.4 %copy-start.17 = (s32[128]{0:T(128)S(1)}, s32[128]{0:T(128)}, u32[]{:S(2)}) copy-start(s32[128]{0:T(128)} %copy-done.16) | copy-start | bytes 1540
  143.9 43.0 %copy-start = (f32[192,128]{1,0:T(8,128)}, f32[192,128]{1,0:T(8,128)S(1)}, u32[]{:S(2)}) copy-start(f32[192,128]{1,0:T(8,128)S(1)} %get-tuple-element.295) | copy-start | bytes 294916
  144.0 41.9 %copy-start.3 = (s32[16384]{0:T(1024)S(1)}, s32[16384]{0:T(1024)}, u32[]{:S(2)}) copy-start(s32[16384]{0:T(1024)} %param.14) | copy-start | bytes 196612
  144.0 41.9 %copy-start.5 = (f32[1,16384]{1,0:T(1,128)S(1)}, f32[1,16384]{1,0:T(1,128)}, u32[]{:S(2)}) copy-start(f32[1,16384]{1,0:T(1,128)} %copy-done.4) | copy-start | bytes 196612
  144.0 41.9 %copy-start.7 = (f32[1,16384]{1,0:T(1,128)S(1)}, f32[1,16384]{1,0:T(1,128)}, u32[]{:S(2)}) copy-start(f32[1,16384]{1,0:T(1,128)} %copy-done.6) | copy-start | bytes 196612
  144.0 41.9 %copy-start.9 = (f32[16384]{0:T(1024)S(1)}, f32[16384]{0:T(1024)}, u32[]{:S(2)}) copy-start(f32[16384]{0:T(1024)} %param.17) | copy-start | bytes 196612
  144.0 41.9 %copy-start.15 = (s32[128]{0:T(128)S(1)}, s32[128]{0:T(128)}, u32[]{:S(2)}) copy-start(s32[128]{0:T(128)} %copy-done.14) | copy-start | bytes 1540
where the time goes:
time: 188 us; the launch traced here: 187 us
  starting transfers between devices  54.2 us (29%)
  blocking collectives  41 us (22%)
  matrix products  38.2 us (20%)
  local copies, waits for them, and re-layouts  19.9 us (11%)
  other arithmetic  16.3 us (9%)
  waiting for transfers between devices  15 us (8%)
    all_to_all x1, blocking collectives, on_device(): lax.all_to_all(values_out, 'cells', split_axis=1, concat_axis=1, tiled=True)  41 us
    dot_general x8, matrix products, one_block(): jnp.dot(flat_field, cols_hot.T, precision=HIGHEST)  19.9 us
    all_to_all x1, starting transfers between devices, on_device(): lax.all_to_all(ids_out.reshape(1, owners, capacity, tile_len), 'cells', s...  15.4 us
    ppermute x8, starting transfers between devices, with_halo(): after = lax.ppermute(leading, axis, down)  14.9 us
    dot_general x8, matrix products, add_block(): return (total + jnp.dot(weighted, cols_hot, precision=HIGHEST), None)  14.9 us
    ppermute x8, starting transfers between devices, with_halo(): before = lax.ppermute(last, axis, up)  13.5 us
    all_to_all x1, starting transfers between devices, on_device(): lax.all_to_all(push_out.reshape(3, owners, capacity, tile_len), 'cells',...  10.4 us
    dynamic_slice x16, local copies, waits for them, and re-layouts, on_device(): lax.scan(add_block, jnp.zeros((3 * patch_rows, patch_cols), jnp.float32),...  8.61 us
  transfers between devices with their start and end apart: 18, of which 5 were waited for; matrix products, arithmetic and copies ran while one was open for 22% of the time, Pallas kernels for 0%

commit v1 on v0

v1 whole, which is shorter than its diff:
```python
import math

import jax
import jax.numpy as jnp
from jax import lax
from jax.experimental import pallas as pl
from jax.experimental.pallas import tpu as pltpu
from jax.sharding import PartitionSpec as P

SUBSTEPS = 4


SPRING_RATE = 2.0
SOFTNESS = 0.25
APPROACH_DAMP = 0.5
FRICTION = 0.4
SLIP_SPEED = 0.1
HOOP_RATE = 0.5
SHELL_DAMP = 0.3
TIME_STEP = 0.2
FULL_TURN = 2.0 * math.pi
HIGHEST = lax.Precision.HIGHEST
BF16 = jnp.bfloat16
F32 = jnp.float32


def normals(column, total_cols):
    angle = (column.astype(jnp.float32) + 0.5) * (FULL_TURN / total_cols)
    return (jnp.cos(angle), jnp.sin(angle))


def contact_push(offset, velocity, radius, cached, facing_cos, facing_sin):
    reach = offset[0] * facing_cos + offset[1] * facing_sin
    intersection = radius + reach - (cached[0] * facing_cos + cached[1] * facing_sin)
    spring = SPRING_RATE * SOFTNESS * jax.nn.softplus(intersection / SOFTNESS)
    approach = velocity[0] * facing_cos + velocity[1] * facing_sin
    pressing = spring + APPROACH_DAMP * approach
    slide_x = velocity[0] - approach * facing_cos
    slide_y = velocity[1] - approach * facing_sin
    slide_z = velocity[2]
    speed = jnp.sqrt(
        slide_x * slide_x + slide_y * slide_y + slide_z * slide_z + SLIP_SPEED * SLIP_SPEED
    )
    friction = FRICTION * spring / speed
    push = jnp.stack(
        [
            pressing * facing_cos + friction * slide_x,
            pressing * facing_sin + friction * slide_y,
            friction * slide_z,
        ]
    )
    return (push, reach)


def advance(displace, velocity, traction, stiffness, vertical, sideways, facing_cos, facing_sin):
    internal = stiffness * (vertical + sideways - 4.0 * displace)
    radial = HOOP_RATE * stiffness * (displace[0] * facing_cos + displace[1] * facing_sin)
    hoop = jnp.stack([radial * facing_cos, radial * facing_sin, jnp.zeros_like(radial)])
    acceleration = internal - hoop + traction - SHELL_DAMP * velocity
    velocity = velocity + TIME_STEP * acceleration
    return (displace + TIME_STEP * velocity, velocity)


def to_bf16_grid(x):
    return lax.reduce_precision(x, exponent_bits=8, mantissa_bits=7)


def _split_ids(ids, shift):
    rows = lax.shift_right_logical(ids, jnp.int32(shift))
    cols = jnp.bitwise_and(ids, jnp.int32((1 << shift) - 1))
    return rows, cols


def _scatter_kernel(ids_ref, push_ref, out_ref, *, patch_rows, shift):
    n_rows, lanes = ids_ref.shape
    patch_cols = 1 << shift
    comps = push_ref.shape[0] // 2
    row_iota = lax.broadcasted_iota(jnp.int32, (patch_rows, lanes), 0)
    col_iota = lax.broadcasted_iota(jnp.int32, (patch_cols, lanes), 0)
    out_ref[...] = jnp.zeros_like(out_ref)

    def step(i, carry):
        base = pl.multiple_of(i * 8, 8)
        ids8 = ids_ref[pl.ds(base, 8), :]
        push8 = push_ref[:, pl.ds(base, 8), :]
        total = None
        for g in range(8):
            rows, cols = _split_ids(ids8[g : g + 1, :], shift)
            rhot = (row_iota == rows).astype(BF16)
            chot = (col_iota == cols).astype(BF16)
            his, los = [], []
            for c in range(comps):
                hi = push8[c, g : g + 1, :].astype(BF16)
                lo = push8[comps + c, g : g + 1, :].astype(BF16)
                his.append(rhot * hi)
                los.append(rhot * lo)
            lhs = jnp.concatenate(
                [jnp.concatenate(his, axis=0), jnp.concatenate(los, axis=0)], axis=1
            )
            rhs = jnp.concatenate([chot, chot], axis=1)
            part = lax.dot_general(
                lhs, rhs, (((1,), (1,)), ((), ())), preferred_element_type=F32
            )
            total = part if total is None else total + part
        out_ref[...] += total
        return carry

    lax.fori_loop(0, n_rows // 8, step, 0)


def scatter_traction(ids, push, patch_rows, patch_cols):
    shift = patch_cols.bit_length() - 1
    comps = push.shape[0]
    hi = to_bf16_grid(push)
    parts = jnp.concatenate([hi, push - hi], axis=0)
    kernel = lambda *refs: _scatter_kernel(*refs, patch_rows=patch_rows, shift=shift)
    out = pl.pallas_call(
        kernel,
        out_shape=jax.ShapeDtypeStruct((comps * patch_rows, patch_cols), F32),
        in_specs=[pl.BlockSpec(memory_space=pltpu.VMEM)] * 2,
        out_specs=pl.BlockSpec(memory_space=pltpu.VMEM),
        name="scatter_traction",
    )(ids, parts)
    return out.reshape(comps, patch_rows, patch_cols)


def _gather_kernel(ids_ref, wt_ref, out_ref, *, patch_rows, shift):
    n_rows, lanes = ids_ref.shape
    patch_cols = 1 << shift
    parts = wt_ref.shape[1] // patch_rows
    row_iota = lax.broadcasted_iota(jnp.int32, (patch_rows, lanes), 0)
    col_iota = lax.broadcasted_iota(jnp.int32, (patch_cols, lanes), 0)

    def step(i, carry):
        base = pl.multiple_of(i * 8, 8)
        ids8 = ids_ref[pl.ds(base, 8), :]
        wt = wt_ref[...]
        outs = []
        for g in range(8):
            rows, cols = _split_ids(ids8[g : g + 1, :], shift)
            rhot = (row_iota == rows).astype(BF16)
            rhs = jnp.concatenate([rhot] * parts, axis=0)
            picked = jnp.dot(wt, rhs, preferred_element_type=F32)
            sel = jnp.where(col_iota == cols, picked, 0.0)
            outs.append(jnp.sum(sel, axis=0, keepdims=True))
        out_ref[pl.ds(base, 8), :] = jnp.concatenate(outs, axis=0)
        return carry

    lax.fori_loop(0, n_rows // 8, step, 0)


def gather_field(ids, field):
    patch_rows, patch_cols = field.shape
    shift = patch_cols.bit_length() - 1
    hi = to_bf16_grid(field)
    rest = field - hi
    mid = to_bf16_grid(rest)
    lo = rest - mid
    wt = jnp.concatenate([hi.T, mid.T, lo.T], axis=1).astype(BF16)
    kernel = lambda *refs: _gather_kernel(*refs, patch_rows=patch_rows, shift=shift)
    return pl.pallas_call(
        kernel,
        out_shape=jax.ShapeDtypeStruct(ids.shape, F32),
        in_specs=[pl.BlockSpec(memory_space=pltpu.VMEM)] * 2,
        out_specs=pl.BlockSpec(memory_space=pltpu.VMEM),
        name="gather_field",
    )(ids, wt)


def with_halo(x, width):
    ch, rows, cols = x.shape
    n = lax.axis_size("cells")
    m = lax.axis_size("slab")
    slab = lax.axis_index("slab")
    fwd = [(i, (i + 1) % n) for i in range(n)]
    bwd = [((i + 1) % n, i) for i in range(n)]
    left = lax.ppermute(x[:, :, cols - width :], "cells", fwd)
    right = lax.ppermute(x[:, :, :width], "cells", bwd)
    facing = jnp.where(slab == 0, x[:, rows - width :, :], x[:, :width, :])
    swap = [(j, m - 1 - j) for j in range(m)]
    across = lax.ppermute(facing, "slab", swap)
    diag_fwd = [(i * m + j, ((i + 1) % n) * m + (m - 1 - j)) for i in range(n) for j in range(m)]
    diag_bwd = [(i * m + j, ((i - 1) % n) * m + (m - 1 - j)) for i in range(n) for j in range(m)]
    corner_left = lax.ppermute(facing[:, :, cols - width :], ("cells", "slab"), diag_fwd)
    corner_right = lax.ppermute(facing[:, :, :width], ("cells", "slab"), diag_bwd)
    band = jnp.concatenate([left, x, right], axis=2)
    cap = jnp.concatenate([corner_left, across, corner_right], axis=2)
    zero = jnp.zeros_like(cap)
    top = jnp.where(slab == 0, zero, cap)
    bottom = jnp.where(slab == 0, cap, zero)
    return jnp.concatenate([top, band, bottom], axis=1)


def on_device(
    block_owner,
    contact_elem,
    grain_offset,
    grain_vel,
    grain_radius,
    disp_cached,
    wall_disp,
    wall_vel,
    wall_stiff,
):
    owners = lax.axis_size("cells")
    blocks = block_owner.shape[0]
    tile_len = contact_elem.shape[0] // blocks
    patch_rows, patch_cols = wall_stiff.shape
    total_cols = patch_cols * owners
    capacity = 2 * (blocks // owners)
    slots = owners * capacity
    width = SUBSTEPS
    elements = contact_elem.reshape(blocks, tile_len)
    radius_tiles = grain_radius.reshape(blocks, tile_len)
    col_index = block_owner[:, None] * patch_cols + elements % patch_cols
    facing_cos, facing_sin = normals(col_index, total_cols)
    push, reach = contact_push(
        grain_offset.reshape(3, blocks, tile_len),
        grain_vel.reshape(3, blocks, tile_len),
        radius_tiles,
        disp_cached.reshape(3, blocks, tile_len),
        facing_cos,
        facing_sin,
    )
    patches = jnp.arange(owners, dtype=jnp.int32)
    member = (block_owner[:, None] == patches[None, :]).astype(jnp.float32)
    tile_ids = jnp.arange(blocks, dtype=jnp.int32)
    before = (tile_ids[None, :] < tile_ids[:, None]).astype(jnp.float32)
    earlier = jnp.dot(before, member, precision=HIGHEST)
    slot = block_owner * capacity + jnp.sum(earlier * member, axis=1).astype(jnp.int32)
    placing = (slot[None, :] == jnp.arange(slots, dtype=jnp.int32)[:, None]).astype(jnp.float32)
    payload = jnp.concatenate([push, elements.astype(jnp.float32)[None]], axis=0)
    send = jnp.einsum("sb,cbl->csl", placing, payload, precision=HIGHEST)
    recv = lax.all_to_all(
        send.reshape(4, owners, capacity, tile_len),
        "cells",
        split_axis=1,
        concat_axis=1,
        tiled=True,
    ).reshape(4, slots, tile_len)
    ids_in = recv[3].astype(jnp.int32)

    state = jnp.concatenate([wall_disp, wall_vel, wall_stiff[None]], axis=0)
    state_ext = with_halo(state, width)
    d_ext, v_ext, stiff_ext = state_ext[:3], state_ext[3:6], state_ext[6]

    traction = scatter_traction(ids_in, recv[:3], patch_rows, patch_cols)
    traction_ext = with_halo(traction, width)

    first_col = lax.axis_index("cells") * patch_cols
    ext_cols = (first_col - width + jnp.arange(patch_cols + 2 * width, dtype=jnp.int32)) % total_cols
    ext_cos, ext_sin = normals(ext_cols, total_cols)
    displace, velocity = (d_ext, v_ext)
    for substep in range(SUBSTEPS):
        padded = jnp.pad(displace, ((0, 0), (1, 1), (0, 0)))
        vertical = padded[:, 2:] + padded[:, :-2]
        padded_c = jnp.pad(displace, ((0, 0), (0, 0), (1, 1)))
        sideways = padded_c[:, :, 2:] + padded_c[:, :, :-2]
        displace, velocity = advance(
            displace, velocity, traction_ext, stiff_ext, vertical, sideways, ext_cos, ext_sin
        )
    wall_next = displace[:, width : width + patch_rows, width : width + patch_cols]
    own_cos = ext_cos[width : width + patch_cols]
    own_sin = ext_sin[width : width + patch_cols]
    radial_field = wall_next[0] * own_cos + wall_next[1] * own_sin
    landed_out = gather_field(ids_in, radial_field)
    landed_back = lax.all_to_all(
        landed_out.reshape(owners, capacity, tile_len),
        "cells",
        split_axis=0,
        concat_axis=0,
        tiled=True,
    ).reshape(slots, tile_len)
    landed = jnp.einsum("sb,sl->bl", placing, landed_back, precision=HIGHEST)
    contact_gap = radius_tiles + reach - landed
    return (wall_next, contact_gap.reshape(-1))


def solution(mesh):
    return jax.shard_map(
        on_device,
        mesh=mesh,
        in_specs=(
            P(("cells", "slab")),
            P(("cells", "slab")),
            P(None, ("cells", "slab")),
            P(None, ("cells", "slab")),
            P(("cells", "slab")),
            P(None, ("cells", "slab")),
            P(None, "slab", "cells"),
            P(None, "slab", "cells"),
            P("slab", "cells"),
        ),
        out_specs=(P(None, "slab", "cells"), P(("cells", "slab"))),
        check_vma=False,
    )
```

time: 188 us -> 117 us (0.62)
  blocking collectives: 41 us -> 0 us
  matrix products: 38.2 us -> 1.68 us
  Pallas kernels: 0 us -> 25.2 us
  waiting for transfers between devices: 15 us -> 27.7 us
  starting transfers between devices: 54.2 us -> 44.1 us
  local copies, waits for them, and re-layouts: 19.9 us -> 9.91 us
  other arithmetic: 16.3 us -> 6.54 us
    all_to_all x1 -> x0, blocking collectives: 41 us -> none  [on_device(): lax.all_to_all(values_out, 'cells', split_axis=1, concat_axis=1, tiled=True)]
    dot_general x19 -> x2, matrix products: 37.3 us -> 1.5 us  [the longest x1 1.11 us: on_device(): landed = jnp.einsum('sb,sl->bl', placing, landed_back, precision=HIGHEST)]
    pallas_call x0 -> x2, Pallas kernels: none -> 25.2 us  [the longest x1 13.8 us: scatter_traction(): pl.pallas_call(kernel, out_shape=jax.ShapeDtypeStruct((comps * patch_rows...]
    ppermute x16 -> x10, starting transfers between devices: 28.4 us -> 12.5 us  [the longest x2 8.61 us: with_halo(): right = lax.ppermute(x[:, :, :width], 'cells', bwd)]
    dynamic_slice x16 -> x0, local copies, waits for them, and re-layouts: 8.61 us -> none  [on_device(): lax.scan(add_block, jnp.zeros((3 * patch_rows, patch_cols), jnp.float32),...]
    all_to_all x2, waiting for transfers between devices: 9.25 us -> 17.8 us  [the longest x1 10.9 us: on_device(): lax.all_to_all(landed_out.reshape(owners, capacity, tile_len), 'cells', s...]
    all_to_all x2, starting transfers between devices: 25.8 us -> 31.7 us  [the longest x1 16.2 us: on_device(): lax.all_to_all(landed_out.reshape(owners, capacity, tile_len), 'cells', s...]
    unnamed x38 -> x20, local copies, waits for them, and re-layouts: 0.09 us -> 4.72 us
  transfers between devices with their start and end apart: 18 -> 12, of which waited for: 5 -> 6; matrix products, arithmetic and copies ran while one was open for 22% -> 7% of each run, Pallas kernels for 0% -> 0%
where the time goes in v1:
time: 117 us; the launch traced here: 116 us
  starting transfers between devices  44.1 us (38%)
  waiting for transfers between devices  27.7 us (24%)
  Pallas kernels  25.2 us (22%)
  local copies, waits for them, and re-layouts  9.91 us (8%)
  other arithmetic  6.54 us (6%)
  matrix products  1.68 us (1%)
    all_to_all x1, starting transfers between devices, on_device(): lax.all_to_all(landed_out.reshape(owners, capacity, tile_len), 'cells', s...  16.2 us
    all_to_all x1, starting transfers between devices, on_device(): lax.all_to_all(send.reshape(4, owners, capacity, tile_len), 'cells', spli...  15.4 us
    pallas_call x1, Pallas kernels, scatter_traction(): pl.pallas_call(kernel, out_shape=jax.ShapeDtypeStruct((comps * patch_rows...  13.8 us
    pallas_call x1, Pallas kernels, gather_field(): pl.pallas_call(kernel, out_shape=jax.ShapeDtypeStruct(ids.shape, F32), in...  11.3 us
    all_to_all x1, waiting for transfers between devices, on_device(): lax.all_to_all(landed_out.reshape(owners, capacity, tile_len), 'cells', s...  10.9 us
    ppermute x2, starting transfers between devices, with_halo(): right = lax.ppermute(x[:, :, :width], 'cells', bwd)  8.61 us
    ppermute x2, waiting for transfers between devices, with_halo(): left = lax.ppermute(x[:, :, cols - width:], 'cells', fwd)  8.43 us
    all_to_all x1, waiting for transfers between devices, on_device(): lax.all_to_all(send.reshape(4, owners, capacity, tile_len), 'cells', spli...  6.82 us
  transfers between devices with their start and end apart: 12, of which 6 were waited for; matrix products, arithmetic and copies ran while one was open for 7% of the time, Pallas kernels for 0%

profile of v1, /device:TPU:2, one launch (start us, length us, event | category | flops | bytes accessed | tf_op | source)
XLA Modules:
  0.0 116.2 jit_solution(15888970528704962108)
XLA Ops:
  0.6 0.9 copy.83
  1.7 0.8 copy-done.4
  2.6 0.2 slice_select_fusion
  2.9 0.5 copy-done
  3.6 0.2 copy-done.2
  3.8 0.1 fusion.96
  4.2 0.6 copy-done.7
  4.8 0.2 fusion.1
  5.3 0.7 copy-done.1
  6.5 0.4 multiply_add_fusion.4
  6.9 0.3 multiply_add_fusion.3
  7.2 0.4 convolution_bitcast_fusion
  7.6 0.2 copy.107
  7.8 1.0 copy.108
  8.8 15.4 %all-to-all-start = ((f32[4,128,2,128]{3,2,0,1:T(2,128)}), f32[4,128,2,128]{3,2,0,1:T(2,128)S(1)}, u32[]{:S(2)}, u32[]{:S(2)}) async-start(f32[4,128,2,128]{3,2,0,1:T(2,128)} %copy.108), calls=%async_computation | async-start | bytes 1048576 | tf_op jit(solution)/shard_map/all_to_all | solution.py:234
  24.2 1.6 %collective-permute-start.2 = (f32[7,4,4]{1,2,0:T(4,128)S(1)}, f32[7,4,4]{1,2,0:T(4,128)S(1)}, u32[]{:S(2)}, u32[]{:S(2)}) collective-permute-start(f32[7,4,4]{1,2,0:T(4,128)S(1)} %get-tuple-element.27), channel_id=1, source_target_pairs={{0,255},{1,254},{2,1},{3,0},{4,3},{5,2},{6,5},{7,4},{8,7},{9,6},{1... | collective-permute-start | bytes 1352 | tf_op jit(solution)/shard_map/ppermute | solution.py:185
  25.8 0.2 collective-permute-start
  26.0 4.9 %collective-permute-start.4 = (f32[7,64,4]{1,2,0:T(4,128)S(1)}, f32[7,64,4]{1,2,0:T(4,128)S(1)}, u32[]{:S(2)}, u32[]{:S(2)}) collective-permute-start(f32[7,64,4]{1,2,0:T(4,128)S(1)} %get-tuple-element.25), channel_id=1, source_target_pairs={{2,0},{4,2},{6,4},{8,6},{10,8},{12,10},{14,12},{16,14},{18,16},{20... | collective-permute-start | bytes 21512 | tf_op jit(solution)/shard_map/ppermute | solution.py:178
  31.5 0.2 copy.87
  31.8 0.2 copy.90
  32.0 0.2 copy.89
  32.3 4.5 %collective-permute-done.3 = f32[7,64,4]{1,2,0:T(4,128)S(1)} collective-permute-done((f32[7,64,4]{1,2,0:T(4,128)S(1)}, f32[7,64,4]{1,2,0:T(4,128)S(1)}, u32[]{:S(2)}, u32[]{:S(2)}) %collective-permute-start.3) | collective-permute-done | bytes 7200 | tf_op jit(solution)/shard_map/ppermute | solution.py:177
  36.8 0.3 pad_maximum_fusion.1
  37.2 0.2 broadcast_multiply_fusion.7
  37.5 6.8 %all-to-all-done = f32[4,128,2,128]{3,2,0,1:T(2,128)S(1)} async-done(((f32[4,128,2,128]{3,2,0,1:T(2,128)}), f32[4,128,2,128]{3,2,0,1:T(2,128)S(1)}, u32[]{:S(2)}, u32[]{:S(2)}) %all-to-all-start) | async-done | bytes 524320 | tf_op jit(solution)/shard_map/all_to_all | solution.py:234
  44.5 0.1 copy.109
  44.7 1.0 pad_maximum_fusion.refs_1_
  45.6 0.7 slice_convert_fusion
  46.3 13.8 %scatter_traction.1 = f32[192,128]{1,0:T(8,128)} custom-call(s32[256,128]{1,0:T(8,128)} %bitcast.66, f32[6,256,128]{2,1,0:T(8,128)} %pad_maximum_fusion.refs_1_), custom_call_target="tpu_custom_call" | custom-call | tf_op jit(solution)/shard_map/scatter_traction/pallas_call | solution.py:117
  60.2 0.7 slice_select_fusion.1
  61.0 1.0 copy.110
  62.0 1.9 %collective-permute-start.7 = (f32[3,4,4]{2,1,0:T(4,128)S(1)}, f32[3,4,4]{2,1,0:T(4,128)S(1)}, u32[]{:S(2)}, u32[]{:S(2)}) collective-permute-start(f32[3,4,4]{2,1,0:T(4,128)S(1)} %get-tuple-element.54), channel_id=1, source_target_pairs={{0,255},{1,254},{2,1},{3,0},{4,3},{5,2},{6,5},{7,4},{8,7},{9,6},{1... | collective-permute-start | bytes 584 | tf_op jit(solution)/shard_map/ppermute | solution.py:185
  64.0 3.8 %collective-permute-start.9 = (f32[3,64,4]{1,2,0:T(4,128)S(1)}, f32[3,64,4]{1,2,0:T(4,128)S(1)}, u32[]{:S(2)}, u32[]{:S(2)}) collective-permute-start(f32[3,64,4]{1,2,0:T(4,128)S(1)} %get-tuple-element.46), channel_id=1, source_target_pairs={{2,0},{4,2},{6,4},{8,6},{10,8},{12,10},{14,12},{16,14},{18,16},{20... | collective-permute-start | bytes 9224 | tf_op jit(solution)/shard_map/ppermute | solution.py:178
  67.7 1.4 %collective-permute-done.5 = f32[3,4,4]{2,1,0:T(4,128)S(1)} collective-permute-done((f32[3,4,4]{2,1,0:T(4,128)S(1)}, f32[3,4,4]{2,1,0:T(4,128)S(1)}, u32[]{:S(2)}, u32[]{:S(2)}) %collective-permute-start.5) | collective-permute-done | bytes 224 | tf_op jit(solution)/shard_map/ppermute | solution.py:184
  69.2 0.2 copy.114
  69.4 0.2 copy.113
  69.5 3.9 %collective-permute-done.8 = f32[3,64,4]{1,2,0:T(4,128)S(1)} collective-permute-done((f32[3,64,4]{1,2,0:T(4,128)S(1)}, f32[3,64,4]{1,2,0:T(4,128)S(1)}, u32[]{:S(2)}, u32[]{:S(2)}) %collective-permute-start.8) | collective-permute-done | bytes 3104 | tf_op jit(solution)/shard_map/ppermute | solution.py:177
  73.4 0.3 multiply_add_fusion.2
  73.9 0.2 multiply_add_fusion.1
  74.2 0.2 multiply_add_fusion
  74.6 0.2 fusion.46
  74.9 0.1 fusion.74
  75.0 0.7 pad_maximum_fusion.5.refs_1_
  75.8 11.3 %gather_field.1 = f32[256,128]{1,0:T(8,128)} custom-call(s32[256,128]{1,0:T(8,128)} %bitcast.67, bf16[128,192]{1,0:T(8,128)(2,1)} %pad_maximum_fusion.5.refs_1_), custom_call_target="tpu_custom_call" | custom-call | tf_op jit(solution)/shard_map/gather_field/pallas_call | solution.py:161
  87.1 16.2 %all-to-all-start.1 = ((f32[128,2,128]{2,1,0:T(2,128)}), f32[128,2,128]{2,1,0:T(2,128)S(1)}, u32[]{:S(2)}, u32[]{:S(2)}) async-start(f32[128,2,128]{2,1,0:T(2,128)} %bitcast.73), calls=%async_computation.1 | async-start | bytes 262144 | tf_op jit(solution)/shard_map/all_to_all | solution.py:267
  103.4 0.8 copy.115
  104.2 10.9 %all-to-all-done.1 = f32[128,2,128]{2,1,0:T(2,128)S(1)} async-done(((f32[128,2,128]{2,1,0:T(2,128)}), f32[128,2,128]{2,1,0:T(2,128)S(1)}, u32[]{:S(2)}, u32[]{:S(2)}) %all-to-all-start.1) | async-done | bytes 131104 | tf_op jit(solution)/shard_map/all_to_all | solution.py:267
  115.1 1.1 fusion
  (60 shorter events, 3.1 us)
Async XLA Ops:
  0.6 0.9 copy-start.3
  1.5 0.9 copy-start.4
  2.6 0.8 copy-start
  2.8 1.0 copy-start.2
  2.8 28.6 %collective-permute-start.1 = (f32[7,4,128]{1,2,0:T(8,128)S(1)}, f32[7,4,128]{1,2,0:T(8,128)S(1)}, u32[]{:S(2)}, u32[]{:S(2)}) collective-permute-start(f32[7,4,128]{1,2,0:T(8,128)S(1)} %slice_select_fusion), channel_id=1, source_target_pairs={{0,1},{1,0},{2,3},{3,2},{4,5},{5,4},{6,7},{7,6},{8,9},{9,8},{10,11... | collective-permute-start | bytes 43016 | tf_op jit(solution)/shard_map/ppermute | solution.py:181
  3.9 1.1 copy-start.5
  4.1 0.7 copy-start.7
  5.0 1.2 copy-start.6
  5.2 0.8 copy-start.1
  8.8 35.6 %all-to-all-start = ((f32[4,128,2,128]{3,2,0,1:T(2,128)}), f32[4,128,2,128]{3,2,0,1:T(2,128)S(1)}, u32[]{:S(2)}, u32[]{:S(2)}) async-start(f32[4,128,2,128]{3,2,0,1:T(2,128)} %copy.108), calls=%async_computation | async-start | bytes 1048576 | tf_op jit(solution)/shard_map/all_to_all | solution.py:234
  24.2 7.0 %collective-permute-start.2 = (f32[7,4,4]{1,2,0:T(4,128)S(1)}, f32[7,4,4]{1,2,0:T(4,128)S(1)}, u32[]{:S(2)}, u32[]{:S(2)}) collective-permute-start(f32[7,4,4]{1,2,0:T(4,128)S(1)} %get-tuple-element.27), channel_id=1, source_target_pairs={{0,255},{1,254},{2,1},{3,0},{4,3},{5,2},{6,5},{7,4},{8,7},{9,6},{1... | collective-permute-start | bytes 1352 | tf_op jit(solution)/shard_map/ppermute | solution.py:185
  25.8 5.5 %collective-permute-start = (f32[7,4,4]{1,2,0:T(4,128)S(1)}, f32[7,4,4]{1,2,0:T(4,128)S(1)}, u32[]{:S(2)}, u32[]{:S(2)}) collective-permute-start(f32[7,4,4]{1,2,0:T(4,128)S(1)} %get-tuple-element.26), channel_id=1, source_target_pairs={{0,3},{1,2},{2,5},{3,4},{4,7},{5,6},{6,9},{7,8},{8,11},{9,10},{10,... | collective-permute-start | bytes 1352 | tf_op jit(solution)/shard_map/ppermute | solution.py:184
  26.0 6.3 %collective-permute-start.4 = (f32[7,64,4]{1,2,0:T(4,128)S(1)}, f32[7,64,4]{1,2,0:T(4,128)S(1)}, u32[]{:S(2)}, u32[]{:S(2)}) collective-permute-start(f32[7,64,4]{1,2,0:T(4,128)S(1)} %get-tuple-element.25), channel_id=1, source_target_pairs={{2,0},{4,2},{6,4},{8,6},{10,8},{12,10},{14,12},{16,14},{18,16},{20... | collective-permute-start | bytes 21512 | tf_op jit(solution)/shard_map/ppermute | solution.py:178
  30.9 5.9 %collective-permute-start.3 = (f32[7,64,4]{1,2,0:T(4,128)S(1)}, f32[7,64,4]{1,2,0:T(4,128)S(1)}, u32[]{:S(2)}, u32[]{:S(2)}) collective-permute-start(f32[7,64,4]{1,2,0:T(4,128)S(1)} %get-tuple-element.24), channel_id=1, source_target_pairs={{0,2},{2,4},{4,6},{6,8},{8,10},{10,12},{12,14},{14,16},{16,18},{18... | collective-permute-start | bytes 21512 | tf_op jit(solution)/shard_map/ppermute | solution.py:177
  61.0 8.1 %collective-permute-start.6 = (f32[3,4,128]{2,1,0:T(4,128)S(1)}, f32[3,4,128]{2,1,0:T(4,128)S(1)}, u32[]{:S(2)}, u32[]{:S(2)}) collective-permute-start(f32[3,4,128]{2,1,0:T(4,128)S(1)} %slice_select_fusion.1), channel_id=1, source_target_pairs={{0,1},{1,0},{2,3},{3,2},{4,5},{5,4},{6,7},{7,6},{8,9},{9,8},{10,11... | collective-permute-start | bytes 18440 | tf_op jit(solution)/shard_map/ppermute | solution.py:181
  62.0 5.7 %collective-permute-start.7 = (f32[3,4,4]{2,1,0:T(4,128)S(1)}, f32[3,4,4]{2,1,0:T(4,128)S(1)}, u32[]{:S(2)}, u32[]{:S(2)}) collective-permute-start(f32[3,4,4]{2,1,0:T(4,128)S(1)} %get-tuple-element.54), channel_id=1, source_target_pairs={{0,255},{1,254},{2,1},{3,0},{4,3},{5,2},{6,5},{7,4},{8,7},{9,6},{1... | collective-permute-start | bytes 584 | tf_op jit(solution)/shard_map/ppermute | solution.py:185
  63.9 5.2 %collective-permute-start.5 = (f32[3,4,4]{2,1,0:T(4,128)S(1)}, f32[3,4,4]{2,1,0:T(4,128)S(1)}, u32[]{:S(2)}, u32[]{:S(2)}) collective-permute-start(f32[3,4,4]{2,1,0:T(4,128)S(1)} %get-tuple-element.53), channel_id=1, source_target_pairs={{0,3},{1,2},{2,5},{3,4},{4,7},{5,6},{6,9},{7,8},{8,11},{9,10},{10,... | collective-permute-start | bytes 584 | tf_op jit(solution)/shard_map/ppermute | solution.py:184
  64.0 5.6 %collective-permute-start.9 = (f32[3,64,4]{1,2,0:T(4,128)S(1)}, f32[3,64,4]{1,2,0:T(4,128)S(1)}, u32[]{:S(2)}, u32[]{:S(2)}) collective-permute-start(f32[3,64,4]{1,2,0:T(4,128)S(1)} %get-tuple-element.46), channel_id=1, source_target_pairs={{2,0},{4,2},{6,4},{8,6},{10,8},{12,10},{14,12},{16,14},{18,16},{20... | collective-permute-start | bytes 9224 | tf_op jit(solution)/shard_map/ppermute | solution.py:178
  67.7 5.7 %collective-permute-start.8 = (f32[3,64,4]{1,2,0:T(4,128)S(1)}, f32[3,64,4]{1,2,0:T(4,128)S(1)}, u32[]{:S(2)}, u32[]{:S(2)}) collective-permute-start(f32[3,64,4]{1,2,0:T(4,128)S(1)} %get-tuple-element.45), channel_id=1, source_target_pairs={{0,2},{2,4},{4,6},{6,8},{8,10},{10,12},{12,14},{14,16},{16,18},{18... | collective-permute-start | bytes 9224 | tf_op jit(solution)/shard_map/ppermute | solution.py:177
  87.1 28.1 %all-to-all-start.1 = ((f32[128,2,128]{2,1,0:T(2,128)}), f32[128,2,128]{2,1,0:T(2,128)S(1)}, u32[]{:S(2)}, u32[]{:S(2)}) async-start(f32[128,2,128]{2,1,0:T(2,128)} %bitcast.73), calls=%async_computation.1 | async-start | bytes 262144 | tf_op jit(solution)/shard_map/all_to_all | solution.py:267

commit v2 on v1

--- a/solution.py
+++ b/solution.py
@@ -240,12 +240,11 @@
     ).reshape(4, slots, tile_len)
     ids_in = recv[3].astype(jnp.int32)
 
-    state = jnp.concatenate([wall_disp, wall_vel, wall_stiff[None]], axis=0)
+    traction = scatter_traction(ids_in, recv[:3], patch_rows, patch_cols)
+    state = jnp.concatenate([wall_disp, wall_vel, wall_stiff[None], traction], axis=0)
     state_ext = with_halo(state, width)
     d_ext, v_ext, stiff_ext = state_ext[:3], state_ext[3:6], state_ext[6]
-
-    traction = scatter_traction(ids_in, recv[:3], patch_rows, patch_cols)
-    traction_ext = with_halo(traction, width)
+    traction_ext = state_ext[7:10]
 
     first_col = lax.axis_index("cells") * patch_cols
     ext_cols = (first_col - width + jnp.arange(patch_cols + 2 * width, dtype=jnp.int32)) % total_cols

time: 117 us -> 117 us (level)
  starting transfers between devices: 44.1 us -> 41.9 us
  waiting for transfers between devices: 27.7 us -> 29.8 us
    all_to_all x1, waiting for transfers between devices: 6.82 us -> 18.1 us  [on_device(): lax.all_to_all(send.reshape(4, owners, capacity, tile_len), 'cells', spli...]
    ppermute x2 -> x1, waiting for transfers between devices: 8.43 us -> 0.74 us  [with_halo(): left = lax.ppermute(x[:, :, cols - width:], 'cells', fwd)]
    ppermute x2 -> x1, starting transfers between devices: 8.61 us -> 4.12 us  [with_halo(): right = lax.ppermute(x[:, :, :width], 'cells', bwd)]
    all_to_all x1, starting transfers between devices: 16.2 us -> 18.3 us  [on_device(): lax.all_to_all(landed_out.reshape(owners, capacity, tile_len), 'cells', s...]
    ppermute x2 -> x1, waiting for transfers between devices: 1.4 us -> 0.01 us  [with_halo(): lax.ppermute(facing[:, :, cols - width:], ('cells', 'slab'), diag_fwd)]
    slice x1, local copies, waits for them, and re-layouts: 0.14 us -> 1.38 us  [contact_push(): approach = velocity[0] * facing_cos + velocity[1] * facing_sin]
    ppermute x2 -> x1, starting transfers between devices: 3.55 us -> 3.84 us  [with_halo(): lax.ppermute(facing[:, :, :width], ('cells', 'slab'), diag_bwd)]
  transfers between devices with their start and end apart: 12 -> 7, of which waited for: 6 -> 3; matrix products, arithmetic and copies ran while one was open for 7% -> 2% of each run, Pallas kernels for 0% -> 0%
where the time goes in v2:
time: 117 us; the launch traced here: 116 us
  starting transfers between devices  41.9 us (36%)
  waiting for transfers between devices  29.8 us (25%)
  Pallas kernels  25.2 us (22%)
  local copies, waits for them, and re-layouts  10.8 us (9%)
  other arithmetic  5.64 us (5%)
  matrix products  1.68 us (1%)
    all_to_all x1, starting transfers between devices, on_device(): lax.all_to_all(landed_out.reshape(owners, capacity, tile_len), 'cells', s...  18.3 us
    all_to_all x1, waiting for transfers between devices, on_device(): lax.all_to_all(send.reshape(4, owners, capacity, tile_len), 'cells', spli...  18.1 us
    all_to_all x1, starting transfers between devices, on_device(): lax.all_to_all(send.reshape(4, owners, capacity, tile_len), 'cells', spli...  15.6 us
    pallas_call x1, Pallas kernels, scatter_traction(): pl.pallas_call(kernel, out_shape=jax.ShapeDtypeStruct((comps * patch_rows...  13.8 us
    pallas_call x1, Pallas kernels, gather_field(): pl.pallas_call(kernel, out_shape=jax.ShapeDtypeStruct(ids.shape, F32), in...  11.3 us
    all_to_all x1, waiting for transfers between devices, on_device(): lax.all_to_all(landed_out.reshape(owners, capacity, tile_len), 'cells', s...  10.9 us
    unnamed x20, local copies, waits for them, and re-layouts  4.55 us
    ppermute x1, starting transfers between devices, with_halo(): right = lax.ppermute(x[:, :, :width], 'cells', bwd)  4.12 us
  transfers between devices with their start and end apart: 7, of which 3 were waited for; matrix products, arithmetic and copies ran while one was open for 2% of the time, Pallas kernels for 0%

profile of v2, /device:TPU:2, one launch (start us, length us, event | category | flops | bytes accessed | tf_op | source)
XLA Modules:
  0.0 116.1 jit_solution(5161922514918807260)
XLA Ops:
  0.6 1.4 %fusion.95 = (f32[1,16384]{1,0:T(1,128)S(1)}, f32[1,16384]{1,0:T(1,128)S(1)}, f32[1,16384]{1,0:T(1,128)S(1)}) fusion(f32[3,16384]{1,0:T(4,128)} %param.12), kind=kLoop, calls=%fused_computation.163 | loop fusion | bytes 393216 | tf_op jit(solution)/shard_map/slice | solution.py:36
  2.3 0.6 copy-done.7
  2.9 0.2 fusion.1
  3.1 0.1 fusion.93
  3.4 0.7 copy-done
  4.2 0.1 fusion.94
  4.6 0.7 copy-done.1
  5.4 0.4 multiply_add_fusion.4
  5.8 0.3 multiply_add_fusion.3
  6.1 0.4 convolution_bitcast_fusion
  6.5 0.2 copy.88
  6.7 1.0 copy.89
  7.7 15.6 %all-to-all-start = ((f32[4,128,2,128]{3,2,0,1:T(2,128)}), f32[4,128,2,128]{3,2,0,1:T(2,128)S(1)}, u32[]{:S(2)}, u32[]{:S(2)}) async-start(f32[4,128,2,128]{3,2,0,1:T(2,128)} %copy.89), calls=%async_computation | async-start | bytes 1048576 | tf_op jit(solution)/shard_map/all_to_all | solution.py:234
  23.3 0.1 copy.91
  23.4 0.8 copy-done.3
  24.2 0.1 copy.92
  24.3 0.6 copy-done.6
  25.3 18.1 %all-to-all-done = f32[4,128,2,128]{3,2,0,1:T(2,128)S(1)} async-done(((f32[4,128,2,128]{3,2,0,1:T(2,128)}), f32[4,128,2,128]{3,2,0,1:T(2,128)S(1)}, u32[]{:S(2)}, u32[]{:S(2)}) %all-to-all-start) | async-done | bytes 524320 | tf_op jit(solution)/shard_map/all_to_all | solution.py:234
  43.6 0.1 copy.90
  43.8 1.0 pad_maximum_fusion.refs_1_
  44.7 0.7 slice_convert_fusion
  45.4 13.8 %scatter_traction.1 = f32[192,128]{1,0:T(8,128)} custom-call(s32[256,128]{1,0:T(8,128)} %bitcast.59, f32[6,256,128]{2,1,0:T(8,128)} %pad_maximum_fusion.refs_1_), custom_call_target="tpu_custom_call" | custom-call | tf_op jit(solution)/shard_map/scatter_traction/pallas_call | solution.py:117
  59.3 1.0 copy.93
  60.4 0.2 slice_select_fusion
  60.6 0.2 copy.94
  60.9 3.8 %collective-permute-start.2 = (f32[10,4,4]{1,2,0:T(4,128)S(1)}, f32[10,4,4]{1,2,0:T(4,128)S(1)}, u32[]{:S(2)}, u32[]{:S(2)}) collective-permute-start(f32[10,4,4]{1,2,0:T(4,128)S(1)} %get-tuple-element.32), channel_id=1, source_target_pairs={{0,255},{1,254},{2,1},{3,0},{4,3},{5,2},{6,5},{7,4},{8,7},{9,6},{1... | collective-permute-start | bytes 1928 | tf_op jit(solution)/shard_map/ppermute | solution.py:185
  64.9 4.1 %collective-permute-start.4 = (f32[10,64,4]{1,2,0:T(4,128)S(1)}, f32[10,64,4]{1,2,0:T(4,128)S(1)}, u32[]{:S(2)}, u32[]{:S(2)}) collective-permute-start(f32[10,64,4]{1,2,0:T(4,128)S(1)} %get-tuple-element.30), channel_id=1, source_target_pairs={{2,0},{4,2},{6,4},{8,6},{10,8},{12,10},{14,12},{16,14},{18,16},{20... | collective-permute-start | bytes 30728 | tf_op jit(solution)/shard_map/ppermute | solution.py:178
  69.0 0.1 copy.95
  69.1 0.1 copy.96
  69.4 0.3 copy.97
  69.7 0.3 copy.98
  70.0 0.7 collective-permute-done.3
  70.7 0.5 pad_maximum_fusion.1
  71.3 0.2 multiply_add_fusion.2
  71.6 0.1 broadcast_multiply_fusion.6
  71.7 0.2 multiply_add_fusion.1
  71.9 0.1 broadcast_multiply_fusion.5
  72.1 0.2 multiply_add_fusion
  72.3 0.1 broadcast_multiply_fusion.4
  72.4 0.2 fusion.46
  72.7 0.1 fusion.74
  72.8 0.7 pad_maximum_fusion.3.refs_1_
  73.6 11.3 %gather_field.1 = f32[256,128]{1,0:T(8,128)} custom-call(s32[256,128]{1,0:T(8,128)} %bitcast.60, bf16[128,192]{1,0:T(8,128)(2,1)} %pad_maximum_fusion.3.refs_1_), custom_call_target="tpu_custom_call" | custom-call | tf_op jit(solution)/shard_map/gather_field/pallas_call | solution.py:161
  84.9 18.3 %all-to-all-start.1 = ((f32[128,2,128]{2,1,0:T(2,128)}), f32[128,2,128]{2,1,0:T(2,128)S(1)}, u32[]{:S(2)}, u32[]{:S(2)}) async-start(f32[128,2,128]{2,1,0:T(2,128)} %bitcast.69), calls=%async_computation.1 | async-start | bytes 262144 | tf_op jit(solution)/shard_map/all_to_all | solution.py:266
  103.2 0.1 slice.228
  103.3 0.8 copy.99
  104.1 10.9 %all-to-all-done.1 = f32[128,2,128]{2,1,0:T(2,128)S(1)} async-done(((f32[128,2,128]{2,1,0:T(2,128)}), f32[128,2,128]{2,1,0:T(2,128)S(1)}, u32[]{:S(2)}, u32[]{:S(2)}) %all-to-all-start.1) | async-done | bytes 131104 | tf_op jit(solution)/shard_map/all_to_all | solution.py:266
  115.0 1.1 fusion
  (43 shorter events, 1.8 us)
Async XLA Ops:
  2.0 1.1 copy-start.4
  2.2 0.7 copy-start.7
  3.1 1.2 %copy-start.5 = (f32[3,16384]{1,0:T(4,128)S(1)}, f32[3,16384]{1,0:T(4,128)}, u32[]{:S(2)}) copy-start(f32[3,16384]{1,0:T(4,128)} %param.14) | copy-start | bytes 589828
  3.3 0.8 copy-start
  4.5 0.8 copy-start.1
  7.7 15.6 %copy-start.2 = (f32[3,64,128]{2,1,0:T(8,128)S(1)}, f32[3,64,128]{2,1,0:T(8,128)}, u32[]{:S(2)}) copy-start(f32[3,64,128]{2,1,0:T(8,128)} %param.15) | copy-start | bytes 294916
  7.7 35.7 %all-to-all-start = ((f32[4,128,2,128]{3,2,0,1:T(2,128)}), f32[4,128,2,128]{3,2,0,1:T(2,128)S(1)}, u32[]{:S(2)}, u32[]{:S(2)}) async-start(f32[4,128,2,128]{3,2,0,1:T(2,128)} %copy.89), calls=%async_computation | async-start | bytes 1048576 | tf_op jit(solution)/shard_map/all_to_all | solution.py:234
  23.3 0.9 copy-start.3
  24.2 0.8 copy-start.6
  60.8 8.1 %collective-permute-start = (f32[10,4,4]{1,2,0:T(4,128)S(1)}, f32[10,4,4]{1,2,0:T(4,128)S(1)}, u32[]{:S(2)}, u32[]{:S(2)}) collective-permute-start(f32[10,4,4]{1,2,0:T(4,128)S(1)} %get-tuple-element.31), channel_id=1, source_target_pairs={{0,3},{1,2},{2,5},{3,4},{4,7},{5,6},{6,9},{7,8},{8,11},{9,10},{10,... | collective-permute-start | bytes 1928 | tf_op jit(solution)/shard_map/ppermute | solution.py:184
  60.9 8.2 %collective-permute-start.2 = (f32[10,4,4]{1,2,0:T(4,128)S(1)}, f32[10,4,4]{1,2,0:T(4,128)S(1)}, u32[]{:S(2)}, u32[]{:S(2)}) collective-permute-start(f32[10,4,4]{1,2,0:T(4,128)S(1)} %get-tuple-element.32), channel_id=1, source_target_pairs={{0,255},{1,254},{2,1},{3,0},{4,3},{5,2},{6,5},{7,4},{8,7},{9,6},{1... | collective-permute-start | bytes 1928 | tf_op jit(solution)/shard_map/ppermute | solution.py:185
  64.7 4.5 %collective-permute-start.1 = (f32[10,4,128]{2,1,0:T(4,128)S(1)}, f32[10,4,128]{2,1,0:T(4,128)S(1)}, u32[]{:S(2)}, u32[]{:S(2)}) collective-permute-start(f32[10,4,128]{2,1,0:T(4,128)S(1)} %copy.94), channel_id=1, source_target_pairs={{0,1},{1,0},{2,3},{3,2},{4,5},{5,4},{6,7},{7,6},{8,9},{9,8},{10,11... | collective-permute-start | bytes 61448 | tf_op jit(solution)/shard_map/ppermute | solution.py:181
  64.8 6.0 %collective-permute-start.3 = (f32[10,64,4]{1,2,0:T(4,128)S(1)}, f32[10,64,4]{1,2,0:T(4,128)S(1)}, u32[]{:S(2)}, u32[]{:S(2)}) collective-permute-start(f32[10,64,4]{1,2,0:T(4,128)S(1)} %get-tuple-element.29), channel_id=1, source_target_pairs={{0,2},{2,4},{4,6},{6,8},{8,10},{10,12},{12,14},{14,16},{16,18},{18... | collective-permute-start | bytes 30728 | tf_op jit(solution)/shard_map/ppermute | solution.py:177
  64.9 5.9 %collective-permute-start.4 = (f32[10,64,4]{1,2,0:T(4,128)S(1)}, f32[10,64,4]{1,2,0:T(4,128)S(1)}, u32[]{:S(2)}, u32[]{:S(2)}) collective-permute-start(f32[10,64,4]{1,2,0:T(4,128)S(1)} %get-tuple-element.30), channel_id=1, source_target_pairs={{2,0},{4,2},{6,4},{8,6},{10,8},{12,10},{14,12},{16,14},{18,16},{20... | collective-permute-start | bytes 30728 | tf_op jit(solution)/shard_map/ppermute | solution.py:178
  84.9 30.1 %all-to-all-start.1 = ((f32[128,2,128]{2,1,0:T(2,128)}), f32[128,2,128]{2,1,0:T(2,128)S(1)}, u32[]{:S(2)}, u32[]{:S(2)}) async-start(f32[128,2,128]{2,1,0:T(2,128)} %bitcast.69), calls=%async_computation.1 | async-start | bytes 262144 | tf_op jit(solution)/shard_map/all_to_all | solution.py:266

commit v3 on v2

--- a/solution.py
+++ b/solution.py
@@ -71,7 +71,7 @@
     return rows, cols
 
 
-def _scatter_kernel(ids_ref, push_ref, out_ref, *, patch_rows, shift):
+def _scatter_kernel(count_ref, ids_ref, push_ref, out_ref, *, patch_rows, shift):
     n_rows, lanes = ids_ref.shape
     patch_cols = 1 << shift
     comps = push_ref.shape[0] // 2
@@ -105,10 +105,10 @@
         out_ref[...] += total
         return carry
 
-    lax.fori_loop(0, n_rows // 8, step, 0)
-
-
-def scatter_traction(ids, push, patch_rows, patch_cols):
+    lax.fori_loop(0, count_ref[0] // 8, step, 0)
+
+
+def scatter_traction(count, ids, push, patch_rows, patch_cols):
     shift = patch_cols.bit_length() - 1
     comps = push.shape[0]
     hi = to_bf16_grid(push)
@@ -117,19 +117,21 @@
     out = pl.pallas_call(
         kernel,
         out_shape=jax.ShapeDtypeStruct((comps * patch_rows, patch_cols), F32),
-        in_specs=[pl.BlockSpec(memory_space=pltpu.VMEM)] * 2,
+        in_specs=[pl.BlockSpec(memory_space=pltpu.SMEM)]
+        + [pl.BlockSpec(memory_space=pltpu.VMEM)] * 2,
         out_specs=pl.BlockSpec(memory_space=pltpu.VMEM),
         name="scatter_traction",
-    )(ids, parts)
+    )(count, ids, parts)
     return out.reshape(comps, patch_rows, patch_cols)
 
 
-def _gather_kernel(ids_ref, wt_ref, out_ref, *, patch_rows, shift):
+def _gather_kernel(count_ref, ids_ref, wt_ref, out_ref, *, patch_rows, shift):
     n_rows, lanes = ids_ref.shape
     patch_cols = 1 << shift
     parts = wt_ref.shape[1] // patch_rows
     row_iota = lax.broadcasted_iota(jnp.int32, (patch_rows, lanes), 0)
     col_iota = lax.broadcasted_iota(jnp.int32, (patch_cols, lanes), 0)
+    out_ref[...] = jnp.zeros_like(out_ref)
 
     def step(i, carry):
         base = pl.multiple_of(i * 8, 8)
@@ -146,10 +148,10 @@
         out_ref[pl.ds(base, 8), :] = jnp.concatenate(outs, axis=0)
         return carry
 
-    lax.fori_loop(0, n_rows // 8, step, 0)
-
-
-def gather_field(ids, field):
+    lax.fori_loop(0, count_ref[0] // 8, step, 0)
+
+
+def gather_field(count, ids, field):
     patch_rows, patch_cols = field.shape
     shift = patch_cols.bit_length() - 1
     hi = to_bf16_grid(field)
@@ -161,10 +163,11 @@
     return pl.pallas_call(
         kernel,
         out_shape=jax.ShapeDtypeStruct(ids.shape, F32),
-        in_specs=[pl.BlockSpec(memory_space=pltpu.VMEM)] * 2,
+        in_specs=[pl.BlockSpec(memory_space=pltpu.SMEM)]
+        + [pl.BlockSpec(memory_space=pltpu.VMEM)] * 2,
         out_specs=pl.BlockSpec(memory_space=pltpu.VMEM),
         name="gather_field",
-    )(ids, wt)
+    )(count, ids, wt)
 
 
 def with_halo(x, width):
@@ -227,20 +230,28 @@
     tile_ids = jnp.arange(blocks, dtype=jnp.int32)
     before = (tile_ids[None, :] < tile_ids[:, None]).astype(jnp.float32)
     earlier = jnp.dot(before, member, precision=HIGHEST)
-    slot = block_owner * capacity + jnp.sum(earlier * member, axis=1).astype(jnp.int32)
+    slot = jnp.sum(earlier * member, axis=1).astype(jnp.int32) * owners + block_owner
     placing = (slot[None, :] == jnp.arange(slots, dtype=jnp.int32)[:, None]).astype(jnp.float32)
+    sentinel = patch_rows * patch_cols
     payload = jnp.concatenate([push, elements.astype(jnp.float32)[None]], axis=0)
     send = jnp.einsum("sb,cbl->csl", placing, payload, precision=HIGHEST)
+    filled = jnp.sum(placing, axis=1) > 0.5
+    send = jnp.concatenate(
+        [send[:3], jnp.where(filled[:, None], send[3], float(sentinel))[None]], axis=0
+    )
     recv = lax.all_to_all(
-        send.reshape(4, owners, capacity, tile_len),
+        send.reshape(4, capacity, owners, tile_len),
         "cells",
-        split_axis=1,
-        concat_axis=1,
+        split_axis=2,
+        concat_axis=2,
         tiled=True,
     ).reshape(4, slots, tile_len)
     ids_in = recv[3].astype(jnp.int32)
-
-    traction = scatter_traction(ids_in, recv[:3], patch_rows, patch_cols)
+    round_used = jnp.any(ids_in.reshape(capacity, owners * tile_len) < sentinel, axis=1)
+    rounds = jnp.max(jnp.where(round_used, jnp.arange(1, capacity + 1, dtype=jnp.int32), 0))
+    count = (rounds * owners).reshape(1)
+
+    traction = scatter_traction(count, ids_in, recv[:3], patch_rows, patch_cols)
     state = jnp.concatenate([wall_disp, wall_vel, wall_stiff[None], traction], axis=0)
     state_ext = with_halo(state, width)
     d_ext, v_ext, stiff_ext = state_ext[:3], state_ext[3:6], state_ext[6]
@@ -262,12 +273,12 @@
     own_cos = ext_cos[width : width + patch_cols]
     own_sin = ext_sin[width : width + patch_cols]
     radial_field = wall_next[0] * own_cos + wall_next[1] * own_sin
-    landed_out = gather_field(ids_in, radial_field)
+    landed_out = gather_field(count, ids_in, radial_field)
     landed_back = lax.all_to_all(
-        landed_out.reshape(owners, capacity, tile_len),
+        landed_out.reshape(capacity, owners, tile_len),
         "cells",
-        split_axis=0,
-        concat_axis=0,
+        split_axis=1,
+        concat_axis=1,
         tiled=True,
     ).reshape(slots, tile_len)
     landed = jnp.einsum("sb,sl->bl", placing, landed_back, precision=HIGHEST)

time: 117 us -> 109 us (0.932)
  Pallas kernels: 25.2 us -> 14.3 us
  other arithmetic: 5.64 us -> 7.53 us
    pallas_call x1, Pallas kernels: 13.8 us -> 7.86 us  [scatter_traction(): pl.pallas_call(kernel, out_shape=jax.ShapeDtypeStruct((comps * patch_rows...]
    pallas_call x1, Pallas kernels: 11.3 us -> 6.44 us  [gather_field(): pl.pallas_call(kernel, out_shape=jax.ShapeDtypeStruct(ids.shape, F32), in...]
where the time goes in v3:
time: 109 us
  starting transfers between devices  41.8 us (38%)
  waiting for transfers between devices  29.8 us (27%)
  Pallas kernels  14.3 us (13%)
  local copies, waits for them, and re-layouts  11.9 us (11%)
  other arithmetic  7.53 us (7%)
  between operations  1.75 us (2%)
  matrix products  1.68 us (2%)
    all_to_all x1, waiting for transfers between devices, on_device(): lax.all_to_all(send.reshape(4, capacity, owners, tile_len), 'cells', spli...  18.1 us
    all_to_all x1, starting transfers between devices, on_device(): lax.all_to_all(landed_out.reshape(capacity, owners, tile_len), 'cells', s...  18.1 us
    all_to_all x1, starting transfers between devices, on_device(): lax.all_to_all(send.reshape(4, capacity, owners, tile_len), 'cells', spli...  15.6 us
    all_to_all x1, waiting for transfers between devices, on_device(): lax.all_to_all(landed_out.reshape(capacity, owners, tile_len), 'cells', s...  10.9 us
    pallas_call x1, Pallas kernels, scatter_traction(): pl.pallas_call(kernel, out_shape=jax.ShapeDtypeStruct((comps * patch_rows...  7.86 us
    pallas_call x1, Pallas kernels, gather_field(): pl.pallas_call(kernel, out_shape=jax.ShapeDtypeStruct(ids.shape, F32), in...  6.44 us
    unnamed x20, local copies, waits for them, and re-layouts  4.55 us
    ppermute x1, starting transfers between devices, with_halo(): right = lax.ppermute(x[:, :, :width], 'cells', bwd)  4.12 us
  transfers between devices with their start and end apart: 7, of which 3 were waited for; matrix products, arithmetic and copies ran while one was open for 2% of the time, Pallas kernels for 0%

profile of v3, /device:TPU:2, one launch (start us, length us, event | category | flops | bytes accessed | tf_op | source)
XLA Modules:
  0.0 108.8 jit_solution(183108759699052202)
XLA Ops:
  0.6 1.4 %fusion.94 = (f32[1,16384]{1,0:T(1,128)S(1)}, f32[1,16384]{1,0:T(1,128)S(1)}, f32[1,16384]{1,0:T(1,128)S(1)}) fusion(f32[3,16384]{1,0:T(4,128)} %param.12), kind=kLoop, calls=%fused_computation.169 | loop fusion | bytes 393216 | tf_op jit(solution)/shard_map/slice | solution.py:36
  2.3 0.6 copy-done.7
  2.9 0.2 fusion.1
  3.4 0.7 copy-done
  4.6 0.7 copy-done.1
  5.4 0.4 multiply_add_fusion.4
  5.8 0.3 multiply_add_fusion.3
  6.1 0.1 convert_reduce_fusion
  6.3 0.4 convolution_bitcast_fusion
  6.8 0.1 copy.129
  6.9 0.2 concatenate.31
  7.1 0.3 copy.128
  7.4 1.0 pad_maximum_fusion.3
  8.5 15.6 %all-to-all-start = ((f32[4,2,128,128]{3,1,0,2:T(2,128)}), f32[4,2,128,128]{3,1,0,2:T(2,128)S(1)}, u32[]{:S(2)}, u32[]{:S(2)}) async-start(f32[4,2,128,128]{3,1,0,2:T(2,128)} %pad_maximum_fusion.3), calls=%async_computation | async-start | bytes 1048576 | tf_op jit(solution)/shard_map/all_to_all | solution.py:242
  24.0 0.1 copy.132
  24.2 0.8 copy-done.3
  24.9 0.1 copy.133
  25.1 0.6 copy-done.6
  26.1 18.1 %all-to-all-done = f32[4,2,128,128]{3,1,0,2:T(2,128)S(1)} async-done(((f32[4,2,128,128]{3,1,0,2:T(2,128)}), f32[4,2,128,128]{3,1,0,2:T(2,128)S(1)}, u32[]{:S(2)}, u32[]{:S(2)}) %all-to-all-start) | async-done | bytes 524320 | tf_op jit(solution)/shard_map/all_to_all | solution.py:242
  44.2 0.7 copy_convert_fusion
  44.9 0.1 compare_reduce_fusion
  45.2 0.6 select_reduce_fusion
  46.5 0.9 pad_maximum_fusion.refs_2_
  47.5 7.9 %scatter_traction.1 = f32[192,128]{1,0:T(8,128)} custom-call(s32[1]{0:T(128)} %bitcast.12.refs_0_, s32[256,128]{1,0:T(8,128)} %bitcast.65, f32[6,256,128]{2,1,0:T(8,128)} %pad_maximum_fusion.refs_2_), custom_call_target="tpu_custom_call" | custom-call | tf_op jit(solution)/shard_map/scatter_traction/pallas_call | solution.py:117
  55.3 1.0 copy.134
  56.4 0.2 slice_select_fusion
  56.7 0.2 copy.135
  56.9 3.8 %collective-permute-start.2 = (f32[10,4,4]{1,2,0:T(4,128)S(1)}, f32[10,4,4]{1,2,0:T(4,128)S(1)}, u32[]{:S(2)}, u32[]{:S(2)}) collective-permute-start(f32[10,4,4]{1,2,0:T(4,128)S(1)} %get-tuple-element.34), channel_id=1, source_target_pairs={{0,255},{1,254},{2,1},{3,0},{4,3},{5,2},{6,5},{7,4},{8,7},{9,6},{1... | collective-permute-start | bytes 1928 | tf_op jit(solution)/shard_map/ppermute | solution.py:188
  60.9 4.1 %collective-permute-start.4 = (f32[10,64,4]{1,2,0:T(4,128)S(1)}, f32[10,64,4]{1,2,0:T(4,128)S(1)}, u32[]{:S(2)}, u32[]{:S(2)}) collective-permute-start(f32[10,64,4]{1,2,0:T(4,128)S(1)} %get-tuple-element.32), channel_id=1, source_target_pairs={{2,0},{4,2},{6,4},{8,6},{10,8},{12,10},{14,12},{16,14},{18,16},{20... | collective-permute-start | bytes 30728 | tf_op jit(solution)/shard_map/ppermute | solution.py:181
  65.0 0.1 copy.136
  65.2 0.1 copy.137
  65.4 0.3 copy.138
  65.7 0.3 copy.139
  66.0 0.7 collective-permute-done.3
  66.8 0.5 pad_maximum_fusion.1
  67.4 0.2 multiply_add_fusion.2
  67.7 0.2 multiply_add_fusion.1
  68.1 0.2 multiply_add_fusion
  68.5 0.2 fusion.46
  68.7 0.1 fusion.74
  68.9 0.7 pad_maximum_fusion.4.refs_2_
  69.6 6.4 %gather_field.1 = f32[256,128]{1,0:T(8,128)} custom-call(s32[1]{0:T(128)} %bitcast.12.refs_0_, s32[256,128]{1,0:T(8,128)} %bitcast.66, bf16[128,192]{1,0:T(8,128)(2,1)} %pad_maximum_fusion.4.refs_2_), custom_call_target="tpu_custom_call" | custom-call | tf_op jit(solution)/shard_map/gather_field/pallas_call | solution.py:163
  76.0 1.7 %copy.140 = f32[2,128,128]{2,0,1:T(2,128)} copy(f32[2,128,128]{2,1,0:T(8,128)} %bitcast.75) | data formatting | bytes 262144 | tf_op jit(solution)/shard_map/reshape | solution.py:278
  77.7 18.1 %all-to-all-start.1 = ((f32[2,128,128]{2,0,1:T(2,128)}), f32[2,128,128]{2,0,1:T(2,128)S(1)}, u32[]{:S(2)}, u32[]{:S(2)}) async-start(f32[2,128,128]{2,0,1:T(2,128)} %copy.140), calls=%async_computation.1 | async-start | bytes 262144 | tf_op jit(solution)/shard_map/all_to_all | solution.py:277
  95.8 0.1 slice.238
  95.9 0.8 copy.142
  96.7 10.9 %all-to-all-done.1 = f32[2,128,128]{2,0,1:T(2,128)S(1)} async-done(((f32[2,128,128]{2,0,1:T(2,128)}), f32[2,128,128]{2,0,1:T(2,128)S(1)}, u32[]{:S(2)}, u32[]{:S(2)}) %all-to-all-start.1) | async-done | bytes 131104 | tf_op jit(solution)/shard_map/all_to_all | solution.py:277
  107.6 1.1 %fusion = f32[16384]{0:T(1024)} fusion(f32[256,128]{1,0:T(8,128)S(1)} %bitcast.74, f32[16384]{0:T(1024)S(1)} %copy-done.1, f32[128,128]{1,0:T(8,128)S(1)} %bitcast.73, f32[128,128]{1,0:T(8,128)S(1)} %bitcast.71, s32[128]{0:T(128)S(1)} %get-tuple-element.50, s32[16384]{0:T(1024)S(1)} %copy-done, s32[128]{0:T(128)S(1)} %get-tuple-element.51), kind=kOutput, calls=%fused_computation.3 | convolution fusion | flops 50692096 | bytes 459776 | tf_op jit(solution)/shard_map/sb,sl->bl/dot_general | solution.py:284
  (55 shorter events, 2.5 us)
Async XLA Ops:
  2.0 1.1 copy-start.4
  2.2 0.7 copy-start.7
  3.1 1.2 %copy-start.5 = (f32[3,16384]{1,0:T(4,128)S(1)}, f32[3,16384]{1,0:T(4,128)}, u32[]{:S(2)}) copy-start(f32[3,16384]{1,0:T(4,128)} %param.14) | copy-start | bytes 589828
  3.3 0.8 copy-start
  4.5 0.8 copy-start.1
  8.4 15.6 %copy-start.2 = (f32[3,64,128]{2,1,0:T(8,128)S(1)}, f32[3,64,128]{2,1,0:T(8,128)}, u32[]{:S(2)}) copy-start(f32[3,64,128]{2,1,0:T(8,128)} %param.15) | copy-start | bytes 294916
  8.5 35.7 %all-to-all-start = ((f32[4,2,128,128]{3,1,0,2:T(2,128)}), f32[4,2,128,128]{3,1,0,2:T(2,128)S(1)}, u32[]{:S(2)}, u32[]{:S(2)}) async-start(f32[4,2,128,128]{3,1,0,2:T(2,128)} %pad_maximum_fusion.3), calls=%async_computation | async-start | bytes 1048576 | tf_op jit(solution)/shard_map/all_to_all | solution.py:242
  24.0 0.9 copy-start.3
  24.9 0.8 copy-start.6
  56.9 8.1 %collective-permute-start = (f32[10,4,4]{1,2,0:T(4,128)S(1)}, f32[10,4,4]{1,2,0:T(4,128)S(1)}, u32[]{:S(2)}, u32[]{:S(2)}) collective-permute-start(f32[10,4,4]{1,2,0:T(4,128)S(1)} %get-tuple-element.33), channel_id=1, source_target_pairs={{0,3},{1,2},{2,5},{3,4},{4,7},{5,6},{6,9},{7,8},{8,11},{9,10},{10,... | collective-permute-start | bytes 1928 | tf_op jit(solution)/shard_map/ppermute | solution.py:187
  56.9 8.2 %collective-permute-start.2 = (f32[10,4,4]{1,2,0:T(4,128)S(1)}, f32[10,4,4]{1,2,0:T(4,128)S(1)}, u32[]{:S(2)}, u32[]{:S(2)}) collective-permute-start(f32[10,4,4]{1,2,0:T(4,128)S(1)} %get-tuple-element.34), channel_id=1, source_target_pairs={{0,255},{1,254},{2,1},{3,0},{4,3},{5,2},{6,5},{7,4},{8,7},{9,6},{1... | collective-permute-start | bytes 1928 | tf_op jit(solution)/shard_map/ppermute | solution.py:188
  60.8 4.5 %collective-permute-start.1 = (f32[10,4,128]{2,1,0:T(4,128)S(1)}, f32[10,4,128]{2,1,0:T(4,128)S(1)}, u32[]{:S(2)}, u32[]{:S(2)}) collective-permute-start(f32[10,4,128]{2,1,0:T(4,128)S(1)} %copy.135), channel_id=1, source_target_pairs={{0,1},{1,0},{2,3},{3,2},{4,5},{5,4},{6,7},{7,6},{8,9},{9,8},{10,11... | collective-permute-start | bytes 61448 | tf_op jit(solution)/shard_map/ppermute | solution.py:184
  60.8 6.0 %collective-permute-start.3 = (f32[10,64,4]{1,2,0:T(4,128)S(1)}, f32[10,64,4]{1,2,0:T(4,128)S(1)}, u32[]{:S(2)}, u32[]{:S(2)}) collective-permute-start(f32[10,64,4]{1,2,0:T(4,128)S(1)} %get-tuple-element.31), channel_id=1, source_target_pairs={{0,2},{2,4},{4,6},{6,8},{8,10},{10,12},{12,14},{14,16},{16,18},{18... | collective-permute-start | bytes 30728 | tf_op jit(solution)/shard_map/ppermute | solution.py:180
  60.9 5.9 %collective-permute-start.4 = (f32[10,64,4]{1,2,0:T(4,128)S(1)}, f32[10,64,4]{1,2,0:T(4,128)S(1)}, u32[]{:S(2)}, u32[]{:S(2)}) collective-permute-start(f32[10,64,4]{1,2,0:T(4,128)S(1)} %get-tuple-element.32), channel_id=1, source_target_pairs={{2,0},{4,2},{6,4},{8,6},{10,8},{12,10},{14,12},{16,14},{18,16},{20... | collective-permute-start | bytes 30728 | tf_op jit(solution)/shard_map/ppermute | solution.py:181
  77.7 29.9 %all-to-all-start.1 = ((f32[2,128,128]{2,0,1:T(2,128)}), f32[2,128,128]{2,0,1:T(2,128)S(1)}, u32[]{:S(2)}, u32[]{:S(2)}) async-start(f32[2,128,128]{2,0,1:T(2,128)} %copy.140), calls=%async_computation.1 | async-start | bytes 262144 | tf_op jit(solution)/shard_map/all_to_all | solution.py:277

commit v4 on v3

--- a/solution.py
+++ b/solution.py
@@ -71,18 +71,18 @@
     return rows, cols
 
 
-def _scatter_kernel(count_ref, ids_ref, push_ref, out_ref, *, patch_rows, shift):
-    n_rows, lanes = ids_ref.shape
+def _scatter_kernel(count_ref, recv_ref, out_ref, *, patch_rows, shift):
+    comps = recv_ref.shape[0] - 1
+    lanes = recv_ref.shape[2]
     patch_cols = 1 << shift
-    comps = push_ref.shape[0] // 2
     row_iota = lax.broadcasted_iota(jnp.int32, (patch_rows, lanes), 0)
     col_iota = lax.broadcasted_iota(jnp.int32, (patch_cols, lanes), 0)
     out_ref[...] = jnp.zeros_like(out_ref)
 
     def step(i, carry):
         base = pl.multiple_of(i * 8, 8)
-        ids8 = ids_ref[pl.ds(base, 8), :]
-        push8 = push_ref[:, pl.ds(base, 8), :]
+        blk = recv_ref[:, pl.ds(base, 8), :]
+        ids8 = blk[comps].astype(jnp.int32)
         total = None
         for g in range(8):
             rows, cols = _split_ids(ids8[g : g + 1, :], shift)
@@ -90,8 +90,9 @@
             chot = (col_iota == cols).astype(BF16)
             his, los = [], []
             for c in range(comps):
-                hi = push8[c, g : g + 1, :].astype(BF16)
-                lo = push8[comps + c, g : g + 1, :].astype(BF16)
+                p = blk[c, g : g + 1, :]
+                hi = p.astype(BF16)
+                lo = (p - hi.astype(F32)).astype(BF16)
                 his.append(rhot * hi)
                 los.append(rhot * lo)
             lhs = jnp.concatenate(
@@ -108,25 +109,24 @@
     lax.fori_loop(0, count_ref[0] // 8, step, 0)
 
 
-def scatter_traction(count, ids, push, patch_rows, patch_cols):
+def scatter_traction(count, recv, patch_rows, patch_cols):
     shift = patch_cols.bit_length() - 1
-    comps = push.shape[0]
-    hi = to_bf16_grid(push)
-    parts = jnp.concatenate([hi, push - hi], axis=0)
+    comps = recv.shape[0] - 1
     kernel = lambda *refs: _scatter_kernel(*refs, patch_rows=patch_rows, shift=shift)
     out = pl.pallas_call(
         kernel,
         out_shape=jax.ShapeDtypeStruct((comps * patch_rows, patch_cols), F32),
-        in_specs=[pl.BlockSpec(memory_space=pltpu.SMEM)]
-        + [pl.BlockSpec(memory_space=pltpu.VMEM)] * 2,
+        in_specs=[pl.BlockSpec(memory_space=pltpu.SMEM), pl.BlockSpec(memory_space=pltpu.VMEM)],
         out_specs=pl.BlockSpec(memory_space=pltpu.VMEM),
         name="scatter_traction",
-    )(count, ids, parts)
+    )(count, recv)
     return out.reshape(comps, patch_rows, patch_cols)
 
 
-def _gather_kernel(count_ref, ids_ref, wt_ref, out_ref, *, patch_rows, shift):
-    n_rows, lanes = ids_ref.shape
+def _gather_kernel(count_ref, recv_ref, wt_ref, out_ref, *, patch_rows, shift):
+    owners = out_ref.shape[0]
+    lanes = recv_ref.shape[2]
+    id_row = recv_ref.shape[0] - 1
     patch_cols = 1 << shift
     parts = wt_ref.shape[1] // patch_rows
     row_iota = lax.broadcasted_iota(jnp.int32, (patch_rows, lanes), 0)
@@ -135,7 +135,7 @@
 
     def step(i, carry):
         base = pl.multiple_of(i * 8, 8)
-        ids8 = ids_ref[pl.ds(base, 8), :]
+        ids8 = recv_ref[id_row, pl.ds(base, 8), :].astype(jnp.int32)
         wt = wt_ref[...]
         outs = []
         for g in range(8):
@@ -145,13 +145,15 @@
             picked = jnp.dot(wt, rhs, preferred_element_type=F32)
             sel = jnp.where(col_iota == cols, picked, 0.0)
             outs.append(jnp.sum(sel, axis=0, keepdims=True))
-        out_ref[pl.ds(base, 8), :] = jnp.concatenate(outs, axis=0)
+        rnd = base // owners
+        first = pl.multiple_of(base - rnd * owners, 8)
+        out_ref[pl.ds(first, 8), rnd, :] = jnp.concatenate(outs, axis=0)
         return carry
 
     lax.fori_loop(0, count_ref[0] // 8, step, 0)
 
 
-def gather_field(count, ids, field):
+def gather_field(count, recv, field, owners, capacity):
     patch_rows, patch_cols = field.shape
     shift = patch_cols.bit_length() - 1
     hi = to_bf16_grid(field)
@@ -162,12 +164,12 @@
     kernel = lambda *refs: _gather_kernel(*refs, patch_rows=patch_rows, shift=shift)
     return pl.pallas_call(
         kernel,
-        out_shape=jax.ShapeDtypeStruct(ids.shape, F32),
+        out_shape=jax.ShapeDtypeStruct((owners, capacity, recv.shape[2]), F32),
         in_specs=[pl.BlockSpec(memory_space=pltpu.SMEM)]
         + [pl.BlockSpec(memory_space=pltpu.VMEM)] * 2,
         out_specs=pl.BlockSpec(memory_space=pltpu.VMEM),
         name="gather_field",
-    )(count, ids, wt)
+    )(count, recv, wt)
 
 
 def with_halo(x, width):
@@ -246,12 +248,11 @@
         concat_axis=2,
         tiled=True,
     ).reshape(4, slots, tile_len)
-    ids_in = recv[3].astype(jnp.int32)
-    round_used = jnp.any(ids_in.reshape(capacity, owners * tile_len) < sentinel, axis=1)
+    round_used = jnp.any(recv[3].reshape(capacity, owners * tile_len) < sentinel, axis=1)
     rounds = jnp.max(jnp.where(round_used, jnp.arange(1, capacity + 1, dtype=jnp.int32), 0))
     count = (rounds * owners).reshape(1)
 
-    traction = scatter_traction(count, ids_in, recv[:3], patch_rows, patch_cols)
+    traction = scatter_traction(count, recv, patch_rows, patch_cols)
     state = jnp.concatenate([wall_disp, wall_vel, wall_stiff[None], traction], axis=0)
     state_ext = with_halo(state, width)
     d_ext, v_ext, stiff_ext = state_ext[:3], state_ext[3:6], state_ext[6]
@@ -273,15 +274,13 @@
     own_cos = ext_cos[width : width + patch_cols]
     own_sin = ext_sin[width : width + patch_cols]
     radial_field = wall_next[0] * own_cos + wall_next[1] * own_sin
-    landed_out = gather_field(count, ids_in, radial_field)
+    landed_out = gather_field(count, recv, radial_field, owners, capacity)
     landed_back = lax.all_to_all(
-        landed_out.reshape(capacity, owners, tile_len),
-        "cells",
-        split_axis=1,
-        concat_axis=1,
-        tiled=True,
+        landed_out, "cells", split_axis=0, concat_axis=0, tiled=True
     ).reshape(slots, tile_len)
-    landed = jnp.einsum("sb,sl->bl", placing, landed_back, precision=HIGHEST)
+    back_slot = block_owner * capacity + jnp.sum(earlier * member, axis=1).astype(jnp.int32)
+    taking = (back_slot[None, :] == jnp.arange(slots, dtype=jnp.int32)[:, None]).astype(jnp.float32)
+    landed = jnp.einsum("sb,sl->bl", taking, landed_back, precision=HIGHEST)
     contact_gap = radius_tiles + reach - landed
     return (wall_next, contact_gap.reshape(-1))
 

time: 109 us -> 108 us (level)
  other arithmetic: 7.53 us -> 5.98 us
    reshape x1 -> x0, local copies, waits for them, and re-layouts: 1.66 us -> none  [on_device(): landed_out.reshape(capacity, owners, tile_len)]
where the time goes in v4:
time: 108 us; the launch traced here: 107 us
  starting transfers between devices  41.8 us (39%)
  waiting for transfers between devices  29.8 us (28%)
  Pallas kernels  14.5 us (13%)
  local copies, waits for them, and re-layouts  11.2 us (10%)
  other arithmetic  5.98 us (6%)
  matrix products  2.43 us (2%)
  between operations  1.71 us (2%)
    all_to_all x1, waiting for transfers between devices, on_device(): lax.all_to_all(send.reshape(4, capacity, owners, tile_len), 'cells', spli...  18.1 us
    all_to_all x1, starting transfers between devices, on_device(): lax.all_to_all(landed_out, 'cells', split_axis=0, concat_axis=0, tiled=True)  18.1 us
    all_to_all x1, starting transfers between devices, on_device(): lax.all_to_all(send.reshape(4, capacity, owners, tile_len), 'cells', spli...  15.6 us
    all_to_all x1, waiting for transfers between devices, on_device(): lax.all_to_all(landed_out, 'cells', split_axis=0, concat_axis=0, tiled=True)  10.9 us
    pallas_call x1, Pallas kernels, scatter_traction(): pl.pallas_call(kernel, out_shape=jax.ShapeDtypeStruct((comps * patch_rows...  7.75 us
    pallas_call x1, Pallas kernels, gather_field(): pl.pallas_call(kernel, out_shape=jax.ShapeDtypeStruct((owners, capacity,...  6.73 us
    unnamed x20, local copies, waits for them, and re-layouts  4.63 us
    ppermute x1, starting transfers between devices, with_halo(): right = lax.ppermute(x[:, :, :width], 'cells', bwd)  4.12 us
  transfers between devices with their start and end apart: 7, of which 3 were waited for; matrix products, arithmetic and copies ran while one was open for 2% of the time, Pallas kernels for 0%

profile of v4, /device:TPU:2, one launch (start us, length us, event | category | flops | bytes accessed | tf_op | source)
XLA Modules:
  0.0 107.4 jit_solution(1243467616837950151)
XLA Ops:
  0.6 0.9 fusion.1
  1.6 1.5 %fusion.94 = (f32[1,16384]{1,0:T(1,128)S(1)}, f32[1,16384]{1,0:T(1,128)S(1)}, f32[1,16384]{1,0:T(1,128)S(1)}) fusion(f32[3,16384]{1,0:T(4,128)} %param.12), kind=kLoop, calls=%fused_computation.167 | loop fusion | bytes 393216 | tf_op jit(solution)/shard_map/slice | solution.py:36
  3.4 0.6 copy-done.4
  4.3 0.7 copy-done
  5.5 0.7 copy-done.1
  6.4 0.4 multiply_add_fusion.4
  6.7 0.3 multiply_add_fusion.3
  7.1 0.1 convert_reduce_fusion
  7.2 0.4 convolution_bitcast_fusion
  7.7 0.1 copy.91
  7.9 0.2 concatenate.28
  8.1 0.3 copy.90
  8.3 1.0 pad_maximum_fusion.2
  9.4 15.6 %all-to-all-start = ((f32[4,2,128,128]{3,1,0,2:T(2,128)}), f32[4,2,128,128]{3,1,0,2:T(2,128)S(1)}, u32[]{:S(2)}, u32[]{:S(2)}) async-start(f32[4,2,128,128]{3,1,0,2:T(2,128)} %pad_maximum_fusion.2), calls=%async_computation | async-start | bytes 1048576 | tf_op jit(solution)/shard_map/all_to_all | solution.py:244
  25.0 0.1 copy.93
  25.1 0.8 copy-done.3
  25.9 0.1 copy.94
  26.0 0.6 copy-done.6
  27.0 18.1 %all-to-all-done = f32[4,2,128,128]{3,1,0,2:T(2,128)S(1)} async-done(((f32[4,2,128,128]{3,1,0,2:T(2,128)}), f32[4,2,128,128]{3,1,0,2:T(2,128)S(1)}, u32[]{:S(2)}, u32[]{:S(2)}) %all-to-all-start) | async-done | bytes 524320 | tf_op jit(solution)/shard_map/all_to_all | solution.py:244
  45.1 0.2 compare_reduce_fusion
  45.4 0.6 select_reduce_fusion
  46.7 0.9 copy.92
  47.6 7.8 %scatter_traction.1 = f32[192,128]{1,0:T(8,128)} custom-call(s32[1]{0:T(128)} %bitcast.12.refs_0_, f32[4,256,128]{2,1,0:T(8,128)} %bitcast.59), custom_call_target="tpu_custom_call" | custom-call | tf_op jit(solution)/shard_map/scatter_traction/pallas_call | solution.py:116
  55.3 1.0 copy.95
  56.4 0.2 slice_select_fusion
  56.7 0.2 copy.96
  57.0 3.8 %collective-permute-start.2 = (f32[10,4,4]{1,2,0:T(4,128)S(1)}, f32[10,4,4]{1,2,0:T(4,128)S(1)}, u32[]{:S(2)}, u32[]{:S(2)}) collective-permute-start(f32[10,4,4]{1,2,0:T(4,128)S(1)} %get-tuple-element.32), channel_id=1, source_target_pairs={{0,255},{1,254},{2,1},{3,0},{4,3},{5,2},{6,5},{7,4},{8,7},{9,6},{1... | collective-permute-start | bytes 1928 | tf_op jit(solution)/shard_map/ppermute | solution.py:190
  60.9 4.1 %collective-permute-start.4 = (f32[10,64,4]{1,2,0:T(4,128)S(1)}, f32[10,64,4]{1,2,0:T(4,128)S(1)}, u32[]{:S(2)}, u32[]{:S(2)}) collective-permute-start(f32[10,64,4]{1,2,0:T(4,128)S(1)} %get-tuple-element.30), channel_id=1, source_target_pairs={{2,0},{4,2},{6,4},{8,6},{10,8},{12,10},{14,12},{16,14},{18,16},{20... | collective-permute-start | bytes 30728 | tf_op jit(solution)/shard_map/ppermute | solution.py:183
  65.0 0.1 copy.97
  65.2 0.1 copy.98
  65.4 0.3 copy.100
  65.7 0.3 copy.99
  66.0 0.7 collective-permute-done.3
  66.8 0.5 pad_maximum_fusion
  67.4 0.2 multiply_add_fusion.2
  67.6 0.1 broadcast_multiply_fusion.6
  67.7 0.2 multiply_add_fusion.1
  68.0 0.1 broadcast_multiply_fusion.5
  68.1 0.2 multiply_add_fusion
  68.5 0.2 fusion.46
  68.7 0.1 fusion.74
  68.9 0.7 pad_maximum_fusion.3.refs_2_
  69.6 6.7 %gather_field.1 = f32[128,2,128]{2,1,0:T(2,128)} custom-call(s32[1]{0:T(128)} %bitcast.12.refs_0_, f32[4,256,128]{2,1,0:T(8,128)} %bitcast.60, bf16[128,192]{1,0:T(8,128)(2,1)} %pad_maximum_fusion.3.refs_2_), custom_call_target="tpu_custom_call" | custom-call | tf_op jit(solution)/shard_map/gather_field/pallas_call | solution.py:165
  76.3 18.1 %all-to-all-start.1 = ((f32[128,2,128]{2,1,0:T(2,128)}), f32[128,2,128]{2,1,0:T(2,128)S(1)}, u32[]{:S(2)}, u32[]{:S(2)}) async-start(f32[128,2,128]{2,1,0:T(2,128)} %gather_field.1), calls=%async_computation.1 | async-start | bytes 262144 | tf_op jit(solution)/shard_map/all_to_all | solution.py:278
  94.4 0.1 slice.229
  94.5 0.8 copy.101
  95.3 10.9 %all-to-all-done.1 = f32[128,2,128]{2,1,0:T(2,128)S(1)} async-done(((f32[128,2,128]{2,1,0:T(2,128)}), f32[128,2,128]{2,1,0:T(2,128)S(1)}, u32[]{:S(2)}, u32[]{:S(2)}) %all-to-all-start.1) | async-done | bytes 131104 | tf_op jit(solution)/shard_map/all_to_all | solution.py:278
  106.2 1.1 %fusion = f32[16384]{0:T(1024)} fusion(f32[256,128]{1,0:T(8,128)S(1)} %bitcast.68, f32[16384]{0:T(1024)S(1)} %copy-done.1, s32[128]{0:T(128)S(1)} %get-tuple-element.46, f32[128,128]{1,0:T(8,128)S(1)} %bitcast.67, f32[128,128]{1,0:T(8,128)S(1)} %bitcast.65, s32[16384]{0:T(1024)S(1)} %copy-done, s32[128]{0:T(128)S(1)} %get-tuple-element.48), kind=kOutput, calls=%fused_computation.3 | convolution fusion | flops 50692096 | bytes 459776 | tf_op jit(solution)/shard_map/sb,sl->bl/dot_general | solution.py:283
  (48 shorter events, 2.1 us)
Async XLA Ops:
  0.6 0.9 copy-start.7
  3.1 1.0 copy-start.4
  4.0 1.1 %copy-start.5 = (f32[3,16384]{1,0:T(4,128)S(1)}, f32[3,16384]{1,0:T(4,128)}, u32[]{:S(2)}) copy-start(f32[3,16384]{1,0:T(4,128)} %param.14) | copy-start | bytes 589828
  4.2 0.8 copy-start
  5.4 0.8 copy-start.1
  9.4 15.6 %copy-start.2 = (f32[3,64,128]{2,1,0:T(8,128)S(1)}, f32[3,64,128]{2,1,0:T(8,128)}, u32[]{:S(2)}) copy-start(f32[3,64,128]{2,1,0:T(8,128)} %param.15) | copy-start | bytes 294916
  9.4 35.7 %all-to-all-start = ((f32[4,2,128,128]{3,1,0,2:T(2,128)}), f32[4,2,128,128]{3,1,0,2:T(2,128)S(1)}, u32[]{:S(2)}, u32[]{:S(2)}) async-start(f32[4,2,128,128]{3,1,0,2:T(2,128)} %pad_maximum_fusion.2), calls=%async_computation | async-start | bytes 1048576 | tf_op jit(solution)/shard_map/all_to_all | solution.py:244
  25.0 0.9 copy-start.3
  25.9 0.8 copy-start.6
  56.9 8.1 %collective-permute-start = (f32[10,4,4]{1,2,0:T(4,128)S(1)}, f32[10,4,4]{1,2,0:T(4,128)S(1)}, u32[]{:S(2)}, u32[]{:S(2)}) collective-permute-start(f32[10,4,4]{1,2,0:T(4,128)S(1)} %get-tuple-element.31), channel_id=1, source_target_pairs={{0,3},{1,2},{2,5},{3,4},{4,7},{5,6},{6,9},{7,8},{8,11},{9,10},{10,... | collective-permute-start | bytes 1928 | tf_op jit(solution)/shard_map/ppermute | solution.py:189
  57.0 8.2 %collective-permute-start.2 = (f32[10,4,4]{1,2,0:T(4,128)S(1)}, f32[10,4,4]{1,2,0:T(4,128)S(1)}, u32[]{:S(2)}, u32[]{:S(2)}) collective-permute-start(f32[10,4,4]{1,2,0:T(4,128)S(1)} %get-tuple-element.32), channel_id=1, source_target_pairs={{0,255},{1,254},{2,1},{3,0},{4,3},{5,2},{6,5},{7,4},{8,7},{9,6},{1... | collective-permute-start | bytes 1928 | tf_op jit(solution)/shard_map/ppermute | solution.py:190
  60.8 4.5 %collective-permute-start.1 = (f32[10,4,128]{2,1,0:T(4,128)S(1)}, f32[10,4,128]{2,1,0:T(4,128)S(1)}, u32[]{:S(2)}, u32[]{:S(2)}) collective-permute-start(f32[10,4,128]{2,1,0:T(4,128)S(1)} %copy.96), channel_id=1, source_target_pairs={{0,1},{1,0},{2,3},{3,2},{4,5},{5,4},{6,7},{7,6},{8,9},{9,8},{10,11... | collective-permute-start | bytes 61448 | tf_op jit(solution)/shard_map/ppermute | solution.py:186
  60.8 6.0 %collective-permute-start.3 = (f32[10,64,4]{1,2,0:T(4,128)S(1)}, f32[10,64,4]{1,2,0:T(4,128)S(1)}, u32[]{:S(2)}, u32[]{:S(2)}) collective-permute-start(f32[10,64,4]{1,2,0:T(4,128)S(1)} %get-tuple-element.29), channel_id=1, source_target_pairs={{0,2},{2,4},{4,6},{6,8},{8,10},{10,12},{12,14},{14,16},{16,18},{18... | collective-permute-start | bytes 30728 | tf_op jit(solution)/shard_map/ppermute | solution.py:182
  60.9 5.9 %collective-permute-start.4 = (f32[10,64,4]{1,2,0:T(4,128)S(1)}, f32[10,64,4]{1,2,0:T(4,128)S(1)}, u32[]{:S(2)}, u32[]{:S(2)}) collective-permute-start(f32[10,64,4]{1,2,0:T(4,128)S(1)} %get-tuple-element.30), channel_id=1, source_target_pairs={{2,0},{4,2},{6,4},{8,6},{10,8},{12,10},{14,12},{16,14},{18,16},{20... | collective-permute-start | bytes 30728 | tf_op jit(solution)/shard_map/ppermute | solution.py:183
  76.3 29.9 %all-to-all-start.1 = ((f32[128,2,128]{2,1,0:T(2,128)}), f32[128,2,128]{2,1,0:T(2,128)S(1)}, u32[]{:S(2)}, u32[]{:S(2)}) async-start(f32[128,2,128]{2,1,0:T(2,128)} %gather_field.1), calls=%async_computation.1 | async-start | bytes 262144 | tf_op jit(solution)/shard_map/all_to_all | solution.py:278

commit v5 on v4

--- a/solution.py
+++ b/solution.py
@@ -184,12 +184,11 @@
     facing = jnp.where(slab == 0, x[:, rows - width :, :], x[:, :width, :])
     swap = [(j, m - 1 - j) for j in range(m)]
     across = lax.ppermute(facing, "slab", swap)
-    diag_fwd = [(i * m + j, ((i + 1) % n) * m + (m - 1 - j)) for i in range(n) for j in range(m)]
-    diag_bwd = [(i * m + j, ((i - 1) % n) * m + (m - 1 - j)) for i in range(n) for j in range(m)]
-    corner_left = lax.ppermute(facing[:, :, cols - width :], ("cells", "slab"), diag_fwd)
-    corner_right = lax.ppermute(facing[:, :, :width], ("cells", "slab"), diag_bwd)
+    sides = jnp.concatenate([left, right], axis=2)
+    facing_sides = jnp.where(slab == 0, sides[:, rows - width :, :], sides[:, :width, :])
+    corners = lax.ppermute(facing_sides, "slab", swap)
     band = jnp.concatenate([left, x, right], axis=2)
-    cap = jnp.concatenate([corner_left, across, corner_right], axis=2)
+    cap = jnp.concatenate([corners[:, :, :width], across, corners[:, :, width:]], axis=2)
     zero = jnp.zeros_like(cap)
     top = jnp.where(slab == 0, zero, cap)
     bottom = jnp.where(slab == 0, cap, zero)

time: 108 us -> 104 us (0.963)
  starting transfers between devices: 41.8 us -> 36.5 us
  waiting for transfers between devices: 29.8 us -> 31.1 us
    ppermute x2 -> x1, starting transfers between devices: 3.9 us -> 0.09 us  [with_halo(): corners = lax.ppermute(facing_sides, 'slab', swap)]
    all_to_all x1, starting transfers between devices: 18.1 us -> 16.2 us  [on_device(): lax.all_to_all(landed_out, 'cells', split_axis=0, concat_axis=0, tiled=True)]
  transfers between devices with their start and end apart: 7 -> 6, of which waited for: 3 -> 4; matrix products, arithmetic and copies ran while one was open for 2% -> 2% of each run, Pallas kernels for 0% -> 0%
where the time goes in v5:
time: 104 us
  starting transfers between devices  36.5 us (35%)
  waiting for transfers between devices  31.1 us (30%)
  Pallas kernels  14.5 us (14%)
  local copies, waits for them, and re-layouts  11.7 us (11%)
  other arithmetic  5.86 us (6%)
  matrix products  2.43 us (2%)
  between operations  1.71 us (2%)
    all_to_all x1, waiting for transfers between devices, on_device(): lax.all_to_all(send.reshape(4, capacity, owners, tile_len), 'cells', spli...  18.1 us
    all_to_all x1, starting transfers between devices, on_device(): lax.all_to_all(landed_out, 'cells', split_axis=0, concat_axis=0, tiled=True)  16.2 us
    all_to_all x1, starting transfers between devices, on_device(): lax.all_to_all(send.reshape(4, capacity, owners, tile_len), 'cells', spli...  15.6 us
    all_to_all x1, waiting for transfers between devices, on_device(): lax.all_to_all(landed_out, 'cells', split_axis=0, concat_axis=0, tiled=True)  11.3 us
    pallas_call x1, Pallas kernels, scatter_traction(): pl.pallas_call(kernel, out_shape=jax.ShapeDtypeStruct((comps * patch_rows...  7.75 us
    pallas_call x1, Pallas kernels, gather_field(): pl.pallas_call(kernel, out_shape=jax.ShapeDtypeStruct((owners, capacity,...  6.73 us
    unnamed x20, local copies, waits for them, and re-layouts  4.63 us
    ppermute x1, starting transfers between devices, with_halo(): right = lax.ppermute(x[:, :, :width], 'cells', bwd)  3.71 us
  transfers between devices with their start and end apart: 6, of which 4 were waited for; matrix products, arithmetic and copies ran while one was open for 2% of the time, Pallas kernels for 0%

profile of v5, /device:TPU:2, one launch (start us, length us, event | category | flops | bytes accessed | tf_op | source)
XLA Modules:
  0.0 103.8 jit_solution(17920571503092993027)
XLA Ops:
  0.6 0.9 fusion.1
  1.6 1.5 %fusion.95 = (f32[1,16384]{1,0:T(1,128)S(1)}, f32[1,16384]{1,0:T(1,128)S(1)}, f32[1,16384]{1,0:T(1,128)S(1)}) fusion(f32[3,16384]{1,0:T(4,128)} %param.12), kind=kLoop, calls=%fused_computation.169 | loop fusion | bytes 393216 | tf_op jit(solution)/shard_map/slice | solution.py:36
  3.4 0.6 copy-done.4
  4.3 0.7 copy-done
  5.5 0.7 copy-done.1
  6.4 0.4 multiply_add_fusion.4
  6.7 0.3 multiply_add_fusion.3
  7.1 0.1 convert_reduce_fusion
  7.2 0.4 convolution_bitcast_fusion
  7.7 0.1 copy.93
  7.9 0.2 concatenate.31
  8.1 0.3 copy.92
  8.3 1.0 %pad_maximum_fusion.2 = f32[4,2,128,128]{3,1,0,2:T(2,128)} fusion(f32[1,2,128,128]{3,1,0,2:T(2,128)S(1)} %copy.93, f32[3,2,128,128]{3,1,0,2:T(2,128)S(1)} %copy.92), kind=kLoop, calls=%fused_computation.7 | loop fusion | flops 131072 | bytes 1048576 | tf_op jit(solution)/shard_map/concatenate | solution.py:240
  9.4 15.6 %all-to-all-start = ((f32[4,2,128,128]{3,1,0,2:T(2,128)}), f32[4,2,128,128]{3,1,0,2:T(2,128)S(1)}, u32[]{:S(2)}, u32[]{:S(2)}) async-start(f32[4,2,128,128]{3,1,0,2:T(2,128)} %pad_maximum_fusion.2), calls=%async_computation | async-start | bytes 1048576 | tf_op jit(solution)/shard_map/all_to_all | solution.py:243
  25.0 0.1 copy.95
  25.1 0.8 copy-done.3
  25.9 0.1 copy.96
  26.0 0.6 copy-done.6
  27.0 18.1 %all-to-all-done = f32[4,2,128,128]{3,1,0,2:T(2,128)S(1)} async-done(((f32[4,2,128,128]{3,1,0,2:T(2,128)}), f32[4,2,128,128]{3,1,0,2:T(2,128)S(1)}, u32[]{:S(2)}, u32[]{:S(2)}) %all-to-all-start) | async-done | bytes 524320 | tf_op jit(solution)/shard_map/all_to_all | solution.py:243
  45.1 0.2 compare_reduce_fusion
  45.4 0.6 select_reduce_fusion
  46.7 0.9 copy.94
  47.6 7.8 %scatter_traction.1 = f32[192,128]{1,0:T(8,128)} custom-call(s32[1]{0:T(128)} %bitcast.12.refs_0_, f32[4,256,128]{2,1,0:T(8,128)} %bitcast.62), custom_call_target="tpu_custom_call" | custom-call | tf_op jit(solution)/shard_map/scatter_traction/pallas_call | solution.py:116
  55.3 1.0 copy.97
  56.4 0.5 collective-permute-start
  56.9 3.7 %collective-permute-start.1 = (f32[10,64,4]{1,2,0:T(4,128)S(1)}, f32[10,64,4]{1,2,0:T(4,128)S(1)}, u32[]{:S(2)}, u32[]{:S(2)}) collective-permute-start(f32[10,64,4]{1,2,0:T(4,128)S(1)} %get-tuple-element.32), channel_id=1, source_target_pairs={{2,0},{4,2},{6,4},{8,6},{10,8},{12,10},{14,12},{16,14},{18,16},{20... | collective-permute-start | bytes 30728 | tf_op jit(solution)/shard_map/ppermute | solution.py:183
  60.6 0.2 fusion.92
  60.9 0.2 copy.98
  61.1 0.2 copy.99
  61.4 1.0 %collective-permute-done = f32[10,64,4]{1,2,0:T(4,128)S(1)} collective-permute-done((f32[10,64,4]{1,2,0:T(4,128)S(1)}, f32[10,64,4]{1,2,0:T(4,128)S(1)}, u32[]{:S(2)}, u32[]{:S(2)}) %collective-permute-start) | collective-permute-done | bytes 10272 | tf_op jit(solution)/shard_map/ppermute | solution.py:182
  62.6 0.5 collective-permute-start.3
  63.1 0.7 collective-permute-done.2
  63.8 0.1 copy.100
  64.0 0.1 copy.101
  64.2 0.3 copy.102
  64.5 0.3 copy.103
  64.8 0.5 pad_maximum_fusion
  65.4 0.2 multiply_add_fusion.2
  65.8 0.2 multiply_add_fusion.1
  66.1 0.2 multiply_add_fusion
  66.5 0.2 fusion.46
  66.8 0.1 fusion.75
  66.9 0.7 pad_maximum_fusion.3.refs_2_
  67.7 6.7 %gather_field.1 = f32[128,2,128]{2,1,0:T(2,128)} custom-call(s32[1]{0:T(128)} %bitcast.12.refs_0_, f32[4,256,128]{2,1,0:T(8,128)} %bitcast.63, bf16[128,192]{1,0:T(8,128)(2,1)} %pad_maximum_fusion.3.refs_2_), custom_call_target="tpu_custom_call" | custom-call | tf_op jit(solution)/shard_map/gather_field/pallas_call | solution.py:165
  74.4 16.2 %all-to-all-start.1 = ((f32[128,2,128]{2,1,0:T(2,128)}), f32[128,2,128]{2,1,0:T(2,128)S(1)}, u32[]{:S(2)}, u32[]{:S(2)}) async-start(f32[128,2,128]{2,1,0:T(2,128)} %gather_field.1), calls=%async_computation.1 | async-start | bytes 262144 | tf_op jit(solution)/shard_map/all_to_all | solution.py:277
  90.7 0.8 copy.104
  91.4 11.3 %all-to-all-done.1 = f32[128,2,128]{2,1,0:T(2,128)S(1)} async-done(((f32[128,2,128]{2,1,0:T(2,128)}), f32[128,2,128]{2,1,0:T(2,128)S(1)}, u32[]{:S(2)}, u32[]{:S(2)}) %all-to-all-start.1) | async-done | bytes 131104 | tf_op jit(solution)/shard_map/all_to_all | solution.py:277
  102.7 1.1 %fusion = f32[16384]{0:T(1024)} fusion(f32[256,128]{1,0:T(8,128)S(1)} %bitcast.71, f32[16384]{0:T(1024)S(1)} %copy-done.1, s32[128]{0:T(128)S(1)} %get-tuple-element.48, f32[128,128]{1,0:T(8,128)S(1)} %bitcast.70, f32[128,128]{1,0:T(8,128)S(1)} %bitcast.68, s32[16384]{0:T(1024)S(1)} %copy-done, s32[128]{0:T(128)S(1)} %get-tuple-element.50), kind=kOutput, calls=%fused_computation.3 | convolution fusion | flops 50692096 | bytes 459776 | tf_op jit(solution)/shard_map/sb,sl->bl/dot_general | solution.py:282
  (49 shorter events, 2.5 us)
Async XLA Ops:
  0.6 0.9 copy-start.7
  3.1 1.0 copy-start.4
  4.0 1.1 %copy-start.5 = (f32[3,16384]{1,0:T(4,128)S(1)}, f32[3,16384]{1,0:T(4,128)}, u32[]{:S(2)}) copy-start(f32[3,16384]{1,0:T(4,128)} %param.14) | copy-start | bytes 589828
  4.2 0.8 copy-start
  5.4 0.8 copy-start.1
  9.4 15.6 %copy-start.2 = (f32[3,64,128]{2,1,0:T(8,128)S(1)}, f32[3,64,128]{2,1,0:T(8,128)}, u32[]{:S(2)}) copy-start(f32[3,64,128]{2,1,0:T(8,128)} %param.15) | copy-start | bytes 294916
  9.4 35.7 %all-to-all-start = ((f32[4,2,128,128]{3,1,0,2:T(2,128)}), f32[4,2,128,128]{3,1,0,2:T(2,128)S(1)}, u32[]{:S(2)}, u32[]{:S(2)}) async-start(f32[4,2,128,128]{3,1,0,2:T(2,128)} %pad_maximum_fusion.2), calls=%async_computation | async-start | bytes 1048576 | tf_op jit(solution)/shard_map/all_to_all | solution.py:243
  25.0 0.9 copy-start.3
  25.9 0.8 copy-start.6
  56.4 6.0 %collective-permute-start = (f32[10,64,4]{1,2,0:T(4,128)S(1)}, f32[10,64,4]{1,2,0:T(4,128)S(1)}, u32[]{:S(2)}, u32[]{:S(2)}) collective-permute-start(f32[10,64,4]{1,2,0:T(4,128)S(1)} %get-tuple-element.31), channel_id=1, source_target_pairs={{0,2},{2,4},{4,6},{6,8},{8,10},{10,12},{12,14},{14,16},{16,18},{18... | collective-permute-start | bytes 30728 | tf_op jit(solution)/shard_map/ppermute | solution.py:182
  56.9 5.5 %collective-permute-start.1 = (f32[10,64,4]{1,2,0:T(4,128)S(1)}, f32[10,64,4]{1,2,0:T(4,128)S(1)}, u32[]{:S(2)}, u32[]{:S(2)}) collective-permute-start(f32[10,64,4]{1,2,0:T(4,128)S(1)} %get-tuple-element.32), channel_id=1, source_target_pairs={{2,0},{4,2},{6,4},{8,6},{10,8},{12,10},{14,12},{16,14},{18,16},{20... | collective-permute-start | bytes 30728 | tf_op jit(solution)/shard_map/ppermute | solution.py:183
  62.5 1.3 %collective-permute-start.2 = (f32[10,4,8]{1,2,0:T(8,128)S(1)}, f32[10,4,8]{1,2,0:T(8,128)S(1)}, u32[]{:S(2)}, u32[]{:S(2)}) collective-permute-start(f32[10,4,8]{1,2,0:T(8,128)S(1)} %fusion.73), channel_id=1, source_target_pairs={{0,1},{1,0},{2,3},{3,2},{4,5},{5,4},{6,7},{7,6},{8,9},{9,8},{10,11... | collective-permute-start | bytes 3848 | tf_op jit(solution)/shard_map/ppermute | solution.py:189
  62.6 1.5 %collective-permute-start.3 = (f32[10,4,128]{2,1,0:T(4,128)S(1)}, f32[10,4,128]{2,1,0:T(4,128)S(1)}, u32[]{:S(2)}, u32[]{:S(2)}) collective-permute-start(f32[10,4,128]{2,1,0:T(4,128)S(1)} %bitcast.82), channel_id=1, source_target_pairs={{0,1},{1,0},{2,3},{3,2},{4,5},{5,4},{6,7},{7,6},{8,9},{9,8},{10,11... | collective-permute-start | bytes 61448 | tf_op jit(solution)/shard_map/ppermute | solution.py:186
  74.4 28.3 %all-to-all-start.1 = ((f32[128,2,128]{2,1,0:T(2,128)}), f32[128,2,128]{2,1,0:T(2,128)S(1)}, u32[]{:S(2)}, u32[]{:S(2)}) async-start(f32[128,2,128]{2,1,0:T(2,128)} %gather_field.1), calls=%async_computation.1 | async-start | bytes 262144 | tf_op jit(solution)/shard_map/all_to_all | solution.py:277

commit v6 on v5

--- a/solution.py
+++ b/solution.py
@@ -278,8 +278,7 @@
         landed_out, "cells", split_axis=0, concat_axis=0, tiled=True
     ).reshape(slots, tile_len)
     back_slot = block_owner * capacity + jnp.sum(earlier * member, axis=1).astype(jnp.int32)
-    taking = (back_slot[None, :] == jnp.arange(slots, dtype=jnp.int32)[:, None]).astype(jnp.float32)
-    landed = jnp.einsum("sb,sl->bl", taking, landed_back, precision=HIGHEST)
+    landed = jnp.take(landed_back, back_slot, axis=0, mode="clip")
     contact_gap = radius_tiles + reach - landed
     return (wall_next, contact_gap.reshape(-1))
 

time: 104 us -> 105 us (level); the launches traced: 104 us -> 104 us
  matrix products: 2.43 us -> 1.32 us
    dot_general x1 -> x0, matrix products: 1.11 us -> none  [on_device(): landed = jnp.einsum('sb,sl->bl', taking, landed_back, precision=HIGHEST)]
where the time goes in v6:
time: 105 us; the launch traced here: 104 us
  starting transfers between devices  35.8 us (34%)
  waiting for transfers between devices  31.1 us (30%)
  Pallas kernels  14.5 us (14%)
  local copies, waits for them, and re-layouts  12.3 us (12%)
  other arithmetic  6.84 us (7%)
  between operations  1.72 us (2%)
  matrix products  1.32 us (1%)
    all_to_all x1, waiting for transfers between devices, on_device(): lax.all_to_all(send.reshape(4, capacity, owners, tile_len), 'cells', spli...  18.1 us
    all_to_all x1, starting transfers between devices, on_device(): lax.all_to_all(send.reshape(4, capacity, owners, tile_len), 'cells', spli...  15.6 us
    all_to_all x1, starting transfers between devices, on_device(): lax.all_to_all(landed_out, 'cells', split_axis=0, concat_axis=0, tiled=True)  15.4 us
    all_to_all x1, waiting for transfers between devices, on_device(): lax.all_to_all(landed_out, 'cells', split_axis=0, concat_axis=0, tiled=True)  11.3 us
    pallas_call x1, Pallas kernels, scatter_traction(): pl.pallas_call(kernel, out_shape=jax.ShapeDtypeStruct((comps * patch_rows...  7.75 us
    pallas_call x1, Pallas kernels, gather_field(): pl.pallas_call(kernel, out_shape=jax.ShapeDtypeStruct((owners, capacity,...  6.73 us
    unnamed x20, local copies, waits for them, and re-layouts  4.63 us
    ppermute x1, starting transfers between devices, with_halo(): right = lax.ppermute(x[:, :, :width], 'cells', bwd)  3.71 us
  transfers between devices with their start and end apart: 6, of which 4 were waited for; matrix products, arithmetic and copies ran while one was open for 2% of the time, Pallas kernels for 0%

profile of v6, /device:TPU:2, one launch (start us, length us, event | category | flops | bytes accessed | tf_op | source)
XLA Modules:
  0.0 103.6 jit_solution(15770570619753733990)
XLA Ops:
  0.6 0.9 fusion
  1.6 1.5 %fusion.93 = (f32[1,16384]{1,0:T(1,128)S(1)}, f32[1,16384]{1,0:T(1,128)S(1)}, f32[1,16384]{1,0:T(1,128)S(1)}) fusion(f32[3,16384]{1,0:T(4,128)} %param.12), kind=kLoop, calls=%fused_computation.167 | loop fusion | bytes 393216 | tf_op jit(solution)/shard_map/slice | solution.py:36
  3.4 0.6 copy-done.4
  4.3 0.7 copy-done
  5.5 0.7 copy-done.1
  6.4 0.4 multiply_add_fusion.4
  6.7 0.3 multiply_add_fusion.3
  7.2 0.4 convolution_bitcast_fusion
  7.7 0.1 copy.93
  7.9 0.2 concatenate.31
  8.1 0.3 copy.92
  8.3 1.0 %pad_maximum_fusion.2 = f32[4,2,128,128]{3,1,0,2:T(2,128)} fusion(f32[1,2,128,128]{3,1,0,2:T(2,128)S(1)} %copy.93, f32[3,2,128,128]{3,1,0,2:T(2,128)S(1)} %copy.92), kind=kLoop, calls=%fused_computation.6 | loop fusion | flops 131072 | bytes 1048576 | tf_op jit(solution)/shard_map/concatenate | solution.py:240
  9.4 15.6 %all-to-all-start = ((f32[4,2,128,128]{3,1,0,2:T(2,128)}), f32[4,2,128,128]{3,1,0,2:T(2,128)S(1)}, u32[]{:S(2)}, u32[]{:S(2)}) async-start(f32[4,2,128,128]{3,1,0,2:T(2,128)} %pad_maximum_fusion.2), calls=%async_computation | async-start | bytes 1048576 | tf_op jit(solution)/shard_map/all_to_all | solution.py:243
  25.0 0.1 copy.95
  25.1 0.8 copy-done.3
  25.9 0.1 copy.96
  26.0 0.6 copy-done.6
  27.0 18.1 %all-to-all-done = f32[4,2,128,128]{3,1,0,2:T(2,128)S(1)} async-done(((f32[4,2,128,128]{3,1,0,2:T(2,128)}), f32[4,2,128,128]{3,1,0,2:T(2,128)S(1)}, u32[]{:S(2)}, u32[]{:S(2)}) %all-to-all-start) | async-done | bytes 524320 | tf_op jit(solution)/shard_map/all_to_all | solution.py:243
  45.1 0.2 compare_reduce_fusion
  45.4 0.6 select_reduce_fusion
  46.7 0.9 copy.94
  47.6 7.8 %scatter_traction.1 = f32[192,128]{1,0:T(8,128)} custom-call(s32[1]{0:T(128)} %bitcast.12.refs_0_, f32[4,256,128]{2,1,0:T(8,128)} %bitcast.57), custom_call_target="tpu_custom_call" | custom-call | tf_op jit(solution)/shard_map/scatter_traction/pallas_call | solution.py:116
  55.3 1.0 copy.97
  56.4 0.5 collective-permute-start
  56.9 3.7 %collective-permute-start.1 = (f32[10,64,4]{1,2,0:T(4,128)S(1)}, f32[10,64,4]{1,2,0:T(4,128)S(1)}, u32[]{:S(2)}, u32[]{:S(2)}) collective-permute-start(f32[10,64,4]{1,2,0:T(4,128)S(1)} %get-tuple-element.32), channel_id=1, source_target_pairs={{2,0},{4,2},{6,4},{8,6},{10,8},{12,10},{14,12},{16,14},{18,16},{20... | collective-permute-start | bytes 30728 | tf_op jit(solution)/shard_map/ppermute | solution.py:183
  60.6 0.2 fusion.90
  60.9 0.2 copy.98
  61.1 0.2 copy.99
  61.4 1.0 %collective-permute-done = f32[10,64,4]{1,2,0:T(4,128)S(1)} collective-permute-done((f32[10,64,4]{1,2,0:T(4,128)S(1)}, f32[10,64,4]{1,2,0:T(4,128)S(1)}, u32[]{:S(2)}, u32[]{:S(2)}) %collective-permute-start) | collective-permute-done | bytes 10272 | tf_op jit(solution)/shard_map/ppermute | solution.py:182
  62.6 0.5 collective-permute-start.3
  63.1 0.7 collective-permute-done.2
  63.8 0.1 copy.100
  64.0 0.1 copy.101
  64.2 0.3 copy.102
  64.5 0.3 copy.103
  64.8 0.5 pad_maximum_fusion
  65.4 0.2 multiply_add_fusion.2
  65.8 0.2 multiply_add_fusion.1
  66.1 0.2 multiply_add_fusion
  66.5 0.2 fusion.45
  66.8 0.1 fusion.73
  66.9 0.7 pad_maximum_fusion.3.refs_2_
  67.7 6.7 %gather_field.1 = f32[128,2,128]{2,1,0:T(2,128)} custom-call(s32[1]{0:T(128)} %bitcast.12.refs_0_, f32[4,256,128]{2,1,0:T(8,128)} %bitcast.58, bf16[128,192]{1,0:T(8,128)(2,1)} %pad_maximum_fusion.3.refs_2_), custom_call_target="tpu_custom_call" | custom-call | tf_op jit(solution)/shard_map/gather_field/pallas_call | solution.py:165
  74.4 15.4 %all-to-all-start.1 = ((f32[128,2,128]{2,1,0:T(2,128)}), f32[128,2,128]{2,1,0:T(2,128)S(1)}, u32[]{:S(2)}, u32[]{:S(2)}) async-start(f32[128,2,128]{2,1,0:T(2,128)} %gather_field.1), calls=%async_computation.1 | async-start | bytes 262144 | tf_op jit(solution)/shard_map/all_to_all | solution.py:277
  89.9 0.8 copy.104
  90.7 11.3 %all-to-all-done.1 = f32[128,2,128]{2,1,0:T(2,128)S(1)} async-done(((f32[128,2,128]{2,1,0:T(2,128)}), f32[128,2,128]{2,1,0:T(2,128)S(1)}, u32[]{:S(2)}, u32[]{:S(2)}) %all-to-all-start.1) | async-done | bytes 131104 | tf_op jit(solution)/shard_map/all_to_all | solution.py:277
  101.9 0.6 gather_fusion
  102.6 1.0 bitcast_subtract_fusion
  (51 shorter events, 2.6 us)
Async XLA Ops:
  0.6 0.9 copy-start.7
  3.1 1.0 copy-start.4
  4.0 1.1 %copy-start.5 = (f32[3,16384]{1,0:T(4,128)S(1)}, f32[3,16384]{1,0:T(4,128)}, u32[]{:S(2)}) copy-start(f32[3,16384]{1,0:T(4,128)} %param.14) | copy-start | bytes 589828
  4.2 0.8 copy-start
  5.4 0.8 copy-start.1
  9.4 15.6 %copy-start.2 = (f32[3,64,128]{2,1,0:T(8,128)S(1)}, f32[3,64,128]{2,1,0:T(8,128)}, u32[]{:S(2)}) copy-start(f32[3,64,128]{2,1,0:T(8,128)} %param.15) | copy-start | bytes 294916
  9.4 35.7 %all-to-all-start = ((f32[4,2,128,128]{3,1,0,2:T(2,128)}), f32[4,2,128,128]{3,1,0,2:T(2,128)S(1)}, u32[]{:S(2)}, u32[]{:S(2)}) async-start(f32[4,2,128,128]{3,1,0,2:T(2,128)} %pad_maximum_fusion.2), calls=%async_computation | async-start | bytes 1048576 | tf_op jit(solution)/shard_map/all_to_all | solution.py:243
  25.0 0.9 copy-start.3
  25.9 0.8 copy-start.6
  56.4 6.0 %collective-permute-start = (f32[10,64,4]{1,2,0:T(4,128)S(1)}, f32[10,64,4]{1,2,0:T(4,128)S(1)}, u32[]{:S(2)}, u32[]{:S(2)}) collective-permute-start(f32[10,64,4]{1,2,0:T(4,128)S(1)} %get-tuple-element.31), channel_id=1, source_target_pairs={{0,2},{2,4},{4,6},{6,8},{8,10},{10,12},{12,14},{14,16},{16,18},{18... | collective-permute-start | bytes 30728 | tf_op jit(solution)/shard_map/ppermute | solution.py:182
  56.9 5.5 %collective-permute-start.1 = (f32[10,64,4]{1,2,0:T(4,128)S(1)}, f32[10,64,4]{1,2,0:T(4,128)S(1)}, u32[]{:S(2)}, u32[]{:S(2)}) collective-permute-start(f32[10,64,4]{1,2,0:T(4,128)S(1)} %get-tuple-element.32), channel_id=1, source_target_pairs={{2,0},{4,2},{6,4},{8,6},{10,8},{12,10},{14,12},{16,14},{18,16},{20... | collective-permute-start | bytes 30728 | tf_op jit(solution)/shard_map/ppermute | solution.py:183
  62.5 1.3 %collective-permute-start.2 = (f32[10,4,8]{1,2,0:T(8,128)S(1)}, f32[10,4,8]{1,2,0:T(8,128)S(1)}, u32[]{:S(2)}, u32[]{:S(2)}) collective-permute-start(f32[10,4,8]{1,2,0:T(8,128)S(1)} %fusion.71), channel_id=1, source_target_pairs={{0,1},{1,0},{2,3},{3,2},{4,5},{5,4},{6,7},{7,6},{8,9},{9,8},{10,11... | collective-permute-start | bytes 3848 | tf_op jit(solution)/shard_map/ppermute | solution.py:189
  62.6 1.5 %collective-permute-start.3 = (f32[10,4,128]{2,1,0:T(4,128)S(1)}, f32[10,4,128]{2,1,0:T(4,128)S(1)}, u32[]{:S(2)}, u32[]{:S(2)}) collective-permute-start(f32[10,4,128]{2,1,0:T(4,128)S(1)} %bitcast.77), channel_id=1, source_target_pairs={{0,1},{1,0},{2,3},{3,2},{4,5},{5,4},{6,7},{7,6},{8,9},{9,8},{10,11... | collective-permute-start | bytes 61448 | tf_op jit(solution)/shard_map/ppermute | solution.py:186
  74.4 27.6 %all-to-all-start.1 = ((f32[128,2,128]{2,1,0:T(2,128)}), f32[128,2,128]{2,1,0:T(2,128)S(1)}, u32[]{:S(2)}, u32[]{:S(2)}) async-start(f32[128,2,128]{2,1,0:T(2,128)} %gather_field.1), calls=%async_computation.1 | async-start | bytes 262144 | tf_op jit(solution)/shard_map/all_to_all | solution.py:277

commit v7 on v5

--- a/solution.py
+++ b/solution.py
@@ -247,8 +247,9 @@
         concat_axis=2,
         tiled=True,
     ).reshape(4, slots, tile_len)
-    round_used = jnp.any(recv[3].reshape(capacity, owners * tile_len) < sentinel, axis=1)
-    rounds = jnp.max(jnp.where(round_used, jnp.arange(1, capacity + 1, dtype=jnp.int32), 0))
+    mine = lax.axis_index("cells")
+    named = jnp.sum((block_owner == mine).astype(jnp.int32))
+    rounds = jnp.clip(named, 1, capacity)
     count = (rounds * owners).reshape(1)
 
     traction = scatter_traction(count, recv, patch_rows, patch_cols)

time: 104 us -> 102 us (0.981)
  starting transfers between devices: 36.5 us -> 35.1 us
    all_to_all x1, starting transfers between devices: 16.2 us -> 14.8 us  [on_device(): lax.all_to_all(landed_out, 'cells', split_axis=0, concat_axis=0, tiled=True)]
where the time goes in v7:
time: 102 us; the launch traced here: 101 us
  starting transfers between devices  35.1 us (34%)
  waiting for transfers between devices  30.5 us (30%)
  Pallas kernels  14.5 us (14%)
  local copies, waits for them, and re-layouts  12.3 us (12%)
  other arithmetic  5.59 us (5%)
  between operations  1.7 us (2%)
  matrix products  1.67 us (2%)
    all_to_all x1, waiting for transfers between devices, on_device(): lax.all_to_all(send.reshape(4, capacity, owners, tile_len), 'cells', spli...  17.5 us
    all_to_all x1, starting transfers between devices, on_device(): lax.all_to_all(send.reshape(4, capacity, owners, tile_len), 'cells', spli...  15.6 us
    all_to_all x1, starting transfers between devices, on_device(): lax.all_to_all(landed_out, 'cells', split_axis=0, concat_axis=0, tiled=True)  14.8 us
    all_to_all x1, waiting for transfers between devices, on_device(): lax.all_to_all(landed_out, 'cells', split_axis=0, concat_axis=0, tiled=True)  11.3 us
    pallas_call x1, Pallas kernels, scatter_traction(): pl.pallas_call(kernel, out_shape=jax.ShapeDtypeStruct((comps * patch_rows...  7.75 us
    pallas_call x1, Pallas kernels, gather_field(): pl.pallas_call(kernel, out_shape=jax.ShapeDtypeStruct((owners, capacity,...  6.72 us
    unnamed x20, local copies, waits for them, and re-layouts  5.28 us
    ppermute x1, starting transfers between devices, with_halo(): right = lax.ppermute(x[:, :, :width], 'cells', bwd)  3.71 us
  transfers between devices with their start and end apart: 6, of which 4 were waited for; matrix products, arithmetic and copies ran while one was open for 2% of the time, Pallas kernels for 0%

profile of v7, /device:TPU:2, one launch (start us, length us, event | category | flops | bytes accessed | tf_op | source)
XLA Modules:
  0.0 101.4 jit_solution(5862564635836636538)
XLA Ops:
  0.6 0.6 copy-done.7
  1.3 0.2 fusion.1
  1.5 1.5 %fusion.96 = (f32[1,16384]{1,0:T(1,128)S(1)}, f32[1,16384]{1,0:T(1,128)S(1)}, f32[1,16384]{1,0:T(1,128)S(1)}) fusion(f32[3,16384]{1,0:T(4,128)} %param.12), kind=kLoop, calls=%fused_computation.169 | loop fusion | bytes 393216 | tf_op jit(solution)/shard_map/slice | solution.py:36
  3.3 0.6 copy-done.4
  4.2 0.7 copy-done
  5.4 0.7 copy-done.1
  6.2 0.6 multiply_add_fusion.6
  6.9 0.4 multiply_add_fusion.4
  7.3 0.3 multiply_add_fusion.3
  7.6 0.1 convert_reduce_fusion
  7.7 0.4 convolution_bitcast_fusion
  8.3 0.1 copy.93
  8.4 0.2 concatenate.31
  8.6 0.3 copy.92
  8.9 1.0 %pad_maximum_fusion.2 = f32[4,2,128,128]{3,1,0,2:T(2,128)} fusion(f32[1,2,128,128]{3,1,0,2:T(2,128)S(1)} %copy.93, f32[3,2,128,128]{3,1,0,2:T(2,128)S(1)} %copy.92), kind=kLoop, calls=%fused_computation.7 | loop fusion | flops 131072 | bytes 1048576 | tf_op jit(solution)/shard_map/concatenate | solution.py:240
  9.9 15.6 %all-to-all-start = ((f32[4,2,128,128]{3,1,0,2:T(2,128)}), f32[4,2,128,128]{3,1,0,2:T(2,128)S(1)}, u32[]{:S(2)}, u32[]{:S(2)}) async-start(f32[4,2,128,128]{3,1,0,2:T(2,128)} %pad_maximum_fusion.2), calls=%async_computation | async-start | bytes 1048576 | tf_op jit(solution)/shard_map/all_to_all | solution.py:243
  26.1 0.1 copy.95
  26.3 0.8 copy-done.3
  27.0 0.1 copy.96
  27.2 0.6 copy-done.6
  28.2 17.5 %all-to-all-done = f32[4,2,128,128]{3,1,0,2:T(2,128)S(1)} async-done(((f32[4,2,128,128]{3,1,0,2:T(2,128)}), f32[4,2,128,128]{3,1,0,2:T(2,128)S(1)}, u32[]{:S(2)}, u32[]{:S(2)}) %all-to-all-start) | async-done | bytes 524320 | tf_op jit(solution)/shard_map/all_to_all | solution.py:243
  45.6 0.9 copy.94
  46.6 7.7 %scatter_traction.1 = f32[192,128]{1,0:T(8,128)} custom-call(s32[1]{0:T(128)} %bitcast.1.refs_0_, f32[4,256,128]{2,1,0:T(8,128)} %bitcast.62), custom_call_target="tpu_custom_call" | custom-call | tf_op jit(solution)/shard_map/scatter_traction/pallas_call | solution.py:116
  54.3 1.0 %copy.97 = f32[3,64,128]{1,2,0:T(8,128)S(1)} copy(f32[3,64,128]{2,1,0:T(8,128)} %bitcast.72) | data formatting | bytes 196608 | tf_op jit(solution)/shard_map/reshape | solution.py:123
  55.4 0.5 collective-permute-start
  55.9 3.7 %collective-permute-start.1 = (f32[10,64,4]{1,2,0:T(4,128)S(1)}, f32[10,64,4]{1,2,0:T(4,128)S(1)}, u32[]{:S(2)}, u32[]{:S(2)}) collective-permute-start(f32[10,64,4]{1,2,0:T(4,128)S(1)} %get-tuple-element.32), channel_id=1, source_target_pairs={{2,0},{4,2},{6,4},{8,6},{10,8},{12,10},{14,12},{16,14},{18,16},{20... | collective-permute-start | bytes 30728 | tf_op jit(solution)/shard_map/ppermute | solution.py:183
  59.6 0.2 fusion.93
  59.9 0.2 copy.98
  60.1 0.2 copy.99
  60.3 1.0 %collective-permute-done = f32[10,64,4]{1,2,0:T(4,128)S(1)} collective-permute-done((f32[10,64,4]{1,2,0:T(4,128)S(1)}, f32[10,64,4]{1,2,0:T(4,128)S(1)}, u32[]{:S(2)}, u32[]{:S(2)}) %collective-permute-start) | collective-permute-done | bytes 10272 | tf_op jit(solution)/shard_map/ppermute | solution.py:182
  61.6 0.5 collective-permute-start.3
  62.1 0.7 collective-permute-done.2
  62.8 0.1 copy.100
  62.9 0.1 copy.101
  63.2 0.3 copy.102
  63.5 0.3 copy.103
  63.8 0.5 pad_maximum_fusion
  64.4 0.2 multiply_add_fusion.2
  64.8 0.2 multiply_add_fusion.1
  65.1 0.2 multiply_add_fusion
  65.5 0.2 fusion.46
  65.7 0.1 fusion.75
  65.9 0.7 pad_maximum_fusion.3.refs_2_
  66.6 6.7 %gather_field.1 = f32[128,2,128]{2,1,0:T(2,128)} custom-call(s32[1]{0:T(128)} %bitcast.1.refs_0_, f32[4,256,128]{2,1,0:T(8,128)} %bitcast.63, bf16[128,192]{1,0:T(8,128)(2,1)} %pad_maximum_fusion.3.refs_2_), custom_call_target="tpu_custom_call" | custom-call | tf_op jit(solution)/shard_map/gather_field/pallas_call | solution.py:165
  73.4 14.8 %all-to-all-start.1 = ((f32[128,2,128]{2,1,0:T(2,128)}), f32[128,2,128]{2,1,0:T(2,128)S(1)}, u32[]{:S(2)}, u32[]{:S(2)}) async-start(f32[128,2,128]{2,1,0:T(2,128)} %gather_field.1), calls=%async_computation.1 | async-start | bytes 262144 | tf_op jit(solution)/shard_map/all_to_all | solution.py:278
  88.3 0.8 copy.104
  89.0 11.3 %all-to-all-done.1 = f32[128,2,128]{2,1,0:T(2,128)S(1)} async-done(((f32[128,2,128]{2,1,0:T(2,128)}), f32[128,2,128]{2,1,0:T(2,128)S(1)}, u32[]{:S(2)}, u32[]{:S(2)}) %all-to-all-start.1) | async-done | bytes 131104 | tf_op jit(solution)/shard_map/all_to_all | solution.py:278
  100.3 1.1 %fusion = f32[16384]{0:T(1024)} fusion(f32[256,128]{1,0:T(8,128)S(1)} %bitcast.71, f32[16384]{0:T(1024)S(1)} %copy-done.1, s32[128]{0:T(128)S(1)} %get-tuple-element.48, f32[128,128]{1,0:T(8,128)S(1)} %bitcast.70, f32[128,128]{1,0:T(8,128)S(1)} %bitcast.68, s32[16384]{0:T(1024)S(1)} %copy-done, s32[128]{0:T(128)S(1)} %get-tuple-element.50), kind=kOutput, calls=%fused_computation.3 | convolution fusion | flops 50692096 | bytes 459776 | tf_op jit(solution)/shard_map/sb,sl->bl/dot_general | solution.py:283
  (47 shorter events, 2.4 us)
Async XLA Ops:
  0.6 0.7 copy-start.7
  3.0 1.0 copy-start.4
  3.9 1.1 %copy-start.5 = (f32[3,16384]{1,0:T(4,128)S(1)}, f32[3,16384]{1,0:T(4,128)}, u32[]{:S(2)}) copy-start(f32[3,16384]{1,0:T(4,128)} %param.14) | copy-start | bytes 589828
  4.1 0.8 copy-start
  5.3 0.8 copy-start.1
  9.9 16.2 %copy-start.2 = (f32[3,64,128]{2,1,0:T(8,128)S(1)}, f32[3,64,128]{2,1,0:T(8,128)}, u32[]{:S(2)}) copy-start(f32[3,64,128]{2,1,0:T(8,128)} %param.15) | copy-start | bytes 294916
  9.9 35.7 %all-to-all-start = ((f32[4,2,128,128]{3,1,0,2:T(2,128)}), f32[4,2,128,128]{3,1,0,2:T(2,128)S(1)}, u32[]{:S(2)}, u32[]{:S(2)}) async-start(f32[4,2,128,128]{3,1,0,2:T(2,128)} %pad_maximum_fusion.2), calls=%async_computation | async-start | bytes 1048576 | tf_op jit(solution)/shard_map/all_to_all | solution.py:243
  26.1 0.9 copy-start.3
  27.0 0.8 copy-start.6
  55.4 6.0 %collective-permute-start = (f32[10,64,4]{1,2,0:T(4,128)S(1)}, f32[10,64,4]{1,2,0:T(4,128)S(1)}, u32[]{:S(2)}, u32[]{:S(2)}) collective-permute-start(f32[10,64,4]{1,2,0:T(4,128)S(1)} %get-tuple-element.31), channel_id=1, source_target_pairs={{0,2},{2,4},{4,6},{6,8},{8,10},{10,12},{12,14},{14,16},{16,18},{18... | collective-permute-start | bytes 30728 | tf_op jit(solution)/shard_map/ppermute | solution.py:182
  55.9 5.5 %collective-permute-start.1 = (f32[10,64,4]{1,2,0:T(4,128)S(1)}, f32[10,64,4]{1,2,0:T(4,128)S(1)}, u32[]{:S(2)}, u32[]{:S(2)}) collective-permute-start(f32[10,64,4]{1,2,0:T(4,128)S(1)} %get-tuple-element.32), channel_id=1, source_target_pairs={{2,0},{4,2},{6,4},{8,6},{10,8},{12,10},{14,12},{16,14},{18,16},{20... | collective-permute-start | bytes 30728 | tf_op jit(solution)/shard_map/ppermute | solution.py:183
  61.5 1.3 %collective-permute-start.2 = (f32[10,4,8]{1,2,0:T(8,128)S(1)}, f32[10,4,8]{1,2,0:T(8,128)S(1)}, u32[]{:S(2)}, u32[]{:S(2)}) collective-permute-start(f32[10,4,8]{1,2,0:T(8,128)S(1)} %fusion.73), channel_id=1, source_target_pairs={{0,1},{1,0},{2,3},{3,2},{4,5},{5,4},{6,7},{7,6},{8,9},{9,8},{10,11... | collective-permute-start | bytes 3848 | tf_op jit(solution)/shard_map/ppermute | solution.py:189
  61.6 1.5 %collective-permute-start.3 = (f32[10,4,128]{2,1,0:T(4,128)S(1)}, f32[10,4,128]{2,1,0:T(4,128)S(1)}, u32[]{:S(2)}, u32[]{:S(2)}) collective-permute-start(f32[10,4,128]{2,1,0:T(4,128)S(1)} %bitcast.82), channel_id=1, source_target_pairs={{0,1},{1,0},{2,3},{3,2},{4,5},{5,4},{6,7},{7,6},{8,9},{9,8},{10,11... | collective-permute-start | bytes 61448 | tf_op jit(solution)/shard_map/ppermute | solution.py:186
  73.4 26.9 %all-to-all-start.1 = ((f32[128,2,128]{2,1,0:T(2,128)}), f32[128,2,128]{2,1,0:T(2,128)S(1)}, u32[]{:S(2)}, u32[]{:S(2)}) async-start(f32[128,2,128]{2,1,0:T(2,128)} %gather_field.1), calls=%async_computation.1 | async-start | bytes 262144 | tf_op jit(solution)/shard_map/all_to_all | solution.py:278

commit v8 on v7

--- a/solution.py
+++ b/solution.py
@@ -71,48 +71,53 @@
     return rows, cols
 
 
-def _scatter_kernel(count_ref, recv_ref, out_ref, *, patch_rows, shift):
-    comps = recv_ref.shape[0] - 1
-    lanes = recv_ref.shape[2]
+def _scatter_kernel(count_ref, recv_ref, out_ref, *, patch_rows, shift, comps):
+    owners, _, lanes = recv_ref.shape
     patch_cols = 1 << shift
+    width = comps + 1
     row_iota = lax.broadcasted_iota(jnp.int32, (patch_rows, lanes), 0)
     col_iota = lax.broadcasted_iota(jnp.int32, (patch_cols, lanes), 0)
     out_ref[...] = jnp.zeros_like(out_ref)
 
-    def step(i, carry):
-        base = pl.multiple_of(i * 8, 8)
-        blk = recv_ref[:, pl.ds(base, 8), :]
-        ids8 = blk[comps].astype(jnp.int32)
-        total = None
-        for g in range(8):
-            rows, cols = _split_ids(ids8[g : g + 1, :], shift)
-            rhot = (row_iota == rows).astype(BF16)
-            chot = (col_iota == cols).astype(BF16)
-            his, los = [], []
-            for c in range(comps):
-                p = blk[c, g : g + 1, :]
-                hi = p.astype(BF16)
-                lo = (p - hi.astype(F32)).astype(BF16)
-                his.append(rhot * hi)
-                los.append(rhot * lo)
-            lhs = jnp.concatenate(
-                [jnp.concatenate(his, axis=0), jnp.concatenate(los, axis=0)], axis=1
-            )
-            rhs = jnp.concatenate([chot, chot], axis=1)
-            part = lax.dot_general(
-                lhs, rhs, (((1,), (1,)), ((), ())), preferred_element_type=F32
-            )
-            total = part if total is None else total + part
-        out_ref[...] += total
-        return carry
-
-    lax.fori_loop(0, count_ref[0] // 8, step, 0)
-
-
-def scatter_traction(count, recv, patch_rows, patch_cols):
+    def make_step(rnd):
+        def step(i, carry):
+            base = pl.multiple_of(i * 8, 8)
+            blk = recv_ref[pl.ds(base, 8), :, :]
+            total = None
+            for g in range(8):
+                ids = blk[g, rnd * width + comps : rnd * width + comps + 1, :].astype(jnp.int32)
+                rows, cols = _split_ids(ids, shift)
+                rhot = (row_iota == rows).astype(BF16)
+                chot = (col_iota == cols).astype(BF16)
+                his, los = [], []
+                for c in range(comps):
+                    p = blk[g, rnd * width + c : rnd * width + c + 1, :]
+                    hi = p.astype(BF16)
+                    lo = (p - hi.astype(F32)).astype(BF16)
+                    his.append(rhot * hi)
+                    los.append(rhot * lo)
+                lhs = jnp.concatenate(
+                    [jnp.concatenate(his, axis=0), jnp.concatenate(los, axis=0)], axis=1
+                )
+                rhs = jnp.concatenate([chot, chot], axis=1)
+                part = lax.dot_general(
+                    lhs, rhs, (((1,), (1,)), ((), ())), preferred_element_type=F32
+                )
+                total = part if total is None else total + part
+            out_ref[...] += total
+            return carry
+
+        return step
+
+    capacity = recv_ref.shape[1] // width
+    for rnd in range(capacity):
+        trips = jnp.clip(count_ref[0] - rnd * owners, 0, owners) // 8
+        lax.fori_loop(0, trips, make_step(rnd), 0)
+
+
+def scatter_traction(count, recv, patch_rows, patch_cols, comps):
     shift = patch_cols.bit_length() - 1
-    comps = recv.shape[0] - 1
-    kernel = lambda *refs: _scatter_kernel(*refs, patch_rows=patch_rows, shift=shift)
+    kernel = lambda *refs: _scatter_kernel(*refs, patch_rows=patch_rows, shift=shift, comps=comps)
     out = pl.pallas_call(
         kernel,
         out_shape=jax.ShapeDtypeStruct((comps * patch_rows, patch_cols), F32),
@@ -123,34 +128,36 @@
     return out.reshape(comps, patch_rows, patch_cols)
 
 
-def _gather_kernel(count_ref, recv_ref, wt_ref, out_ref, *, patch_rows, shift):
-    owners = out_ref.shape[0]
-    lanes = recv_ref.shape[2]
-    id_row = recv_ref.shape[0] - 1
+def _gather_kernel(count_ref, recv_ref, wt_ref, out_ref, *, patch_rows, shift, width):
+    owners, capacity, lanes = out_ref.shape
     patch_cols = 1 << shift
     parts = wt_ref.shape[1] // patch_rows
     row_iota = lax.broadcasted_iota(jnp.int32, (patch_rows, lanes), 0)
     col_iota = lax.broadcasted_iota(jnp.int32, (patch_cols, lanes), 0)
     out_ref[...] = jnp.zeros_like(out_ref)
 
-    def step(i, carry):
-        base = pl.multiple_of(i * 8, 8)
-        ids8 = recv_ref[id_row, pl.ds(base, 8), :].astype(jnp.int32)
-        wt = wt_ref[...]
-        outs = []
-        for g in range(8):
-            rows, cols = _split_ids(ids8[g : g + 1, :], shift)
-            rhot = (row_iota == rows).astype(BF16)
-            rhs = jnp.concatenate([rhot] * parts, axis=0)
-            picked = jnp.dot(wt, rhs, preferred_element_type=F32)
-            sel = jnp.where(col_iota == cols, picked, 0.0)
-            outs.append(jnp.sum(sel, axis=0, keepdims=True))
-        rnd = base // owners
-        first = pl.multiple_of(base - rnd * owners, 8)
-        out_ref[pl.ds(first, 8), rnd, :] = jnp.concatenate(outs, axis=0)
-        return carry
-
-    lax.fori_loop(0, count_ref[0] // 8, step, 0)
+    def make_step(rnd):
+        def step(i, carry):
+            base = pl.multiple_of(i * 8, 8)
+            blk = recv_ref[pl.ds(base, 8), :, :]
+            wt = wt_ref[...]
+            outs = []
+            for g in range(8):
+                ids = blk[g, rnd * width + width - 1 : rnd * width + width, :].astype(jnp.int32)
+                rows, cols = _split_ids(ids, shift)
+                rhot = (row_iota == rows).astype(BF16)
+                rhs = jnp.concatenate([rhot] * parts, axis=0)
+                picked = jnp.dot(wt, rhs, preferred_element_type=F32)
+                sel = jnp.where(col_iota == cols, picked, 0.0)
+                outs.append(jnp.sum(sel, axis=0, keepdims=True))
+            out_ref[pl.ds(base, 8), rnd, :] = jnp.concatenate(outs, axis=0)
+            return carry
+
+        return step
+
+    for rnd in range(capacity):
+        trips = jnp.clip(count_ref[0] - rnd * owners, 0, owners) // 8
+        lax.fori_loop(0, trips, make_step(rnd), 0)
 
 
 def gather_field(count, recv, field, owners, capacity):
@@ -161,7 +168,8 @@
     mid = to_bf16_grid(rest)
     lo = rest - mid
     wt = jnp.concatenate([hi.T, mid.T, lo.T], axis=1).astype(BF16)
-    kernel = lambda *refs: _gather_kernel(*refs, patch_rows=patch_rows, shift=shift)
+    width = recv.shape[1] // capacity
+    kernel = lambda *refs: _gather_kernel(*refs, patch_rows=patch_rows, shift=shift, width=width)
     return pl.pallas_call(
         kernel,
         out_shape=jax.ShapeDtypeStruct((owners, capacity, recv.shape[2]), F32),
@@ -240,19 +248,20 @@
     send = jnp.concatenate(
         [send[:3], jnp.where(filled[:, None], send[3], float(sentinel))[None]], axis=0
     )
+    send = jnp.transpose(send.reshape(4, capacity, owners, tile_len), (2, 1, 0, 3))
     recv = lax.all_to_all(
-        send.reshape(4, capacity, owners, tile_len),
+        send.reshape(owners, capacity * 4, tile_len),
         "cells",
-        split_axis=2,
-        concat_axis=2,
+        split_axis=0,
+        concat_axis=0,
         tiled=True,
-    ).reshape(4, slots, tile_len)
+    )
     mine = lax.axis_index("cells")
     named = jnp.sum((block_owner == mine).astype(jnp.int32))
     rounds = jnp.clip(named, 1, capacity)
     count = (rounds * owners).reshape(1)
 
-    traction = scatter_traction(count, recv, patch_rows, patch_cols)
+    traction = scatter_traction(count, recv, patch_rows, patch_cols, 3)
     state = jnp.concatenate([wall_disp, wall_vel, wall_stiff[None], traction], axis=0)
     state_ext = with_halo(state, width)
     d_ext, v_ext, stiff_ext = state_ext[:3], state_ext[3:6], state_ext[6]

time: 102 us -> 107 us (1.049)
  starting transfers between devices: 35.1 us -> 39.7 us
    all_to_all x1, starting transfers between devices: 14.8 us -> 19.4 us  [on_device(): lax.all_to_all(landed_out, 'cells', split_axis=0, concat_axis=0, tiled=True)]
    unnamed x20 -> x22, local copies, waits for them, and re-layouts: 5.28 us -> 6.09 us
where the time goes in v8:
time: 107 us; the launch traced here: 106 us
  starting transfers between devices  39.7 us (37%)
  waiting for transfers between devices  30.5 us (29%)
  Pallas kernels  14.4 us (13%)
  local copies, waits for them, and re-layouts  12.2 us (11%)
  other arithmetic  5.59 us (5%)
  between operations  1.7 us (2%)
  matrix products  1.68 us (2%)
    all_to_all x1, starting transfers between devices, on_device(): lax.all_to_all(landed_out, 'cells', split_axis=0, concat_axis=0, tiled=True)  19.4 us
    all_to_all x1, waiting for transfers between devices, on_device(): lax.all_to_all(send.reshape(owners, capacity * 4, tile_len), 'cells', spl...  17.5 us
    all_to_all x1, starting transfers between devices, on_device(): lax.all_to_all(send.reshape(owners, capacity * 4, tile_len), 'cells', spl...  15.6 us
    all_to_all x1, waiting for transfers between devices, on_device(): lax.all_to_all(landed_out, 'cells', split_axis=0, concat_axis=0, tiled=True)  11.3 us
    pallas_call x1, Pallas kernels, scatter_traction(): pl.pallas_call(kernel, out_shape=jax.ShapeDtypeStruct((comps * patch_rows...  7.69 us
    pallas_call x1, Pallas kernels, gather_field(): pl.pallas_call(kernel, out_shape=jax.ShapeDtypeStruct((owners, capacity,...  6.74 us
    unnamed x22, local copies, waits for them, and re-layouts  6.09 us
    ppermute x1, starting transfers between devices, with_halo(): right = lax.ppermute(x[:, :, :width], 'cells', bwd)  3.71 us
  transfers between devices with their start and end apart: 6, of which 4 were waited for; matrix products, arithmetic and copies ran while one was open for 2% of the time, Pallas kernels for 0%

profile of v8, /device:TPU:2, one launch (start us, length us, event | category | flops | bytes accessed | tf_op | source)
XLA Modules:
  0.0 105.8 jit_solution(9169589486041797943)
XLA Ops:
  0.6 0.6 copy-done.8
  1.3 0.2 fusion.1
  1.5 1.5 %fusion.96 = (f32[1,16384]{1,0:T(1,128)S(1)}, f32[1,16384]{1,0:T(1,128)S(1)}, f32[1,16384]{1,0:T(1,128)S(1)}) fusion(f32[3,16384]{1,0:T(4,128)} %param.12), kind=kLoop, calls=%fused_computation.169 | loop fusion | bytes 393216 | tf_op jit(solution)/shard_map/slice | solution.py:36
  3.3 0.6 copy-done.5
  4.2 0.7 copy-done.1
  5.4 0.7 copy-done.2
  6.2 0.6 multiply_add_fusion.6
  6.9 0.4 multiply_add_fusion.4
  7.3 0.3 multiply_add_fusion.3
  7.6 0.1 convert_reduce_fusion
  7.7 0.4 convolution_bitcast_fusion
  8.3 0.1 copy.92
  8.4 0.2 concatenate.31
  8.6 0.3 copy.91
  8.9 1.1 pad_maximum_fusion.2
  9.9 15.6 %all-to-all-start = ((f32[128,8,128]{2,1,0:T(8,128)}), f32[128,8,128]{2,1,0:T(8,128)S(1)}, u32[]{:S(2)}, u32[]{:S(2)}) async-start(f32[128,8,128]{2,1,0:T(8,128)} %bitcast.14), calls=%async_computation | async-start | bytes 1048576 | tf_op jit(solution)/shard_map/all_to_all | solution.py:252
  26.2 0.1 copy.93
  26.3 0.8 copy-done.4
  27.0 0.1 copy.94
  27.2 0.6 copy-done.7
  28.2 17.5 %all-to-all-done.refs_1_ = f32[128,8,128]{2,1,0:T(8,128)S(1)} async-done(((f32[128,8,128]{2,1,0:T(8,128)}), f32[128,8,128]{2,1,0:T(8,128)S(1)}, u32[]{:S(2)}, u32[]{:S(2)}) %all-to-all-start) | async-done | bytes 524320 | tf_op jit(solution)/shard_map/all_to_all | solution.py:252
  45.7 0.8 copy-done
  46.5 7.7 %scatter_traction.1 = f32[192,128]{1,0:T(8,128)} custom-call(s32[1]{0:T(128)} %bitcast.1.refs_0_, f32[128,8,128]{2,1,0:T(8,128)} %copy-done), custom_call_target="tpu_custom_call" | custom-call | tf_op jit(solution)/shard_map/scatter_traction/pallas_call | solution.py:121
  54.2 1.0 copy.95
  55.3 0.5 collective-permute-start
  55.8 3.7 %collective-permute-start.1 = (f32[10,64,4]{1,2,0:T(4,128)S(1)}, f32[10,64,4]{1,2,0:T(4,128)S(1)}, u32[]{:S(2)}, u32[]{:S(2)}) collective-permute-start(f32[10,64,4]{1,2,0:T(4,128)S(1)} %get-tuple-element.32), channel_id=1, source_target_pairs={{2,0},{4,2},{6,4},{8,6},{10,8},{12,10},{14,12},{16,14},{18,16},{20... | collective-permute-start | bytes 30728 | tf_op jit(solution)/shard_map/ppermute | solution.py:191
  59.5 0.2 fusion.93
  59.7 0.2 copy.96
  59.9 0.2 copy.97
  60.2 1.0 collective-permute-done
  61.4 0.5 collective-permute-start.3
  61.9 0.7 collective-permute-done.2
  62.6 0.1 copy.98
  62.8 0.1 copy.99
  63.0 0.3 copy.100
  63.3 0.3 copy.101
  63.7 0.5 pad_maximum_fusion
  64.2 0.2 multiply_add_fusion.2
  64.6 0.2 multiply_add_fusion.1
  65.0 0.2 multiply_add_fusion
  65.3 0.2 fusion.46
  65.6 0.1 fusion.75
  65.8 0.7 pad_maximum_fusion.3.refs_2_
  66.5 6.7 %gather_field.1 = f32[128,2,128]{2,1,0:T(2,128)} custom-call(s32[1]{0:T(128)} %bitcast.1.refs_0_, f32[128,8,128]{2,1,0:T(8,128)} %copy-done, bf16[128,192]{1,0:T(8,128)(2,1)} %pad_maximum_fusion.3.refs_2_), custom_call_target="tpu_custom_call" | custom-call | tf_op jit(solution)/shard_map/gather_field/pallas_call | solution.py:173
  73.2 19.4 %all-to-all-start.1 = ((f32[128,2,128]{2,1,0:T(2,128)}), f32[128,2,128]{2,1,0:T(2,128)S(1)}, u32[]{:S(2)}, u32[]{:S(2)}) async-start(f32[128,2,128]{2,1,0:T(2,128)} %gather_field.1), calls=%async_computation.1 | async-start | bytes 262144 | tf_op jit(solution)/shard_map/all_to_all | solution.py:287
  92.7 0.8 copy.102
  93.5 11.3 %all-to-all-done.1 = f32[128,2,128]{2,1,0:T(2,128)S(1)} async-done(((f32[128,2,128]{2,1,0:T(2,128)}), f32[128,2,128]{2,1,0:T(2,128)S(1)}, u32[]{:S(2)}, u32[]{:S(2)}) %all-to-all-start.1) | async-done | bytes 131104 | tf_op jit(solution)/shard_map/all_to_all | solution.py:287
  104.7 1.1 %fusion = f32[16384]{0:T(1024)} fusion(f32[256,128]{1,0:T(8,128)S(1)} %bitcast.71, f32[16384]{0:T(1024)S(1)} %copy-done.2, s32[128]{0:T(128)S(1)} %get-tuple-element.48, f32[128,128]{1,0:T(8,128)S(1)} %bitcast.70, f32[128,128]{1,0:T(8,128)S(1)} %bitcast.68, s32[16384]{0:T(1024)S(1)} %copy-done.1, s32[128]{0:T(128)S(1)} %get-tuple-element.50), kind=kOutput, calls=%fused_computation.3 | convolution fusion | flops 50692096 | bytes 459776 | tf_op jit(solution)/shard_map/sb,sl->bl/dot_general | solution.py:292
  (48 shorter events, 2.5 us)
Async XLA Ops:
  0.6 0.7 copy-start.8
  3.0 1.0 copy-start.5
  3.9 1.1 %copy-start.6 = (f32[3,16384]{1,0:T(4,128)S(1)}, f32[3,16384]{1,0:T(4,128)}, u32[]{:S(2)}) copy-start(f32[3,16384]{1,0:T(4,128)} %param.14) | copy-start | bytes 589828
  4.1 0.8 copy-start.1
  5.3 0.8 copy-start.2
  9.9 16.2 %copy-start.3 = (f32[3,64,128]{2,1,0:T(8,128)S(1)}, f32[3,64,128]{2,1,0:T(8,128)}, u32[]{:S(2)}) copy-start(f32[3,64,128]{2,1,0:T(8,128)} %param.15) | copy-start | bytes 294916
  9.9 35.7 %all-to-all-start = ((f32[128,8,128]{2,1,0:T(8,128)}), f32[128,8,128]{2,1,0:T(8,128)S(1)}, u32[]{:S(2)}, u32[]{:S(2)}) async-start(f32[128,8,128]{2,1,0:T(8,128)} %bitcast.14), calls=%async_computation | async-start | bytes 1048576 | tf_op jit(solution)/shard_map/all_to_all | solution.py:252
  26.1 0.9 copy-start.4
  27.0 0.8 copy-start.7
  45.7 0.8 copy-start
  55.3 6.0 %collective-permute-start = (f32[10,64,4]{1,2,0:T(4,128)S(1)}, f32[10,64,4]{1,2,0:T(4,128)S(1)}, u32[]{:S(2)}, u32[]{:S(2)}) collective-permute-start(f32[10,64,4]{1,2,0:T(4,128)S(1)} %get-tuple-element.31), channel_id=1, source_target_pairs={{0,2},{2,4},{4,6},{6,8},{8,10},{10,12},{12,14},{14,16},{16,18},{18... | collective-permute-start | bytes 30728 | tf_op jit(solution)/shard_map/ppermute | solution.py:190
  55.8 5.5 %collective-permute-start.1 = (f32[10,64,4]{1,2,0:T(4,128)S(1)}, f32[10,64,4]{1,2,0:T(4,128)S(1)}, u32[]{:S(2)}, u32[]{:S(2)}) collective-permute-start(f32[10,64,4]{1,2,0:T(4,128)S(1)} %get-tuple-element.32), channel_id=1, source_target_pairs={{2,0},{4,2},{6,4},{8,6},{10,8},{12,10},{14,12},{16,14},{18,16},{20... | collective-permute-start | bytes 30728 | tf_op jit(solution)/shard_map/ppermute | solution.py:191
  61.3 1.3 %collective-permute-start.2 = (f32[10,4,8]{1,2,0:T(8,128)S(1)}, f32[10,4,8]{1,2,0:T(8,128)S(1)}, u32[]{:S(2)}, u32[]{:S(2)}) collective-permute-start(f32[10,4,8]{1,2,0:T(8,128)S(1)} %fusion.73), channel_id=1, source_target_pairs={{0,1},{1,0},{2,3},{3,2},{4,5},{5,4},{6,7},{7,6},{8,9},{9,8},{10,11... | collective-permute-start | bytes 3848 | tf_op jit(solution)/shard_map/ppermute | solution.py:197
  61.4 1.5 %collective-permute-start.3 = (f32[10,4,128]{2,1,0:T(4,128)S(1)}, f32[10,4,128]{2,1,0:T(4,128)S(1)}, u32[]{:S(2)}, u32[]{:S(2)}) collective-permute-start(f32[10,4,128]{2,1,0:T(4,128)S(1)} %bitcast.82), channel_id=1, source_target_pairs={{0,1},{1,0},{2,3},{3,2},{4,5},{5,4},{6,7},{7,6},{8,9},{9,8},{10,11... | collective-permute-start | bytes 61448 | tf_op jit(solution)/shard_map/ppermute | solution.py:194
  73.2 31.5 %all-to-all-start.1 = ((f32[128,2,128]{2,1,0:T(2,128)}), f32[128,2,128]{2,1,0:T(2,128)S(1)}, u32[]{:S(2)}, u32[]{:S(2)}) async-start(f32[128,2,128]{2,1,0:T(2,128)} %gather_field.1), calls=%async_computation.1 | async-start | bytes 262144 | tf_op jit(solution)/shard_map/all_to_all | solution.py:287

commit v9 on v8

--- a/solution.py
+++ b/solution.py
@@ -128,10 +128,16 @@
     return out.reshape(comps, patch_rows, patch_cols)
 
 
-def _gather_kernel(count_ref, recv_ref, wt_ref, out_ref, *, patch_rows, shift, width):
+def _gather_kernel(count_ref, recv_ref, field_ref, out_ref, wt_ref, *, patch_rows, shift, width):
     owners, capacity, lanes = out_ref.shape
     patch_cols = 1 << shift
     parts = wt_ref.shape[1] // patch_rows
+    field = field_ref[...]
+    hi = field.astype(BF16).astype(F32)
+    rest = field - hi
+    mid = rest.astype(BF16).astype(F32)
+    lo = rest - mid
+    wt_ref[...] = jnp.concatenate([hi, mid, lo], axis=0).T.astype(BF16)
     row_iota = lax.broadcasted_iota(jnp.int32, (patch_rows, lanes), 0)
     col_iota = lax.broadcasted_iota(jnp.int32, (patch_cols, lanes), 0)
     out_ref[...] = jnp.zeros_like(out_ref)
@@ -163,11 +169,6 @@
 def gather_field(count, recv, field, owners, capacity):
     patch_rows, patch_cols = field.shape
     shift = patch_cols.bit_length() - 1
-    hi = to_bf16_grid(field)
-    rest = field - hi
-    mid = to_bf16_grid(rest)
-    lo = rest - mid
-    wt = jnp.concatenate([hi.T, mid.T, lo.T], axis=1).astype(BF16)
     width = recv.shape[1] // capacity
     kernel = lambda *refs: _gather_kernel(*refs, patch_rows=patch_rows, shift=shift, width=width)
     return pl.pallas_call(
@@ -176,8 +177,9 @@
         in_specs=[pl.BlockSpec(memory_space=pltpu.SMEM)]
         + [pl.BlockSpec(memory_space=pltpu.VMEM)] * 2,
         out_specs=pl.BlockSpec(memory_space=pltpu.VMEM),
+        scratch_shapes=[pltpu.VMEM((patch_cols, 3 * patch_rows), BF16)],
         name="gather_field",
-    )(count, recv, wt)
+    )(count, recv, field)
 
 
 def with_halo(x, width):

time: 107 us -> 106 us (level)
  waiting for transfers between devices: 30.5 us -> 37 us
  local copies, waits for them, and re-layouts: 12.2 us -> 7.98 us
  starting transfers between devices: 39.7 us -> 35.8 us
    ppermute x1, waiting for transfers between devices: 1.05 us -> 5.11 us  [with_halo(): left = lax.ppermute(x[:, :, cols - width:], 'cells', fwd)]
    all_to_all x1, starting transfers between devices: 19.4 us -> 15.5 us  [on_device(): lax.all_to_all(landed_out, 'cells', split_axis=0, concat_axis=0, tiled=True)]
    unnamed x22 -> x20, local copies, waits for them, and re-layouts: 6.09 us -> 3.6 us
    all_to_all x1, waiting for transfers between devices: 17.5 us -> 19.5 us  [on_device(): lax.all_to_all(send.reshape(owners, capacity * 4, tile_len), 'cells', spl...]
  transfers between devices with their start and end apart: 6 -> 6, of which waited for: 4 -> 5; matrix products, arithmetic and copies ran while one was open for 2% -> 1% of each run, Pallas kernels for 0% -> 0%
where the time goes in v9:
time: 106 us; the launch traced here: 104 us
  waiting for transfers between devices  37 us (35%)
  starting transfers between devices  35.8 us (34%)
  Pallas kernels  14.5 us (14%)
  local copies, waits for them, and re-layouts  7.98 us (8%)
  other arithmetic  5.87 us (6%)
  matrix products  1.67 us (2%)
  between operations  1.64 us (2%)
    all_to_all x1, waiting for transfers between devices, on_device(): lax.all_to_all(send.reshape(owners, capacity * 4, tile_len), 'cells', spl...  19.5 us
    all_to_all x1, starting transfers between devices, on_device(): lax.all_to_all(landed_out, 'cells', split_axis=0, concat_axis=0, tiled=True)  15.5 us
    all_to_all x1, starting transfers between devices, on_device(): lax.all_to_all(send.reshape(owners, capacity * 4, tile_len), 'cells', spl...  15.4 us
    all_to_all x1, waiting for transfers between devices, on_device(): lax.all_to_all(landed_out, 'cells', split_axis=0, concat_axis=0, tiled=True)  11.6 us
    pallas_call x1, Pallas kernels, scatter_traction(): pl.pallas_call(kernel, out_shape=jax.ShapeDtypeStruct((comps * patch_rows...  7.73 us
    pallas_call x1, Pallas kernels, gather_field(): pl.pallas_call(kernel, out_shape=jax.ShapeDtypeStruct((owners, capacity,...  6.81 us
    ppermute x1, waiting for transfers between devices, with_halo(): left = lax.ppermute(x[:, :, cols - width:], 'cells', fwd)  5.11 us
    ppermute x1, starting transfers between devices, with_halo(): right = lax.ppermute(x[:, :, :width], 'cells', bwd)  3.7 us
  transfers between devices with their start and end apart: 6, of which 5 were waited for; matrix products, arithmetic and copies ran while one was open for 1% of the time, Pallas kernels for 0%

profile of v9, /device:TPU:2, one launch (start us, length us, event | category | flops | bytes accessed | tf_op | source)
XLA Modules:
  0.0 104.5 jit_solution(10684439239936879614)
XLA Ops:
  0.6 0.6 copy-done.9
  1.3 0.2 fusion.1
  1.5 1.5 %fusion.91 = (f32[1,16384]{1,0:T(1,128)S(1)}, f32[1,16384]{1,0:T(1,128)S(1)}, f32[1,16384]{1,0:T(1,128)S(1)}) fusion(f32[3,16384]{1,0:T(4,128)} %param.12), kind=kLoop, calls=%fused_computation.158 | loop fusion | bytes 393216 | tf_op jit(solution)/shard_map/slice | solution.py:36
  3.0 0.1 copy.61
  3.1 0.1 copy.62
  3.2 0.1 copy.65
  3.3 0.6 copy-done.7
  3.9 0.1 fusion.89
  4.0 0.1 copy.56
  4.2 0.7 copy-done.5
  5.1 0.1 fusion.90
  5.3 0.1 copy.60
  5.4 0.7 copy-done.6
  6.2 0.6 multiply_add_fusion.6
  6.9 0.4 multiply_add_fusion.4
  7.3 0.3 multiply_add_fusion.3
  7.6 0.1 convert_reduce_fusion
  7.7 0.4 convolution_bitcast_fusion
  8.3 0.1 copy.70
  8.4 0.2 concatenate.27
  8.6 0.3 copy.69
  8.9 1.0 pad_maximum_fusion.1
  9.9 15.4 %all-to-all-start = ((f32[128,8,128]{2,1,0:T(8,128)}), f32[128,8,128]{2,1,0:T(8,128)S(1)}, u32[]{:S(2)}, u32[]{:S(2)}) async-start(f32[128,8,128]{2,1,0:T(8,128)} %bitcast.14), calls=%async_computation | async-start | bytes 1048576 | tf_op jit(solution)/shard_map/all_to_all | solution.py:254
  26.0 19.5 %all-to-all-done.refs_1_ = f32[128,8,128]{2,1,0:T(8,128)S(1)} async-done(((f32[128,8,128]{2,1,0:T(8,128)}), f32[128,8,128]{2,1,0:T(8,128)S(1)}, u32[]{:S(2)}, u32[]{:S(2)}) %all-to-all-start) | async-done | bytes 524320 | tf_op jit(solution)/shard_map/all_to_all | solution.py:254
  45.5 0.8 copy-done
  46.3 7.7 %scatter_traction.1 = f32[192,128]{1,0:T(8,128)} custom-call(s32[1]{0:T(128)} %bitcast.1.refs_0_, f32[128,8,128]{2,1,0:T(8,128)} %copy-done), custom_call_target="tpu_custom_call" | custom-call | tf_op jit(solution)/shard_map/scatter_traction/pallas_call | solution.py:121
  54.1 0.9 pad_maximum_fusion.2
  55.0 0.2 fusion.88
  55.1 0.5 collective-permute-start
  55.6 3.7 %collective-permute-start.1 = (f32[10,64,4]{2,1,0:T(8,128)S(1)}, f32[10,64,4]{2,1,0:T(8,128)S(1)}, u32[]{:S(2)}, u32[]{:S(2)}) collective-permute-start(f32[10,64,4]{2,1,0:T(8,128)S(1)} %get-tuple-element.22), channel_id=1, source_target_pairs={{2,0},{4,2},{6,4},{8,6},{10,8},{12,10},{14,12},{16,14},{18,16},{20... | collective-permute-start | bytes 30728 | tf_op jit(solution)/shard_map/ppermute | solution.py:193
  59.6 5.1 %collective-permute-done = f32[10,64,4]{2,1,0:T(8,128)S(1)} collective-permute-done((f32[10,64,4]{2,1,0:T(8,128)S(1)}, f32[10,64,4]{2,1,0:T(8,128)S(1)}, u32[]{:S(2)}, u32[]{:S(2)}) %collective-permute-start) | collective-permute-done | bytes 10272 | tf_op jit(solution)/shard_map/ppermute | solution.py:192
  64.7 0.1 fusion.74
  64.8 0.1 collective-permute-start.2
  65.0 0.6 collective-permute-start.3
  65.5 0.6 collective-permute-done.2
  66.2 0.2 collective-permute-done.3
  66.4 0.1 broadcast_select_fusion.1
  66.5 0.4 pad_maximum_fusion
  66.9 0.2 multiply_add_fusion.2
  67.2 0.3 multiply_add_fusion.1
  67.5 0.3 multiply_add_fusion
  67.8 0.2 fusion.46
  68.0 0.7 fusion.70.refs_2_
  68.7 6.8 %gather_field.1 = f32[128,2,128]{2,1,0:T(2,128)} custom-call(s32[1]{0:T(128)} %bitcast.1.refs_0_, f32[128,8,128]{2,1,0:T(8,128)} %copy-done, f32[64,128]{1,0:T(8,128)} %fusion.70.refs_2_), custom_call_target="tpu_custom_call" | custom-call | tf_op jit(solution)/shard_map/gather_field/pallas_call | solution.py:174
  75.6 15.5 %all-to-all-start.1 = ((f32[128,2,128]{2,1,0:T(2,128)}), f32[128,2,128]{2,1,0:T(2,128)S(1)}, u32[]{:S(2)}, u32[]{:S(2)}) async-start(f32[128,2,128]{2,1,0:T(2,128)} %gather_field.1), calls=%async_computation.1 | async-start | bytes 262144 | tf_op jit(solution)/shard_map/all_to_all | solution.py:289
  91.1 0.7 slice.231
  91.8 11.6 %all-to-all-done.1 = f32[128,2,128]{2,1,0:T(2,128)S(1)} async-done(((f32[128,2,128]{2,1,0:T(2,128)}), f32[128,2,128]{2,1,0:T(2,128)S(1)}, u32[]{:S(2)}, u32[]{:S(2)}) %all-to-all-start.1) | async-done | bytes 131104 | tf_op jit(solution)/shard_map/all_to_all | solution.py:289
  103.4 1.1 %fusion = f32[16384]{0:T(1024)} fusion(f32[256,128]{1,0:T(8,128)S(1)} %bitcast.60, f32[16384]{0:T(1024)S(1)} %copy-done.6, s32[128]{0:T(128)S(1)} %get-tuple-element.34, f32[128,128]{1,0:T(8,128)S(1)} %bitcast.59, f32[128,128]{1,0:T(8,128)S(1)} %bitcast.57, s32[16384]{0:T(1024)S(1)} %copy-done.5, s32[128]{0:T(128)S(1)} %get-tuple-element.36), kind=kOutput, calls=%fused_computation.3 | convolution fusion | flops 50692096 | bytes 459776 | tf_op jit(solution)/shard_map/sb,sl->bl/dot_general | solution.py:294
  (36 shorter events, 1.0 us)
Async XLA Ops:
  0.6 0.7 copy-start.9
  3.0 1.0 copy-start.7
  3.9 1.1 %copy-start.8 = (f32[3,16384]{1,0:T(4,128)S(1)}, f32[3,16384]{1,0:T(4,128)}, u32[]{:S(2)}) copy-start(f32[3,16384]{1,0:T(4,128)} %param.14) | copy-start | bytes 589828
  4.1 0.8 copy-start.5
  5.3 0.8 copy-start.6
  9.9 35.6 %all-to-all-start = ((f32[128,8,128]{2,1,0:T(8,128)}), f32[128,8,128]{2,1,0:T(8,128)S(1)}, u32[]{:S(2)}, u32[]{:S(2)}) async-start(f32[128,8,128]{2,1,0:T(8,128)} %bitcast.14), calls=%async_computation | async-start | bytes 1048576 | tf_op jit(solution)/shard_map/all_to_all | solution.py:254
  45.5 0.8 copy-start
  46.3 7.7 %copy-start.2 = (f32[3,64,128]{2,1,0:T(8,128)S(1)}, f32[3,64,128]{2,1,0:T(8,128)}, u32[]{:S(2)}) copy-start(f32[3,64,128]{2,1,0:T(8,128)} %param.16) | copy-start | bytes 294916
  46.3 7.7 %copy-start.3 = (f32[3,64,128]{2,1,0:T(8,128)S(1)}, f32[3,64,128]{2,1,0:T(8,128)}, u32[]{:S(2)}) copy-start(f32[3,64,128]{2,1,0:T(8,128)} %param.15) | copy-start | bytes 294916
  46.3 7.7 %copy-start.4 = (f32[64,128]{1,0:T(8,128)S(1)}, f32[64,128]{1,0:T(8,128)}, u32[]{:S(2)}) copy-start(f32[64,128]{1,0:T(8,128)} %param.17) | copy-start | bytes 98308
  55.1 9.6 %collective-permute-start = (f32[10,64,4]{2,1,0:T(8,128)S(1)}, f32[10,64,4]{2,1,0:T(8,128)S(1)}, u32[]{:S(2)}, u32[]{:S(2)}) collective-permute-start(f32[10,64,4]{2,1,0:T(8,128)S(1)} %get-tuple-element.21), channel_id=1, source_target_pairs={{0,2},{2,4},{4,6},{6,8},{8,10},{10,12},{12,14},{14,16},{16,18},{18... | collective-permute-start | bytes 30728 | tf_op jit(solution)/shard_map/ppermute | solution.py:192
  55.6 9.1 %collective-permute-start.1 = (f32[10,64,4]{2,1,0:T(8,128)S(1)}, f32[10,64,4]{2,1,0:T(8,128)S(1)}, u32[]{:S(2)}, u32[]{:S(2)}) collective-permute-start(f32[10,64,4]{2,1,0:T(8,128)S(1)} %get-tuple-element.22), channel_id=1, source_target_pairs={{2,0},{4,2},{6,4},{8,6},{10,8},{12,10},{14,12},{16,14},{18,16},{20... | collective-permute-start | bytes 30728 | tf_op jit(solution)/shard_map/ppermute | solution.py:193
  59.6 5.3 %copy-start.1 = (f32[192,128]{1,0:T(8,128)S(1)}, f32[192,128]{1,0:T(8,128)}, u32[]{:S(2)}) copy-start(f32[192,128]{1,0:T(8,128)} %scatter_traction.1) | copy-start | bytes 294916
  64.8 1.3 %collective-permute-start.2 = (f32[10,4,8]{2,1,0:T(4,128)S(1)}, f32[10,4,8]{2,1,0:T(4,128)S(1)}, u32[]{:S(2)}, u32[]{:S(2)}) collective-permute-start(f32[10,4,8]{2,1,0:T(4,128)S(1)} %fusion.74), channel_id=1, source_target_pairs={{0,1},{1,0},{2,3},{3,2},{4,5},{5,4},{6,7},{7,6},{8,9},{9,8},{10,11... | collective-permute-start | bytes 3848 | tf_op jit(solution)/shard_map/ppermute | solution.py:199
  65.0 1.4 %collective-permute-start.3 = (f32[10,4,128]{2,1,0:T(4,128)S(1)}, f32[10,4,128]{2,1,0:T(4,128)S(1)}, u32[]{:S(2)}, u32[]{:S(2)}) collective-permute-start(f32[10,4,128]{2,1,0:T(4,128)S(1)} %maximum_select_fusion), channel_id=1, source_target_pairs={{0,1},{1,0},{2,3},{3,2},{4,5},{5,4},{6,7},{7,6},{8,9},{9,8},{10,11... | collective-permute-start | bytes 61448 | tf_op jit(solution)/shard_map/ppermute | solution.py:196
  75.6 27.8 %all-to-all-start.1 = ((f32[128,2,128]{2,1,0:T(2,128)}), f32[128,2,128]{2,1,0:T(2,128)S(1)}, u32[]{:S(2)}, u32[]{:S(2)}) async-start(f32[128,2,128]{2,1,0:T(2,128)} %gather_field.1), calls=%async_computation.1 | async-start | bytes 262144 | tf_op jit(solution)/shard_map/all_to_all | solution.py:289
